TPU v7x, 512 devices: a whole 4x8x8 slice. The times are simulated.
512 devices in a mesh: lon: 64 (over z_hi, y, core), lat: 8 (over z_lo, x).
Axes of the slice: x: 4, y: 8, z: 8 (z_hi: 4, z_lo: 2; z = z_hi * 2 + z_lo), core: 2. Of those that a mesh axis runs over, the one named last changes fastest.
Arguments:
- concentration: float32 [512, 1792, 128], P('lon', 'lat'), may hold values from -6 to 6
- wind: bfloat16 [3, 512, 1792, 128], P(None, 'lon', 'lat'), may hold values from -0.099609375 to 0.099609375
- kappa: bfloat16 [512, 1792, 128], P('lon', 'lat'), may hold values from 0.0099487305 to 0.059814453
- observed: bfloat16 [512, 1792, 128], P('lon', 'lat'), may hold values from -6 to 6
Outputs:
- grad_conc: float32 [512, 1792, 128], P('lon', 'lat')
- grad_kappa: float32 [512, 1792, 128], P('lon', 'lat')
All inputs are finite; a program needn't handle non-finite values.
Results may differ from a plain program's by a relative error of at most 0.0023.
Values may be sent and summed in bfloat16 or wider, within the bound.
No kernel may reach another device: no remote copies, remote signals or barrier semaphores. Data moves between devices by JAX's collectives and lax.ppermute only.
A program may use at most 128 MiB of HBM per device.

v0:
```python
import jax
import jax.numpy as jnp
from jax import lax
from jax.sharding import PartitionSpec as P


def for_sending(array):

    def short(part):
        return part.astype(jnp.bfloat16) if part.dtype == jnp.float32 else part

    return jax.tree.map(short, array)


def passed_along(value, axis, steps):
    count = lax.axis_size(axis)
    pairs = [(source, (source + steps) % count) for source in range(count)]
    return lax.ppermute(value, axis, pairs)


def passed_along_2(value, axis, steps):
    count = lax.axis_size(axis)
    leading, last = (max(0, -steps), min(count, count - steps))
    return lax.ppermute(value, axis, [(source, source + steps) for source in range(leading, last)])


def coefs(speed, diffuse, opened):
    return (
        (jnp.maximum(speed, 0.0) + diffuse) * opened,
        (jnp.minimum(speed, 0.0) - diffuse) * opened,
    )


def level_next(field):
    return jnp.concatenate([field[:, :, 1:], jnp.zeros_like(field[:, :, :1])], 2)


def level_west(field):
    return jnp.concatenate([jnp.zeros_like(field[:, :, :1]), field[:, :, :-1]], 2)


def advance_faces(conc, table):
    rim_lon = passed_along(for_sending(conc[0:1]), "lon", -1)
    rim_lat = passed_along_2(conc[:, 0:1], "lat", -1)
    nexts = (
        jnp.concatenate([conc[1:], rim_lon], 0),
        jnp.concatenate([conc[:, 1:], rim_lat], 1),
        level_next(conc),
    )
    fluxes = tuple((pair[0] * conc + pair[1] * nearby for pair, nearby in zip(table, nexts)))
    back_lon = passed_along(for_sending(fluxes[0][-1:]), "lon", 1)
    back_lat = passed_along_2(fluxes[1][:, -1:], "lat", 1)
    west_lon = jnp.concatenate([back_lon, fluxes[0][:-1]], 0)
    west_lat = jnp.concatenate([back_lat, fluxes[1][:, :-1]], 1)
    west_level = level_west(fluxes[2])
    return (conc - (fluxes[0] + fluxes[1] + fluxes[2]) + (west_lon + west_lat + west_level), nexts)


def retreat_faces(adjoint, table):
    rim_lon = passed_along(for_sending(adjoint[0:1]), "lon", -1)
    rim_lat = passed_along_2(adjoint[:, 0:1], "lat", -1)
    gaps = (
        jnp.concatenate([adjoint[1:], rim_lon], 0) - adjoint,
        jnp.concatenate([adjoint[:, 1:], rim_lat], 1) - adjoint,
        level_next(adjoint) - adjoint,
    )
    parts = tuple((pair[1] * gap for pair, gap in zip(table, gaps)))
    back_lon = passed_along(for_sending(parts[0][-1:]), "lon", 1)
    back_lat = passed_along_2(parts[1][:, -1:], "lat", 1)
    west_lon = jnp.concatenate([back_lon, parts[0][:-1]], 0)
    west_lat = jnp.concatenate([back_lat, parts[1][:, :-1]], 1)
    west_level = level_west(parts[2])
    gained = table[0][0] * gaps[0] + table[1][0] * gaps[1] + table[2][0] * gaps[2]
    return (adjoint + gained + (west_lon + west_lat + west_level), gaps)


def kappa_term(gaps, conc, nexts, north_open, upper_open):
    return (
        gaps[0] * (conc - nexts[0])
        + gaps[1] * (conc - nexts[1]) * north_open
        + gaps[2] * (conc - nexts[2]) * upper_open
    )


def body(concentration, wind, kappa, observed):
    lat_rows = concentration.shape[1]
    levels = concentration.shape[2]
    upper_open = (lax.broadcasted_iota(jnp.int32, (1, 1, levels), 2) < levels - 1).astype(
        jnp.float32
    )
    lat_place = lax.axis_index("lat") * lat_rows + lax.broadcasted_iota(
        jnp.int32, (1, lat_rows, 1), 1
    )
    north_open = (lat_place < lat_rows * lax.axis_size("lat") - 1).astype(jnp.float32)
    speeds = wind.astype(jnp.float32)
    diffuse = kappa.astype(jnp.float32)
    table = (
        coefs(speeds[0], diffuse, 1.0),
        coefs(speeds[1], diffuse, north_open),
        coefs(speeds[2], diffuse, upper_open),
    )
    middle, nexts_first = advance_faces(concentration, table)
    final, nexts_second = advance_faces(middle, table)
    adjoint = final - observed.astype(jnp.float32)
    adjoint, gaps = retreat_faces(adjoint, table)
    grad_kappa = kappa_term(gaps, middle, nexts_second, north_open, upper_open)
    grad_conc, gaps = retreat_faces(adjoint, table)
    grad_kappa = grad_kappa + kappa_term(gaps, concentration, nexts_first, north_open, upper_open)
    return (grad_conc, grad_kappa)


def solution(mesh):
    return jax.shard_map(
        body,
        mesh=mesh,
        in_specs=(
            P("lon", "lat", None),
            P(None, "lon", "lat", None),
            P("lon", "lat", None),
            P("lon", "lat", None),
        ),
        out_specs=(P("lon", "lat", None), P("lon", "lat", None)),
        check_vma=False,
    )
```

profile of v0, /device:TPU:6, one launch (start us, length us, event | category | flops | bytes accessed | tf_op | source)
XLA Modules:
  0.0 108.8 jit_solution(18118584265102434502)
XLA Ops:
  0.6 0.0 copy-start
  0.7 0.9 slice.142
  1.6 2.7 %collective-permute-start.1 = (f32[8,1,128]{2,1,0:T(1,128)S(1)}, f32[8,1,128]{2,1,0:T(1,128)S(1)}, u32[]{:S(2)}, u32[]{:S(2)}) collective-permute-start(f32[8,1,128]{2,1,0:T(1,128)S(1)} %slice.142), channel_id=1, source_target_pairs={{1,0},{2,1},{3,2},{4,3},{5,4},{6,5},{7,6},{9,8},{10,9},{11,10},{12... | collective-permute-start | bytes 12296 | tf_op jit(solution)/shard_map/ppermute | solution.py:24
  4.3 0.9 slice.286
  5.2 13.0 %collective-permute-start = (bf16[1,224,128]{2,1,0:T(8,128)(2,1)S(1)}, bf16[1,224,128]{2,1,0:T(8,128)(2,1)S(1)}, u32[]{:S(2)}, u32[]{:S(2)}) collective-permute-start(bf16[1,224,128]{2,1,0:T(8,128)(2,1)S(1)} %slice.286), channel_id=1, source_target_pairs={{0,504},{8,0},{16,8},{24,16},{32,24},{40,32},{48,40},{56,48},{64,5... | collective-permute-start | bytes 172040 | tf_op jit(solution)/shard_map/ppermute | solution.py:18
  18.2 1.2 %slice.138 = f32[7,224,128]{2,1,0:T(8,128)S(1)} slice(f32[8,224,128]{2,1,0:T(8,128)} %param.4), slice={[1:8], [0:224], [0:128]} | slice | bytes 1605632 | tf_op jit(solution)/shard_map/slice | solution.py:46
  19.4 1.2 %slice.141 = f32[8,223,128]{2,1,0:T(8,128)S(1)} slice(f32[8,224,128]{2,1,0:T(8,128)} %param.4), slice={[0:8], [1:224], [0:128]} | slice | bytes 1826816 | tf_op jit(solution)/shard_map/slice | solution.py:47
  20.7 0.0 copy-start.1
  20.7 0.3 slice.144
  21.0 0.3 convert_element_type.63
  21.3 0.0 collective-permute-done
  21.3 0.0 collective-permute-done.1
  21.4 0.4 copy-done.1
  21.7 0.8 multiply_add_fusion.3
  22.6 1.9 %collective-permute-start.2 = (bf16[1,224,128]{2,1,0:T(8,128)(2,1)S(1)}, bf16[1,224,128]{2,1,0:T(8,128)(2,1)S(1)}, u32[]{:S(2)}, u32[]{:S(2)}) collective-permute-start(bf16[1,224,128]{2,1,0:T(8,128)(2,1)S(1)} %slice.285), channel_id=1, source_target_pairs={{0,8},{8,16},{16,24},{24,32},{32,40},{40,48},{48,56},{56,64},{64,7... | collective-permute-start | bytes 172040 | tf_op jit(solution)/shard_map/ppermute | solution.py:18
  24.5 5.2 %collective-permute-start.3 = (f32[8,1,128]{2,1,0:T(1,128)S(1)}, f32[8,1,128]{2,1,0:T(1,128)S(1)}, u32[]{:S(2)}, u32[]{:S(2)}) collective-permute-start(f32[8,1,128]{2,1,0:T(1,128)S(1)} %slice.186), channel_id=1, source_target_pairs={{0,1},{1,2},{2,3},{3,4},{4,5},{5,6},{6,7},{8,9},{9,10},{10,11},{11... | collective-permute-start | bytes 12296 | tf_op jit(solution)/shard_map/ppermute | solution.py:24
  29.7 0.1 slice.185
  29.8 3.1 %collective-permute-done.2 = bf16[1,224,128]{2,1,0:T(8,128)(2,1)S(1)} collective-permute-done((bf16[1,224,128]{2,1,0:T(8,128)(2,1)S(1)}, bf16[1,224,128]{2,1,0:T(8,128)(2,1)S(1)}, u32[]{:S(2)}, u32[]{:S(2)}) %collective-permute-start.2) | collective-permute-done | bytes 57376 | tf_op jit(solution)/shard_map/ppermute | solution.py:18
  32.9 0.0 collective-permute-done.3
  32.9 0.7 fusion.5
  33.6 5.1 %collective-permute-start.4 = (bf16[1,224,128]{2,1,0:T(8,128)(2,1)S(1)}, bf16[1,224,128]{2,1,0:T(8,128)(2,1)S(1)}, u32[]{:S(2)}, u32[]{:S(2)}) collective-permute-start(bf16[1,224,128]{2,1,0:T(8,128)(2,1)S(1)} %slice.284), channel_id=1, source_target_pairs={{0,504},{8,0},{16,8},{24,16},{32,24},{40,32},{48,40},{56,48},{64,5... | collective-permute-start | bytes 172040 | tf_op jit(solution)/shard_map/ppermute | solution.py:18
  38.8 1.9 %collective-permute-start.5 = (f32[8,1,128]{2,1,0:T(1,128)S(1)}, f32[8,1,128]{2,1,0:T(1,128)S(1)}, u32[]{:S(2)}, u32[]{:S(2)}) collective-permute-start(f32[8,1,128]{2,1,0:T(1,128)S(1)} %slice.192), channel_id=1, source_target_pairs={{1,0},{2,1},{3,2},{4,3},{5,4},{6,5},{7,6},{9,8},{10,9},{11,10},{12... | collective-permute-start | bytes 12296 | tf_op jit(solution)/shard_map/ppermute | solution.py:24
  40.7 0.1 slice.189
  40.7 0.3 slice.193
  41.0 0.1 slice.191
  41.1 0.0 collective-permute-done.4
  41.1 5.2 %collective-permute-done.5 = f32[8,1,128]{2,1,0:T(1,128)S(1)} collective-permute-done((f32[8,1,128]{2,1,0:T(1,128)S(1)}, f32[8,1,128]{2,1,0:T(1,128)S(1)}, u32[]{:S(2)}, u32[]{:S(2)}) %collective-permute-start.5) | collective-permute-done | bytes 4128 | tf_op jit(solution)/shard_map/ppermute | solution.py:24
  46.4 0.8 multiply_add_fusion
  47.2 1.9 %collective-permute-start.6 = (bf16[1,224,128]{2,1,0:T(8,128)(2,1)S(1)}, bf16[1,224,128]{2,1,0:T(8,128)(2,1)S(1)}, u32[]{:S(2)}, u32[]{:S(2)}) collective-permute-start(bf16[1,224,128]{2,1,0:T(8,128)(2,1)S(1)} %slice.283), channel_id=1, source_target_pairs={{0,8},{8,16},{16,24},{24,32},{32,40},{40,48},{48,56},{56,64},{64,7... | collective-permute-start | bytes 172040 | tf_op jit(solution)/shard_map/ppermute | solution.py:18
  49.2 3.9 %collective-permute-start.7 = (f32[8,1,128]{2,1,0:T(1,128)S(1)}, f32[8,1,128]{2,1,0:T(1,128)S(1)}, u32[]{:S(2)}, u32[]{:S(2)}) collective-permute-start(f32[8,1,128]{2,1,0:T(1,128)S(1)} %slice.196), channel_id=1, source_target_pairs={{0,1},{1,2},{2,3},{3,4},{4,5},{5,6},{6,7},{8,9},{9,10},{10,11},{11... | collective-permute-start | bytes 12296 | tf_op jit(solution)/shard_map/ppermute | solution.py:24
  53.1 0.1 slice.195
  53.1 3.8 %collective-permute-done.6 = bf16[1,224,128]{2,1,0:T(8,128)(2,1)S(1)} collective-permute-done((bf16[1,224,128]{2,1,0:T(8,128)(2,1)S(1)}, bf16[1,224,128]{2,1,0:T(8,128)(2,1)S(1)}, u32[]{:S(2)}, u32[]{:S(2)}) %collective-permute-start.6) | collective-permute-done | bytes 57376 | tf_op jit(solution)/shard_map/ppermute | solution.py:18
  57.0 0.0 collective-permute-done.7
  57.0 0.7 fusion.8
  57.7 4.4 %collective-permute-start.8 = (bf16[1,224,128]{2,1,0:T(8,128)(2,1)S(1)}, bf16[1,224,128]{2,1,0:T(8,128)(2,1)S(1)}, u32[]{:S(2)}, u32[]{:S(2)}) collective-permute-start(bf16[1,224,128]{2,1,0:T(8,128)(2,1)S(1)} %slice.282), channel_id=1, source_target_pairs={{0,504},{8,0},{16,8},{24,16},{32,24},{40,32},{48,40},{56,48},{64,5... | collective-permute-start | bytes 172040 | tf_op jit(solution)/shard_map/ppermute | solution.py:18
  62.1 2.0 %collective-permute-start.9 = (f32[8,1,128]{2,1,0:T(1,128)S(1)}, f32[8,1,128]{2,1,0:T(1,128)S(1)}, u32[]{:S(2)}, u32[]{:S(2)}) collective-permute-start(f32[8,1,128]{2,1,0:T(1,128)S(1)} %slice.202), channel_id=1, source_target_pairs={{1,0},{2,1},{3,2},{4,3},{5,4},{6,5},{7,6},{9,8},{10,9},{11,10},{12... | collective-permute-start | bytes 12296 | tf_op jit(solution)/shard_map/ppermute | solution.py:24
  64.1 0.1 slice.199
  64.1 0.3 slice.203
  64.4 0.1 slice.201
  64.5 0.0 collective-permute-done.8
  64.5 5.2 %collective-permute-done.9 = f32[8,1,128]{2,1,0:T(1,128)S(1)} collective-permute-done((f32[8,1,128]{2,1,0:T(1,128)S(1)}, f32[8,1,128]{2,1,0:T(1,128)S(1)}, u32[]{:S(2)}, u32[]{:S(2)}) %collective-permute-start.9) | collective-permute-done | bytes 4128 | tf_op jit(solution)/shard_map/ppermute | solution.py:24
  69.7 0.5 fusion.16
  70.3 3.9 %collective-permute-start.11 = (f32[8,1,128]{2,1,0:T(1,128)S(1)}, f32[8,1,128]{2,1,0:T(1,128)S(1)}, u32[]{:S(2)}, u32[]{:S(2)}) collective-permute-start(f32[8,1,128]{2,1,0:T(1,128)S(1)} %slice.206), channel_id=1, source_target_pairs={{0,1},{1,2},{2,3},{3,4},{4,5},{5,6},{6,7},{8,9},{9,10},{10,11},{11... | collective-permute-start | bytes 12296 | tf_op jit(solution)/shard_map/ppermute | solution.py:24
  74.2 1.9 %collective-permute-start.10 = (bf16[1,224,128]{2,1,0:T(8,128)(2,1)S(1)}, bf16[1,224,128]{2,1,0:T(8,128)(2,1)S(1)}, u32[]{:S(2)}, u32[]{:S(2)}) collective-permute-start(bf16[1,224,128]{2,1,0:T(8,128)(2,1)S(1)} %slice.281), channel_id=1, source_target_pairs={{0,8},{8,16},{16,24},{24,32},{32,40},{40,48},{48,56},{56,64},{64,7... | collective-permute-start | bytes 172040 | tf_op jit(solution)/shard_map/ppermute | solution.py:18
  76.1 0.1 slice_multiply_fusion.1
  76.2 0.1 slice.205
  76.3 7.6 %collective-permute-done.10 = bf16[1,224,128]{2,1,0:T(8,128)(2,1)S(1)} collective-permute-done((bf16[1,224,128]{2,1,0:T(8,128)(2,1)S(1)}, bf16[1,224,128]{2,1,0:T(8,128)(2,1)S(1)}, u32[]{:S(2)}, u32[]{:S(2)}) %collective-permute-start.10) | collective-permute-done | bytes 57376 | tf_op jit(solution)/shard_map/ppermute | solution.py:18
  83.9 0.0 collective-permute-done.11
  83.9 1.1 fusion.10
  85.0 1.9 %collective-permute-start.12 = (bf16[1,224,128]{2,1,0:T(8,128)(2,1)S(1)}, bf16[1,224,128]{2,1,0:T(8,128)(2,1)S(1)}, u32[]{:S(2)}, u32[]{:S(2)}) collective-permute-start(bf16[1,224,128]{2,1,0:T(8,128)(2,1)S(1)} %slice.280), channel_id=1, source_target_pairs={{0,504},{8,0},{16,8},{24,16},{32,24},{40,32},{48,40},{56,48},{64,5... | collective-permute-start | bytes 172040 | tf_op jit(solution)/shard_map/ppermute | solution.py:18
  87.0 2.0 %collective-permute-start.13 = (f32[8,1,128]{2,1,0:T(1,128)S(1)}, f32[8,1,128]{2,1,0:T(1,128)S(1)}, u32[]{:S(2)}, u32[]{:S(2)}) collective-permute-start(f32[8,1,128]{2,1,0:T(1,128)S(1)} %slice.213), channel_id=1, source_target_pairs={{1,0},{2,1},{3,2},{4,3},{5,4},{6,5},{7,6},{9,8},{10,9},{11,10},{12... | collective-permute-start | bytes 12296 | tf_op jit(solution)/shard_map/ppermute | solution.py:24
  88.9 0.1 slice.210
  89.0 0.3 slice.214
  89.3 0.1 slice.212
  89.4 0.0 collective-permute-done.12
  89.4 5.2 %collective-permute-done.13 = f32[8,1,128]{2,1,0:T(1,128)S(1)} collective-permute-done((f32[8,1,128]{2,1,0:T(1,128)S(1)}, f32[8,1,128]{2,1,0:T(1,128)S(1)}, u32[]{:S(2)}, u32[]{:S(2)}) %collective-permute-start.13) | collective-permute-done | bytes 4128 | tf_op jit(solution)/shard_map/ppermute | solution.py:24
  94.6 0.5 fusion.15
  95.1 1.9 %collective-permute-start.15 = (f32[8,1,128]{2,1,0:T(1,128)S(1)}, f32[8,1,128]{2,1,0:T(1,128)S(1)}, u32[]{:S(2)}, u32[]{:S(2)}) collective-permute-start(f32[8,1,128]{2,1,0:T(1,128)S(1)} %slice.217), channel_id=1, source_target_pairs={{0,1},{1,2},{2,3},{3,4},{4,5},{5,6},{6,7},{8,9},{9,10},{10,11},{11... | collective-permute-start | bytes 12296 | tf_op jit(solution)/shard_map/ppermute | solution.py:24
  97.1 1.9 %collective-permute-start.14 = (bf16[1,224,128]{2,1,0:T(8,128)(2,1)S(1)}, bf16[1,224,128]{2,1,0:T(8,128)(2,1)S(1)}, u32[]{:S(2)}, u32[]{:S(2)}) collective-permute-start(bf16[1,224,128]{2,1,0:T(8,128)(2,1)S(1)} %slice.279), channel_id=1, source_target_pairs={{0,8},{8,16},{16,24},{24,32},{32,40},{40,48},{48,56},{56,64},{64,7... | collective-permute-start | bytes 172040 | tf_op jit(solution)/shard_map/ppermute | solution.py:18
  99.0 3.1 %add_add_fusion = f32[8,224,128]{2,1,0:T(8,128)} fusion(f32[8,224,128]{2,1,0:T(8,128)S(1)} %copy-done, f32[8,224,128]{2,1,0:T(8,128)S(1)} %fusion.5, f32[8,224,127]{2,1,0:T(8,128)S(1)} %slice.193, f32[8,224,127]{2,1,0:T(8,128)S(1)} %slice.144, f32[1,224,128]{2,1,0:T(8,128)S(1)} %convert_element_type.69, f32[7,224,128]{2,1,0:T(8,128)S(1)} %slice.189, ...), kind=kLoop, calls=%fused_computation.33 | loop fusion | flops 8028160 | bytes 15570304 | tf_op jit(solution)/shard_map/add | solution.py:108
  102.1 0.1 slice_multiply_fusion
  102.3 0.1 slice.216
  102.3 4.5 %collective-permute-done.14 = bf16[1,224,128]{2,1,0:T(8,128)(2,1)S(1)} collective-permute-done((bf16[1,224,128]{2,1,0:T(8,128)(2,1)S(1)}, bf16[1,224,128]{2,1,0:T(8,128)(2,1)S(1)}, u32[]{:S(2)}, u32[]{:S(2)}) %collective-permute-start.14) | collective-permute-done | bytes 57376 | tf_op jit(solution)/shard_map/ppermute | solution.py:18
  106.8 2.0 %fusion.12 = f32[8,224,128]{2,1,0:T(8,128)} fusion(f32[7,224,128]{2,1,0:T(8,128)S(1)} %slice.216, f32[1,224,128]{2,1,0:T(8,128)S(1)} %convert_element_type.75, f32[8,223,128]{2,1,0:T(8,128)S(1)} %bitcast.63, f32[8,1,128]{2,1,0:T(1,128)S(1)} %collective-permute-done.15, f32[8,224,127]{2,1,0:T(8,128)S(1)} %slice_multiply_fusion, ...), kind=kLoop, calls=%fused_computation.32 | loop fusion | flops 5734400 | bytes 10538368 | tf_op jit(solution)/shard_map/add | solution.py:74
  (30 shorter events, 0.2 us)
Async XLA Ops:
  0.6 20.0 %copy-start = (f32[8,224,128]{2,1,0:T(8,128)S(1)}, f32[8,224,128]{2,1,0:T(8,128)}, u32[]{:S(2)}) copy-start(f32[8,224,128]{2,1,0:T(8,128)} %param.4) | copy-start | bytes 2752516
  0.6 20.4 %copy-start.2 = (bf16[3,8,224,128]{3,2,1,0:T(8,128)(2,1)S(1)}, bf16[3,8,224,128]{3,2,1,0:T(8,128)(2,1)}, u32[]{:S(2)}) copy-start(bf16[3,8,224,128]{3,2,1,0:T(8,128)(2,1)} %param.5) | copy-start | bytes 4128772
  1.6 19.8 %collective-permute-start.1 = (f32[8,1,128]{2,1,0:T(1,128)S(1)}, f32[8,1,128]{2,1,0:T(1,128)S(1)}, u32[]{:S(2)}, u32[]{:S(2)}) collective-permute-start(f32[8,1,128]{2,1,0:T(1,128)S(1)} %slice.142), channel_id=1, source_target_pairs={{1,0},{2,1},{3,2},{4,3},{5,4},{6,5},{7,6},{9,8},{10,9},{11,10},{12... | collective-permute-start | bytes 12296 | tf_op jit(solution)/shard_map/ppermute | solution.py:24
  5.2 16.1 %collective-permute-start = (bf16[1,224,128]{2,1,0:T(8,128)(2,1)S(1)}, bf16[1,224,128]{2,1,0:T(8,128)(2,1)S(1)}, u32[]{:S(2)}, u32[]{:S(2)}) collective-permute-start(bf16[1,224,128]{2,1,0:T(8,128)(2,1)S(1)} %slice.286), channel_id=1, source_target_pairs={{0,504},{8,0},{16,8},{24,16},{32,24},{40,32},{48,40},{56,48},{64,5... | collective-permute-start | bytes 172040 | tf_op jit(solution)/shard_map/ppermute | solution.py:18
  20.7 1.0 copy-start.1
  22.6 10.3 %collective-permute-start.2 = (bf16[1,224,128]{2,1,0:T(8,128)(2,1)S(1)}, bf16[1,224,128]{2,1,0:T(8,128)(2,1)S(1)}, u32[]{:S(2)}, u32[]{:S(2)}) collective-permute-start(bf16[1,224,128]{2,1,0:T(8,128)(2,1)S(1)} %slice.285), channel_id=1, source_target_pairs={{0,8},{8,16},{16,24},{24,32},{32,40},{40,48},{48,56},{56,64},{64,7... | collective-permute-start | bytes 172040 | tf_op jit(solution)/shard_map/ppermute | solution.py:18
  24.5 8.4 %collective-permute-start.3 = (f32[8,1,128]{2,1,0:T(1,128)S(1)}, f32[8,1,128]{2,1,0:T(1,128)S(1)}, u32[]{:S(2)}, u32[]{:S(2)}) collective-permute-start(f32[8,1,128]{2,1,0:T(1,128)S(1)} %slice.186), channel_id=1, source_target_pairs={{0,1},{1,2},{2,3},{3,4},{4,5},{5,6},{6,7},{8,9},{9,10},{10,11},{11... | collective-permute-start | bytes 12296 | tf_op jit(solution)/shard_map/ppermute | solution.py:24
  33.6 7.5 %collective-permute-start.4 = (bf16[1,224,128]{2,1,0:T(8,128)(2,1)S(1)}, bf16[1,224,128]{2,1,0:T(8,128)(2,1)S(1)}, u32[]{:S(2)}, u32[]{:S(2)}) collective-permute-start(bf16[1,224,128]{2,1,0:T(8,128)(2,1)S(1)} %slice.284), channel_id=1, source_target_pairs={{0,504},{8,0},{16,8},{24,16},{32,24},{40,32},{48,40},{56,48},{64,5... | collective-permute-start | bytes 172040 | tf_op jit(solution)/shard_map/ppermute | solution.py:18
  38.8 7.6 %collective-permute-start.5 = (f32[8,1,128]{2,1,0:T(1,128)S(1)}, f32[8,1,128]{2,1,0:T(1,128)S(1)}, u32[]{:S(2)}, u32[]{:S(2)}) collective-permute-start(f32[8,1,128]{2,1,0:T(1,128)S(1)} %slice.192), channel_id=1, source_target_pairs={{1,0},{2,1},{3,2},{4,3},{5,4},{6,5},{7,6},{9,8},{10,9},{11,10},{12... | collective-permute-start | bytes 12296 | tf_op jit(solution)/shard_map/ppermute | solution.py:24
  46.4 10.6 %copy-start.3 = (bf16[8,224,128]{2,1,0:T(8,128)(2,1)S(1)}, bf16[8,224,128]{2,1,0:T(8,128)(2,1)}, u32[]{:S(2)}) copy-start(bf16[8,224,128]{2,1,0:T(8,128)(2,1)} %param.7) | copy-start | bytes 1376260
  47.2 9.7 %collective-permute-start.6 = (bf16[1,224,128]{2,1,0:T(8,128)(2,1)S(1)}, bf16[1,224,128]{2,1,0:T(8,128)(2,1)S(1)}, u32[]{:S(2)}, u32[]{:S(2)}) collective-permute-start(bf16[1,224,128]{2,1,0:T(8,128)(2,1)S(1)} %slice.283), channel_id=1, source_target_pairs={{0,8},{8,16},{16,24},{24,32},{32,40},{40,48},{48,56},{56,64},{64,7... | collective-permute-start | bytes 172040 | tf_op jit(solution)/shard_map/ppermute | solution.py:18
  49.2 7.8 %collective-permute-start.7 = (f32[8,1,128]{2,1,0:T(1,128)S(1)}, f32[8,1,128]{2,1,0:T(1,128)S(1)}, u32[]{:S(2)}, u32[]{:S(2)}) collective-permute-start(f32[8,1,128]{2,1,0:T(1,128)S(1)} %slice.196), channel_id=1, source_target_pairs={{0,1},{1,2},{2,3},{3,4},{4,5},{5,6},{6,7},{8,9},{9,10},{10,11},{11... | collective-permute-start | bytes 12296 | tf_op jit(solution)/shard_map/ppermute | solution.py:24
  57.7 6.8 %collective-permute-start.8 = (bf16[1,224,128]{2,1,0:T(8,128)(2,1)S(1)}, bf16[1,224,128]{2,1,0:T(8,128)(2,1)S(1)}, u32[]{:S(2)}, u32[]{:S(2)}) collective-permute-start(bf16[1,224,128]{2,1,0:T(8,128)(2,1)S(1)} %slice.282), channel_id=1, source_target_pairs={{0,504},{8,0},{16,8},{24,16},{32,24},{40,32},{48,40},{56,48},{64,5... | collective-permute-start | bytes 172040 | tf_op jit(solution)/shard_map/ppermute | solution.py:18
  62.1 7.6 %collective-permute-start.9 = (f32[8,1,128]{2,1,0:T(1,128)S(1)}, f32[8,1,128]{2,1,0:T(1,128)S(1)}, u32[]{:S(2)}, u32[]{:S(2)}) collective-permute-start(f32[8,1,128]{2,1,0:T(1,128)S(1)} %slice.202), channel_id=1, source_target_pairs={{1,0},{2,1},{3,2},{4,3},{5,4},{6,5},{7,6},{9,8},{10,9},{11,10},{12... | collective-permute-start | bytes 12296 | tf_op jit(solution)/shard_map/ppermute | solution.py:24
  70.3 13.6 %collective-permute-start.11 = (f32[8,1,128]{2,1,0:T(1,128)S(1)}, f32[8,1,128]{2,1,0:T(1,128)S(1)}, u32[]{:S(2)}, u32[]{:S(2)}) collective-permute-start(f32[8,1,128]{2,1,0:T(1,128)S(1)} %slice.206), channel_id=1, source_target_pairs={{0,1},{1,2},{2,3},{3,4},{4,5},{5,6},{6,7},{8,9},{9,10},{10,11},{11... | collective-permute-start | bytes 12296 | tf_op jit(solution)/shard_map/ppermute | solution.py:24
  74.2 9.7 %collective-permute-start.10 = (bf16[1,224,128]{2,1,0:T(8,128)(2,1)S(1)}, bf16[1,224,128]{2,1,0:T(8,128)(2,1)S(1)}, u32[]{:S(2)}, u32[]{:S(2)}) collective-permute-start(bf16[1,224,128]{2,1,0:T(8,128)(2,1)S(1)} %slice.281), channel_id=1, source_target_pairs={{0,8},{8,16},{16,24},{24,32},{32,40},{40,48},{48,56},{56,64},{64,7... | collective-permute-start | bytes 172040 | tf_op jit(solution)/shard_map/ppermute | solution.py:18
  85.0 4.3 %collective-permute-start.12 = (bf16[1,224,128]{2,1,0:T(8,128)(2,1)S(1)}, bf16[1,224,128]{2,1,0:T(8,128)(2,1)S(1)}, u32[]{:S(2)}, u32[]{:S(2)}) collective-permute-start(bf16[1,224,128]{2,1,0:T(8,128)(2,1)S(1)} %slice.280), channel_id=1, source_target_pairs={{0,504},{8,0},{16,8},{24,16},{32,24},{40,32},{48,40},{56,48},{64,5... | collective-permute-start | bytes 172040 | tf_op jit(solution)/shard_map/ppermute | solution.py:18
  87.0 7.6 %collective-permute-start.13 = (f32[8,1,128]{2,1,0:T(1,128)S(1)}, f32[8,1,128]{2,1,0:T(1,128)S(1)}, u32[]{:S(2)}, u32[]{:S(2)}) collective-permute-start(f32[8,1,128]{2,1,0:T(1,128)S(1)} %slice.213), channel_id=1, source_target_pairs={{1,0},{2,1},{3,2},{4,3},{5,4},{6,5},{7,6},{9,8},{10,9},{11,10},{12... | collective-permute-start | bytes 12296 | tf_op jit(solution)/shard_map/ppermute | solution.py:24
  95.1 11.7 %collective-permute-start.15 = (f32[8,1,128]{2,1,0:T(1,128)S(1)}, f32[8,1,128]{2,1,0:T(1,128)S(1)}, u32[]{:S(2)}, u32[]{:S(2)}) collective-permute-start(f32[8,1,128]{2,1,0:T(1,128)S(1)} %slice.217), channel_id=1, source_target_pairs={{0,1},{1,2},{2,3},{3,4},{4,5},{5,6},{6,7},{8,9},{9,10},{10,11},{11... | collective-permute-start | bytes 12296 | tf_op jit(solution)/shard_map/ppermute | solution.py:24
  97.1 9.7 %collective-permute-start.14 = (bf16[1,224,128]{2,1,0:T(8,128)(2,1)S(1)}, bf16[1,224,128]{2,1,0:T(8,128)(2,1)S(1)}, u32[]{:S(2)}, u32[]{:S(2)}) collective-permute-start(bf16[1,224,128]{2,1,0:T(8,128)(2,1)S(1)} %slice.279), channel_id=1, source_target_pairs={{0,8},{8,16},{16,24},{24,32},{32,40},{40,48},{48,56},{56,64},{64,7... | collective-permute-start | bytes 172040 | tf_op jit(solution)/shard_map/ppermute | solution.py:18
where the time goes:
time: 111 us; the launch traced here: 109 us
  starting transfers between devices  55.6 us (50%)
  waiting for transfers between devices  34.6 us (31%)
  other arithmetic  10.9 us (10%)
  local copies, waits for them, and re-layouts  6.51 us (6%)
  between operations  1.19 us (1%)
    ppermute x8, starting transfers between devices, passed_along(): return lax.ppermute(value, axis, pairs)  32.1 us
    ppermute x8, starting transfers between devices, passed_along_2(): lax.ppermute(value, axis, [(source, source + steps) for source in range(l...  23.5 us
    ppermute x8, waiting for transfers between devices, passed_along(): return lax.ppermute(value, axis, pairs)  19 us
    ppermute x8, waiting for transfers between devices, passed_along_2(): lax.ppermute(value, axis, [(source, source + steps) for source in range(l...  15.6 us
    add x1, other arithmetic, body(): grad_kappa + kappa_term(gaps, concentration, nexts_first, north_open, upp...  3.13 us
    add x2, other arithmetic, retreat_faces(): return (adjoint + gained + (west_lon + west_lat + west_level), gaps)  3.02 us
  transfers between devices with their start and end apart: 16, of which 7 were waited for; matrix products, arithmetic and copies ran while one was open for 8% of the time, Pallas kernels for 0%

commit v1 on v0

v1 whole, which is shorter than its diff:
```python
import jax
import jax.numpy as jnp
from jax import lax
from jax.sharding import PartitionSpec as P

HALO = 4


def passed_along(value, axis, steps, periodic):
    count = lax.axis_size(axis)
    if periodic:
        pairs = [(source, (source + steps) % count) for source in range(count)]
    else:
        pairs = [(source, source + steps) for source in range(count) if 0 <= source + steps < count]
    return lax.ppermute(value, axis, pairs)


def pad_rows(part, axis, before, after):
    widths = [(0, 0)] * part.ndim
    widths[axis] = (before, after)
    return jnp.pad(part, widths)


def lon_halo(fields, west_rows, east_rows):
    size = fields[0].shape[0]
    parts = {}
    for key, rows, start in (("east", east_rows, lambda e: 0), ("west", west_rows, lambda w: size - w)):
        pieces = [lax.slice_in_dim(f, start(r), start(r) + r, axis=0) for f, r in zip(fields, rows)]
        wide = pieces[0]
        narrow = jnp.concatenate(pieces[1:], 0)
        parts[key] = passed_along((wide, narrow), "lon", -1 if key == "east" else 1, True)
    out = []
    for key in ("east", "west"):
        wide, narrow = parts[key]
        rows = east_rows if key == "east" else west_rows
        got = [wide]
        at = 0
        for r in rows[1:]:
            got.append(narrow[at:at + r])
            at += r
        parts[key] = got
    for f, w, e, west, east in zip(fields, west_rows, east_rows, parts["west"], parts["east"]):
        west = pad_rows(west, 0, HALO - w, 0)
        east = pad_rows(east, 0, 0, HALO - e)
        out.append(jnp.concatenate([west, f, east], 0))
    return out


def lat_halo(fields):
    size = fields[0].shape[1]
    lows = jnp.stack([f[:, :HALO].astype(jnp.float32) for f in fields])
    highs = jnp.stack([f[:, size - HALO:].astype(jnp.float32) for f in fields])
    from_north = passed_along(lows, "lat", -1, False)
    from_south = passed_along(highs, "lat", 1, False)
    return [
        jnp.concatenate([from_south[n].astype(f.dtype), f, from_north[n].astype(f.dtype)], 1)
        for n, f in enumerate(fields)
    ]


def next_of(field, axis):
    if axis == 2:
        return jnp.concatenate([field[:, :, 1:], jnp.zeros_like(field[:, :, :1])], 2)
    size = field.shape[axis]
    return jnp.concatenate(
        [lax.slice_in_dim(field, 1, size, axis=axis), lax.slice_in_dim(field, size - 1, size, axis=axis)], axis
    )


def back_of(field, axis):
    if axis == 2:
        return jnp.concatenate([jnp.zeros_like(field[:, :, :1]), field[:, :, :-1]], 2)
    size = field.shape[axis]
    return jnp.concatenate(
        [lax.slice_in_dim(field, 0, 1, axis=axis), lax.slice_in_dim(field, 0, size - 1, axis=axis)], axis
    )


def advance(conc, table):
    nexts = tuple(next_of(conc, d) for d in range(3))
    fluxes = tuple(pair[0] * conc + pair[1] * nearby for pair, nearby in zip(table, nexts))
    wests = tuple(back_of(f, d) for d, f in enumerate(fluxes))
    return conc - (fluxes[0] + fluxes[1] + fluxes[2]) + (wests[0] + wests[1] + wests[2]), nexts


def retreat(adjoint, table):
    gaps = tuple(next_of(adjoint, d) - adjoint for d in range(3))
    parts = tuple(pair[1] * gap for pair, gap in zip(table, gaps))
    wests = tuple(back_of(p, d) for d, p in enumerate(parts))
    gained = table[0][0] * gaps[0] + table[1][0] * gaps[1] + table[2][0] * gaps[2]
    return adjoint + gained + (wests[0] + wests[1] + wests[2]), gaps


def kappa_term(gaps, conc, nexts, north_open, upper_open):
    return (
        gaps[0] * (conc - nexts[0])
        + gaps[1] * (conc - nexts[1]) * north_open
        + gaps[2] * (conc - nexts[2]) * upper_open
    )


def coefs(speed, diffuse, opened):
    return (
        (jnp.maximum(speed, 0.0) + diffuse) * opened,
        (jnp.minimum(speed, 0.0) - diffuse) * opened,
    )


def body(concentration, wind, kappa, observed):
    lon_rows, lat_rows, levels = concentration.shape
    lat_total = lat_rows * lax.axis_size("lat")
    fields = [concentration, wind[0], wind[1], wind[2], kappa, observed]
    west_rows = [4, 4, 4, 4, 4, 2]
    east_rows = [4, 3, 3, 3, 3, 2]
    fields = lon_halo(fields, west_rows, east_rows)
    fields = lat_halo(fields)
    conc, a0, a1, a2, kap, obs = fields
    ext_rows = conc.shape[1]

    upper_open = (lax.broadcasted_iota(jnp.int32, (1, 1, levels), 2) < levels - 1).astype(jnp.float32)
    lat_place = (
        lax.axis_index("lat") * lat_rows - HALO + lax.broadcasted_iota(jnp.int32, (1, ext_rows, 1), 1)
    )
    north_open = ((lat_place >= 0) & (lat_place < lat_total - 1)).astype(jnp.float32)
    diffuse = kap.astype(jnp.float32)
    table = (
        coefs(a0.astype(jnp.float32), diffuse, 1.0),
        coefs(a1.astype(jnp.float32), diffuse, north_open),
        coefs(a2.astype(jnp.float32), diffuse, upper_open),
    )
    middle, nexts_first = advance(conc, table)
    final, nexts_second = advance(middle, table)
    adjoint = final - obs.astype(jnp.float32)
    adjoint, gaps = retreat(adjoint, table)
    grad_kappa = kappa_term(gaps, middle, nexts_second, north_open, upper_open)
    grad_conc, gaps = retreat(adjoint, table)
    grad_kappa = grad_kappa + kappa_term(gaps, conc, nexts_first, north_open, upper_open)
    centre = (slice(HALO, HALO + lon_rows), slice(HALO, HALO + lat_rows), slice(None))
    return (grad_conc[centre], grad_kappa[centre])


def solution(mesh):
    return jax.shard_map(
        body,
        mesh=mesh,
        in_specs=(
            P("lon", "lat", None),
            P(None, "lon", "lat", None),
            P("lon", "lat", None),
            P("lon", "lat", None),
        ),
        out_specs=(P("lon", "lat", None), P("lon", "lat", None)),
        check_vma=False,
    )
```

time: 111 us -> 149 us (1.34)
  the two profiles are of different devices: /device:TPU:6 before, /device:TPU:249 now
where the time goes in v1:
time: 149 us; the launch traced here: 148 us
  other arithmetic  60.4 us (41%)
  waiting for transfers between devices  36.7 us (25%)
  local copies, waits for them, and re-layouts  32.2 us (22%)
  starting transfers between devices  17.6 us (12%)
    ppermute x6, waiting for transfers between devices, passed_along(): return lax.ppermute(value, axis, pairs)  36.7 us
    ppermute x6, starting transfers between devices, passed_along(): return lax.ppermute(value, axis, pairs)  17.6 us
    add x6, other arithmetic, advance(): pair[0] * conc + pair[1] * nearby  16.5 us
    unnamed x75, local copies, waits for them, and re-layouts  15.6 us
    mul x6, other arithmetic, retreat(): parts = tuple((pair[1] * gap for pair, gap in zip(table, gaps)))  13.9 us
    add x2, other arithmetic, retreat(): return (adjoint + gained + (wests[0] + wests[1] + wests[2]), gaps)  11.7 us
    add x1, other arithmetic, body(): grad_kappa + kappa_term(gaps, conc, nexts_first, north_open, upper_open)  4.43 us
    mul x2, other arithmetic, coefs(): (jnp.maximum(speed, 0.0) + diffuse) * opened  4.39 us
  transfers between devices with their start and end apart: 6, of which 3 were waited for; matrix products, arithmetic and copies ran while one was open for 8% of the time, Pallas kernels for 0%

profile of v1, /device:TPU:249, one launch (start us, length us, event | category | flops | bytes accessed | tf_op | source)
XLA Modules:
  0.0 148.3 jit_solution(17854482337471540146)
XLA Ops:
  0.6 2.3 %fusion.55 = (f32[4,224,128]{2,1,0:T(8,128)}, f32[4,224,128]{2,1,0:T(8,128)}) fusion(f32[8,224,128]{2,1,0:T(8,128)} %param.4), kind=kLoop, calls=%fused_computation.167 | loop fusion | bytes 1835008 | tf_op jit(solution)/shard_map/slice | solution.py:28
  2.9 6.0 %collective-permute-start = (f32[4,224,128]{2,1,0:T(8,128)}, f32[4,224,128]{2,1,0:T(8,128)}, u32[]{:S(2)}, u32[]{:S(2)}) collective-permute-start(f32[4,224,128]{2,1,0:T(8,128)} %get-tuple-element.32), channel_id=1, source_target_pairs={{0,8},{8,16},{16,24},{24,32},{32,40},{40,48},{48,56},{56,64},{64,7... | collective-permute-start | bytes 1376264 | tf_op jit(solution)/shard_map/ppermute | solution.py:15
  9.0 0.7 bitcast_dynamic-update-slice_fusion.2
  9.7 0.7 bitcast_dynamic-update-slice_fusion.5
  10.4 0.7 bitcast_dynamic-update-slice_fusion.1
  11.1 0.7 bitcast_dynamic-update-slice_fusion
  11.8 0.7 bitcast_dynamic-update-slice_fusion.4
  12.4 0.7 bitcast_dynamic-update-slice_fusion.3
  13.1 0.7 slice_dynamic-update-slice_fusion
  13.8 0.7 slice_dynamic-update-slice_fusion.1
  14.5 0.7 slice_dynamic-update-slice_fusion.3
  15.2 2.0 %collective-permute-start.2 = (bf16[18,224,128]{2,1,0:T(8,128)(2,1)}, bf16[18,224,128]{2,1,0:T(8,128)(2,1)}, u32[]{:S(2)}, u32[]{:S(2)}) collective-permute-start(bf16[18,224,128]{2,1,0:T(8,128)(2,1)} %get-tuple-element.36), channel_id=1, source_target_pairs={{0,8},{8,16},{16,24},{24,32},{32,40},{40,48},{48,56},{56,64},{64,7... | collective-permute-start | bytes 3096584 | tf_op jit(solution)/shard_map/ppermute | solution.py:15
  17.3 2.4 %collective-permute-start.3 = (bf16[14,224,128]{2,1,0:T(8,128)(2,1)}, bf16[14,224,128]{2,1,0:T(8,128)(2,1)S(1)}, u32[]{:S(2)}, u32[]{:S(2)}) collective-permute-start(bf16[14,224,128]{2,1,0:T(8,128)(2,1)} %get-tuple-element.37), channel_id=1, source_target_pairs={{0,504},{8,0},{16,8},{24,16},{32,24},{40,32},{48,40},{56,48},{64,5... | collective-permute-start | bytes 2408456 | tf_op jit(solution)/shard_map/ppermute | solution.py:15
  19.7 1.9 %collective-permute-start.1 = (f32[4,224,128]{2,1,0:T(8,128)}, f32[4,224,128]{2,1,0:T(8,128)}, u32[]{:S(2)}, u32[]{:S(2)}) collective-permute-start(f32[4,224,128]{2,1,0:T(8,128)} %get-tuple-element.31), channel_id=1, source_target_pairs={{0,504},{8,0},{16,8},{24,16},{32,24},{40,32},{48,40},{56,48},{64,5... | collective-permute-start | bytes 1376264 | tf_op jit(solution)/shard_map/ppermute | solution.py:15
  21.7 1.1 constant_dynamic-update-slice_fusion.2
  22.9 30.6 %collective-permute-done.1 = f32[4,224,128]{2,1,0:T(8,128)} collective-permute-done((f32[4,224,128]{2,1,0:T(8,128)}, f32[4,224,128]{2,1,0:T(8,128)}, u32[]{:S(2)}, u32[]{:S(2)}) %collective-permute-start.1) | collective-permute-done | bytes 458784 | tf_op jit(solution)/shard_map/ppermute | solution.py:15
  53.5 1.0 constant_dynamic-update-slice_fusion
  54.7 0.8 copy-done.27
  55.5 0.9 slice.415
  56.5 1.1 slice_select_fusion
  57.6 0.9 slice.414
  58.6 1.4 fusion.54
  60.1 1.0 copy-done.20
  61.1 2.8 %collective-permute-start.5 = (f32[6,16,4,128]{3,2,1,0:T(4,128)S(1)}, f32[6,16,4,128]{3,2,1,0:T(4,128)S(1)}, u32[]{:S(2)}, u32[]{:S(2)}) collective-permute-start(f32[6,16,4,128]{3,2,1,0:T(4,128)S(1)} %get-tuple-element.22), channel_id=1, source_target_pairs={{1,0},{2,1},{3,2},{4,3},{5,4},{6,5},{7,6},{9,8},{10,9},{11,10},{12... | collective-permute-start | bytes 589832 | tf_op jit(solution)/shard_map/ppermute | solution.py:15
  63.9 0.7 slice.491
  64.6 2.5 %collective-permute-start.4 = (f32[6,16,4,128]{3,2,1,0:T(4,128)S(1)}, f32[6,16,4,128]{3,2,1,0:T(4,128)S(1)}, u32[]{:S(2)}, u32[]{:S(2)}) collective-permute-start(f32[6,16,4,128]{3,2,1,0:T(4,128)S(1)} %get-tuple-element.21), channel_id=1, source_target_pairs={{0,1},{1,2},{2,3},{3,4},{4,5},{5,6},{6,7},{8,9},{9,10},{10,11},{11... | collective-permute-start | bytes 589832 | tf_op jit(solution)/shard_map/ppermute | solution.py:15
  67.1 0.5 collective-permute-done.5
  67.5 5.6 %collective-permute-done.4 = f32[6,16,4,128]{3,2,1,0:T(4,128)S(1)} collective-permute-done((f32[6,16,4,128]{3,2,1,0:T(4,128)S(1)}, f32[6,16,4,128]{3,2,1,0:T(4,128)S(1)}, u32[]{:S(2)}, u32[]{:S(2)}) %collective-permute-start.4) | collective-permute-done | bytes 196640 | tf_op jit(solution)/shard_map/ppermute | solution.py:15
  73.3 0.6 slice.431
  74.2 0.8 slice_bitcast_fusion.8
  75.0 0.6 slice_bitcast_fusion.7
  75.6 2.9 %fusion.3 = f32[16,232,128]{2,1,0:T(8,128)S(1)} fusion(f32[1,232,128]{2,1,0:T(8,128)S(1)} %slice.424, f32[15,232,128]{2,1,0:T(8,128)S(1)} %slice.423, f32[16,4,128]{2,1,0:T(4,128)S(1)} %slice_bitcast_fusion.3, f32[16,224,128]{2,1,0:T(8,128)S(1)} %constant_dynamic-update-slice_fusion, f32[16,4,128]{2,1,0:T(4,128)S(1)} %slice_bitcast_fusion.5, ...), kind=kLoop, calls=%fused_computation.23 | loop fusion | flops 14254080 | bytes 7602176 | tf_op jit(solution)/shard_map/add | solution.py:81
  78.5 1.3 copy-done.3
  79.8 1.0 fusion.11
  80.8 2.9 %multiply_add_fusion.1 = f32[16,232,128]{2,1,0:T(8,128)S(1)} fusion(f32[16,232,127]{2,1,0:T(8,128)S(1)} %slice.431, f32[16,4,128]{2,1,0:T(4,128)S(1)} %slice_bitcast_fusion.3, f32[16,224,128]{2,1,0:T(8,128)S(1)} %constant_dynamic-update-slice_fusion, f32[16,4,128]{2,1,0:T(4,128)S(1)} %slice_bitcast_fusion.5, f32[128]{0:T(128)S(1)} %compare_convert_fusion, ...), kind=kLoop, calls=%fused_computation.52 | loop fusion | flops 14729216 | bytes 7587840 | tf_op jit(solution)/shard_map/add | solution.py:81
  83.7 1.3 fusion.7
  85.2 0.5 slice-done.2
  85.8 1.1 fusion.13
  86.9 0.6 slice.441
  87.8 2.7 %fusion.1 = f32[16,232,128]{2,1,0:T(8,128)S(1)} fusion(f32[1,232,128]{2,1,0:T(8,128)S(1)} %slice.438, f32[16,232,128]{2,1,0:T(8,128)S(1)} %fusion.13, f32[15,232,128]{2,1,0:T(8,128)S(1)} %slice.437, bf16[16,4,128]{2,1,0:T(4,128)(2,1)S(1)} %get-tuple-element.47, bf16[4,224,128]{2,1,0:T(8,128)(2,1)S(1)} %slice_select_fusion, ...), kind=kLoop, calls=%fused_computation.21 | loop fusion | flops 13303808 | bytes 7602176 | tf_op jit(solution)/shard_map/add | solution.py:81
  90.5 1.3 copy-done.5
  91.8 3.6 %multiply_add_fusion = f32[16,232,128]{2,1,0:T(8,128)} fusion(f32[16,232,127]{2,1,0:T(8,128)S(1)} %slice.441, f32[16,232,128]{2,1,0:T(8,128)S(1)} %fusion.13, f32[128]{0:T(128)S(1)} %compare_convert_fusion, bf16[16,4,128]{2,1,0:T(4,128)(2,1)S(1)} %get-tuple-element.44, bf16[4,224,128]{2,1,0:T(8,128)(2,1)S(1)} %pad.31, ...), kind=kLoop, calls=%fused_computation.51 | loop fusion | flops 13778944 | bytes 7587840 | tf_op jit(solution)/shard_map/add | solution.py:81
  95.4 3.3 %fusion.5 = f32[16,232,128]{2,1,0:T(8,128)S(1)} fusion(f32[16,1,128]{2,1,0:T(1,128)S(1)} %slice.440, f32[16,232,128]{2,1,0:T(8,128)S(1)} %fusion.13, f32[16,231,128]{2,1,0:T(8,128)S(1)} %slice.439, f32[232]{0:T(256)S(1)} %and_convert_fusion, bf16[16,4,128]{2,1,0:T(4,128)(2,1)S(1)} %get-tuple-element.45, bf16[4,224,128]{2,1,0:T(8,128)(2,1)S(1)} %pad.30, ...), kind=kLoop, calls=%fused_computation.25 | loop fusion | flops 14254080 | bytes 7603104 | tf_op jit(solution)/shard_map/add | solution.py:81
  98.6 0.6 slice.444
  99.2 3.7 %fusion.16 = f32[16,232,128]{2,1,0:T(8,128)S(1)} fusion(f32[15,232,128]{2,1,0:T(8,128)S(1)} %slice-done.4, f32[1,232,128]{2,1,0:T(8,128)S(1)} %slice-done.5, f32[16,231,128]{2,1,0:T(8,128)S(1)} %bitcast.107, f32[16,1,128]{2,1,0:T(1,128)} %slice.444, f32[16,232,127]{2,1,0:T(8,128)} %bitcast.109, f32[16,232,128]{2,1,0:T(8,128)S(1)} %fusion.13, ...), kind=kLoop, calls=%fused_computation.41 | loop fusion | flops 9027584 | bytes 16139776 | tf_op jit(solution)/shard_map/sub | solution.py:133
  103.0 0.6 slice.453
  103.8 2.5 %fusion.20 = (f32[16,232,128]{2,1,0:T(8,128)S(1)}, f32[16,232,128]{2,1,0:T(8,128)S(1)}) fusion(bf16[16,4,128]{2,1,0:T(4,128)(2,1)S(1)} %get-tuple-element.47, bf16[4,224,128]{2,1,0:T(8,128)(2,1)S(1)} %slice_select_fusion, bf16[8,224,128]{2,1,0:T(8,128)(2,1)S(1)} %get-tuple-element.15, bf16[4,224,128]{2,1,0:T(8,128)(2,1)S(1)} %get-tuple-element.20, ...), kind=kLoop, calls=%fused_computation.58 | loop fusion | flops 11878400 | bytes 9502720 | tf_op jit(solution)/shard_map/mul | solution.py:88
  106.3 1.4 slice.455
  107.7 3.1 %fusion.53 = (f32[16,232,128]{2,1,0:T(8,128)S(1)}, f32[16,232,128]{2,1,0:T(8,128)S(1)}, f32[16,232,128]{2,1,0:T(8,128)S(1)}) fusion(f32[232]{0:T(256)S(1)} %and_convert_fusion, bf16[16,4,128]{2,1,0:T(4,128)(2,1)S(1)} %get-tuple-element.45, bf16[4,224,128]{2,1,0:T(8,128)(2,1)S(1)} %pad.30, bf16[8,224,128]{2,1,0:T(8,128)(2,1)S(1)} %get-tuple-element.16, ...), kind=kLoop, calls=%fused_computation.165 | loop fusion | flops 12828672 | bytes 13289888 | tf_op jit(solution)/shard_map/mul | solution.py:88
  110.8 1.5 %slice_multiply_fusion.1 = f32[16,232,127]{2,1,0:T(8,128)} fusion(f32[16,232,128]{2,1,0:T(8,128)S(1)} %get-tuple-element.11, f32[16,232,128]{2,1,0:T(8,128)S(1)} %fusion.11), kind=kLoop, calls=%fused_computation.33 | loop fusion | flops 471424 | bytes 5657088 | tf_op jit(solution)/shard_map/mul | solution.py:88
  112.3 7.2 %fusion.18 = f32[16,232,128]{2,1,0:T(8,128)S(1)} fusion(f32[15,232,128]{2,1,0:T(8,128)} %slice.455, f32[1,232,128]{2,1,0:T(8,128)S(1)} %slice.454, f32[16,231,128]{2,1,0:T(8,128)S(1)} %bitcast.111, f32[16,1,128]{2,1,0:T(1,128)S(1)} %slice.456, f32[16,232,127]{2,1,0:T(8,128)} %slice_multiply_fusion.1, f32[16,232,128]{2,1,0:T(8,128)S(1)} %fusion.16, ...), kind=kLoop, calls=%fused_computation.46 | loop fusion | flops 28508160 | bytes 18977184 | tf_op jit(solution)/shard_map/add | solution.py:91
  119.7 1.8 %slice.464 = f32[16,232,127]{2,1,0:T(8,128)} slice(f32[16,232,128]{2,1,0:T(8,128)S(1)} %fusion.18), slice={[0:16], [0:232], [1:128]} | slice | bytes 3771392 | tf_op jit(solution)/shard_map/slice | solution.py:63
  121.5 2.2 %convert_add_fusion.2 = f32[16,232,128]{2,1,0:T(8,128)} fusion(bf16[16,4,128]{2,1,0:T(4,128)(2,1)S(1)} %get-tuple-element.47, bf16[4,224,128]{2,1,0:T(8,128)(2,1)S(1)} %slice_select_fusion, bf16[8,224,128]{2,1,0:T(8,128)(2,1)S(1)} %get-tuple-element.15, bf16[4,224,128]{2,1,0:T(8,128)(2,1)S(1)} %get-tuple-element.20, ...), kind=kLoop, calls=%fused_computation.5 | loop fusion | flops 10452992 | bytes 3801088 | tf_op jit(solution)/shard_map/add | solution.py:104
  123.6 2.1 %fusion.8 = f32[16,232,128]{2,1,0:T(8,128)} fusion(f32[232]{0:T(256)S(1)} %and_convert_fusion, bf16[16,4,128]{2,1,0:T(4,128)(2,1)S(1)} %get-tuple-element.45, bf16[4,224,128]{2,1,0:T(8,128)(2,1)S(1)} %pad.30, bf16[8,224,128]{2,1,0:T(8,128)(2,1)S(1)} %get-tuple-element.16, bf16[4,224,128]{2,1,0:T(8,128)(2,1)S(1)} %get-tuple-element.19, ...), kind=kLoop, calls=%fused_computation.28 | loop fusion | flops 10928128 | bytes 3802016 | tf_op jit(solution)/shard_map/mul | solution.py:104
  125.7 2.3 %fusion.10 = f32[16,232,128]{2,1,0:T(8,128)} fusion(f32[128]{0:T(128)S(1)} %copy-done.29, bf16[16,4,128]{2,1,0:T(4,128)(2,1)S(1)} %get-tuple-element.44, bf16[4,224,128]{2,1,0:T(8,128)(2,1)S(1)} %pad.31, bf16[8,224,128]{2,1,0:T(8,128)(2,1)S(1)} %get-tuple-element.14, bf16[4,224,128]{2,1,0:T(8,128)(2,1)S(1)} %copy-done.14, ...), kind=kLoop, calls=%fused_computation.30 | loop fusion | flops 10928128 | bytes 3801600 | tf_op jit(solution)/shard_map/mul | solution.py:104
  128.0 3.4 %fusion.19 = (f32[16,232,128]{2,1,0:T(8,128)S(1)}, f32[16,232,128]{2,1,0:T(8,128)}) fusion(bf16[16,4,128]{2,1,0:T(4,128)(2,1)S(1)} %get-tuple-element.47, bf16[4,224,128]{2,1,0:T(8,128)(2,1)S(1)} %slice_select_fusion, bf16[8,224,128]{2,1,0:T(8,128)(2,1)S(1)} %get-tuple-element.15, bf16[4,224,128]{2,1,0:T(8,128)(2,1)S(1)} %get-tuple-element.20, ...), kind=kLoop, calls=%fused_computation.57 | loop fusion | flops 11878400 | bytes 9502720 | tf_op jit(solution)/shard_map/mul | solution.py:88
  131.6 1.4 copy-done.15
  133.0 3.0 %fusion.52 = (f32[16,232,128]{2,1,0:T(8,128)S(1)}, f32[16,232,128]{2,1,0:T(8,128)S(1)}, f32[16,232,128]{2,1,0:T(8,128)S(1)}) fusion(f32[232]{0:T(256)S(1)} %and_convert_fusion, bf16[16,4,128]{2,1,0:T(4,128)(2,1)S(1)} %get-tuple-element.45, bf16[4,224,128]{2,1,0:T(8,128)(2,1)S(1)} %pad.30, bf16[8,224,128]{2,1,0:T(8,128)(2,1)S(1)} %get-tuple-element.16, ...), kind=kLoop, calls=%fused_computation.164 | loop fusion | flops 12828672 | bytes 13289888 | tf_op jit(solution)/shard_map/mul | solution.py:88
  136.4 0.9 copy-done.16
  137.2 1.0 copy-done.8
  138.2 0.5 copy-done.10
  138.8 0.5 copy-done.12
  139.3 4.4 %fusion.27 = f32[8,224,128]{2,1,0:T(8,128)} fusion(f32[16,231,128]{2,1,0:T(8,128)S(1)} %slice.439, f32[16,231,128]{2,1,0:T(8,128)S(1)} %slice.427, f32[15,232,128]{2,1,0:T(8,128)S(1)} %copy-done.12, f32[15,232,128]{2,1,0:T(8,128)S(1)} %copy-done.10, f32[1,232,128]{2,1,0:T(8,128)S(1)} %copy-done.26, f32[1,232,128]{2,1,0:T(8,128)S(1)} %copy-done.24, ...), kind=kLoop, calls=%fused_computation.69 | loop fusion | flops 5734400 | bytes 19632512 | tf_op jit(solution)/shard_map/add | solution.py:137
  143.7 4.5 %fusion.43 = f32[8,224,128]{2,1,0:T(8,128)} fusion(f32[16,232,127]{2,1,0:T(8,128)S(1)} %slice_multiply_fusion, f32[16,232,128]{2,1,0:T(8,128)S(1)} %copy-done.2, f32[15,232,128]{2,1,0:T(8,128)S(1)} %slice.466, f32[1,232,128]{2,1,0:T(8,128)S(1)} %slice.465, f32[16,231,128]{2,1,0:T(8,128)S(1)} %bitcast.110, f32[16,1,128]{2,1,0:T(1,128)S(1)} %slice.467, ...), kind=kLoop, calls=%fused_computation.89 | loop fusion | flops 2523136 | bytes 13026816 | tf_op jit(solution)/shard_map/add | solution.py:91
  (111 shorter events, 2.4 us)
Async XLA Ops:
  0.6 8.3 %copy-start.17 = (bf16[3,8,224,128]{3,2,1,0:T(8,128)(2,1)S(1)}, bf16[3,8,224,128]{3,2,1,0:T(8,128)(2,1)}, u32[]{:S(2)}) copy-start(bf16[3,8,224,128]{3,2,1,0:T(8,128)(2,1)} %param.5) | copy-start | bytes 4128772
  0.6 12.5 %copy-start = (bf16[8,224,128]{2,1,0:T(8,128)(2,1)S(1)}, bf16[8,224,128]{2,1,0:T(8,128)(2,1)}, u32[]{:S(2)}) copy-start(bf16[8,224,128]{2,1,0:T(8,128)(2,1)} %param.6) | copy-start | bytes 1376260
  2.9 11.6 %copy-start.19 = (bf16[8,224,128]{2,1,0:T(8,128)(2,1)S(1)}, bf16[8,224,128]{2,1,0:T(8,128)(2,1)}, u32[]{:S(2)}) copy-start(bf16[8,224,128]{2,1,0:T(8,128)(2,1)} %param.7) | copy-start | bytes 1376260
  2.9 18.8 %collective-permute-start = (f32[4,224,128]{2,1,0:T(8,128)}, f32[4,224,128]{2,1,0:T(8,128)}, u32[]{:S(2)}, u32[]{:S(2)}) collective-permute-start(f32[4,224,128]{2,1,0:T(8,128)} %get-tuple-element.32), channel_id=1, source_target_pairs={{0,8},{8,16},{16,24},{24,32},{32,40},{40,48},{48,56},{56,64},{64,7... | collective-permute-start | bytes 1376264 | tf_op jit(solution)/shard_map/ppermute | solution.py:15
  15.2 7.6 %copy-start.18 = (f32[8,224,128]{2,1,0:T(8,128)S(1)}, f32[8,224,128]{2,1,0:T(8,128)}, u32[]{:S(2)}) copy-start(f32[8,224,128]{2,1,0:T(8,128)} %param.4) | copy-start | bytes 2752516
  15.2 42.4 %collective-permute-start.2 = (bf16[18,224,128]{2,1,0:T(8,128)(2,1)}, bf16[18,224,128]{2,1,0:T(8,128)(2,1)}, u32[]{:S(2)}, u32[]{:S(2)}) collective-permute-start(bf16[18,224,128]{2,1,0:T(8,128)(2,1)} %get-tuple-element.36), channel_id=1, source_target_pairs={{0,8},{8,16},{16,24},{24,32},{32,40},{40,48},{48,56},{56,64},{64,7... | collective-permute-start | bytes 3096584 | tf_op jit(solution)/shard_map/ppermute | solution.py:15
  17.3 37.3 %collective-permute-start.3 = (bf16[14,224,128]{2,1,0:T(8,128)(2,1)}, bf16[14,224,128]{2,1,0:T(8,128)(2,1)S(1)}, u32[]{:S(2)}, u32[]{:S(2)}) collective-permute-start(bf16[14,224,128]{2,1,0:T(8,128)(2,1)} %get-tuple-element.37), channel_id=1, source_target_pairs={{0,504},{8,0},{16,8},{24,16},{32,24},{40,32},{48,40},{56,48},{64,5... | collective-permute-start | bytes 2408456 | tf_op jit(solution)/shard_map/ppermute | solution.py:15
  19.7 33.8 %collective-permute-start.1 = (f32[4,224,128]{2,1,0:T(8,128)}, f32[4,224,128]{2,1,0:T(8,128)}, u32[]{:S(2)}, u32[]{:S(2)}) collective-permute-start(f32[4,224,128]{2,1,0:T(8,128)} %get-tuple-element.31), channel_id=1, source_target_pairs={{0,504},{8,0},{16,8},{24,16},{32,24},{40,32},{48,40},{56,48},{64,5... | collective-permute-start | bytes 1376264 | tf_op jit(solution)/shard_map/ppermute | solution.py:15
  22.9 33.6 %copy-start.31 = (pred[4]{0:T(512)(128)(4,1)S(1)}, pred[4]{0:T(512)(128)(4,1)}, u32[]{:S(2)}) copy-start(pred[4]{0:T(512)(128)(4,1)} %constant.9.clone.1) | copy-start | bytes 16
  54.6 0.9 copy-start.27
  56.5 3.6 %copy-start.21 = (bf16[4,224,128]{2,1,0:T(8,128)(2,1)}, bf16[4,224,128]{2,1,0:T(8,128)(2,1)S(1)}, u32[]{:S(2)}) copy-start(bf16[4,224,128]{2,1,0:T(8,128)(2,1)S(1)} %pad.34) | copy-start | bytes 688132
  58.6 1.6 %copy-start.22 = (bf16[4,224,128]{2,1,0:T(8,128)(2,1)}, bf16[4,224,128]{2,1,0:T(8,128)(2,1)S(1)}, u32[]{:S(2)}) copy-start(bf16[4,224,128]{2,1,0:T(8,128)(2,1)S(1)} %pad.33) | copy-start | bytes 688132
  60.0 30.5 %copy-start.13 = (bf16[4,224,128]{2,1,0:T(8,128)(2,1)}, bf16[4,224,128]{2,1,0:T(8,128)(2,1)S(1)}, u32[]{:S(2)}) copy-start(bf16[4,224,128]{2,1,0:T(8,128)(2,1)S(1)} %get-tuple-element.18) | copy-start | bytes 688132
  60.0 1.1 copy-start.20
  61.1 6.4 %collective-permute-start.5 = (f32[6,16,4,128]{3,2,1,0:T(4,128)S(1)}, f32[6,16,4,128]{3,2,1,0:T(4,128)S(1)}, u32[]{:S(2)}, u32[]{:S(2)}) collective-permute-start(f32[6,16,4,128]{3,2,1,0:T(4,128)S(1)} %get-tuple-element.22), channel_id=1, source_target_pairs={{1,0},{2,1},{3,2},{4,3},{5,4},{6,5},{7,6},{9,8},{10,9},{11,10},{12... | collective-permute-start | bytes 589832 | tf_op jit(solution)/shard_map/ppermute | solution.py:15
  64.6 25.9 %copy-start.28 = (f32[128]{0:T(128)}, f32[128]{0:T(128)S(1)}, u32[]{:S(2)}) copy-start(f32[128]{0:T(128)S(1)} %compare_convert_fusion) | copy-start | bytes 1540
  64.6 8.5 %collective-permute-start.4 = (f32[6,16,4,128]{3,2,1,0:T(4,128)S(1)}, f32[6,16,4,128]{3,2,1,0:T(4,128)S(1)}, u32[]{:S(2)}, u32[]{:S(2)}) collective-permute-start(f32[6,16,4,128]{3,2,1,0:T(4,128)S(1)} %get-tuple-element.21), channel_id=1, source_target_pairs={{0,1},{1,2},{2,3},{3,4},{4,5},{5,6},{6,7},{8,9},{9,10},{10,11},{11... | collective-permute-start | bytes 589832 | tf_op jit(solution)/shard_map/ppermute | solution.py:15
  74.1 4.4 %copy-start.9 = (f32[15,232,128]{2,1,0:T(8,128)}, f32[15,232,128]{2,1,0:T(8,128)S(1)}, u32[]{:S(2)}) copy-start(f32[15,232,128]{2,1,0:T(8,128)S(1)} %slice.423) | copy-start | bytes 5345284
  74.1 4.4 %copy-start.23 = (f32[1,232,128]{2,1,0:T(8,128)}, f32[1,232,128]{2,1,0:T(8,128)S(1)}, u32[]{:S(2)}) copy-start(f32[1,232,128]{2,1,0:T(8,128)S(1)} %slice.424) | copy-start | bytes 356356
  78.5 1.3 copy-start.3
  83.7 1.5 %copy-start.4 = (f32[16,232,128]{2,1,0:T(8,128)S(1)}, f32[16,232,128]{2,1,0:T(8,128)}, u32[]{:S(2)}) copy-start(f32[16,232,128]{2,1,0:T(8,128)} %copy-done.3) | copy-start | bytes 5701636
  83.7 2.0 %slice-start.2 = ((f32[16,232,128]{2,1,0:T(8,128)}), f32[15,232,128]{2,1,0:T(8,128)S(1)}, s32[]{:S(2)}) async-start(f32[16,232,128]{2,1,0:T(8,128)} %copy-done.3), calls=%async_computation.2 | async-start | bytes 3563520 | tf_op jit(solution)/shard_map/slice | solution.py:75
  83.7 2.0 %slice-start.3 = ((f32[16,232,128]{2,1,0:T(8,128)}), f32[1,232,128]{2,1,0:T(8,128)S(1)}, s32[]{:S(2)}) async-start(f32[16,232,128]{2,1,0:T(8,128)} %copy-done.3), calls=%async_computation.3 | async-start | bytes 237568 | tf_op jit(solution)/shard_map/slice | solution.py:75
  87.4 3.0 %copy-start.7 = (f32[16,232,127]{2,1,0:T(8,128)}, f32[16,232,127]{2,1,0:T(8,128)S(1)}, u32[]{:S(2)}) copy-start(f32[16,232,127]{2,1,0:T(8,128)S(1)} %slice.441) | copy-start | bytes 5657092
  87.7 2.7 %copy-start.11 = (f32[15,232,128]{2,1,0:T(8,128)}, f32[15,232,128]{2,1,0:T(8,128)S(1)}, u32[]{:S(2)}) copy-start(f32[15,232,128]{2,1,0:T(8,128)S(1)} %slice.437) | copy-start | bytes 5345284
  87.8 2.7 %copy-start.25 = (f32[1,232,128]{2,1,0:T(8,128)}, f32[1,232,128]{2,1,0:T(8,128)S(1)}, u32[]{:S(2)}) copy-start(f32[1,232,128]{2,1,0:T(8,128)S(1)} %slice.438) | copy-start | bytes 356356
  90.5 1.3 copy-start.5
  95.4 3.9 %copy-start.6 = (f32[16,232,128]{2,1,0:T(8,128)S(1)}, f32[16,232,128]{2,1,0:T(8,128)}, u32[]{:S(2)}) copy-start(f32[16,232,128]{2,1,0:T(8,128)} %copy-done.5) | copy-start | bytes 5701636
  95.4 3.9 %slice-start.4 = ((f32[16,232,128]{2,1,0:T(8,128)}), f32[15,232,128]{2,1,0:T(8,128)S(1)}, s32[]{:S(2)}) async-start(f32[16,232,128]{2,1,0:T(8,128)} %copy-done.5), calls=%async_computation.4 | async-start | bytes 3563520 | tf_op jit(solution)/shard_map/slice | solution.py:75
  95.4 3.9 %slice-start.5 = ((f32[16,232,128]{2,1,0:T(8,128)}), f32[1,232,128]{2,1,0:T(8,128)S(1)}, s32[]{:S(2)}) async-start(f32[16,232,128]{2,1,0:T(8,128)} %copy-done.5), calls=%async_computation.5 | async-start | bytes 237568 | tf_op jit(solution)/shard_map/slice | solution.py:75
  110.8 1.6 %copy-start.14 = (bf16[4,224,128]{2,1,0:T(8,128)(2,1)S(1)}, bf16[4,224,128]{2,1,0:T(8,128)(2,1)}, u32[]{:S(2)}) copy-start(bf16[4,224,128]{2,1,0:T(8,128)(2,1)} %copy-done.13) | copy-start | bytes 688132
  110.8 1.6 %copy-start.29 = (f32[128]{0:T(128)S(1)}, f32[128]{0:T(128)}, u32[]{:S(2)}) copy-start(f32[128]{0:T(128)} %copy-done.28) | copy-start | bytes 1540
  119.5 1.9 %copy-start.1 = (f32[16,232,128]{2,1,0:T(8,128)}, f32[16,232,128]{2,1,0:T(8,128)S(1)}, u32[]{:S(2)}) copy-start(f32[16,232,128]{2,1,0:T(8,128)S(1)} %fusion.18) | copy-start | bytes 5701636
  125.7 2.3 %copy-start.2 = (f32[16,232,128]{2,1,0:T(8,128)S(1)}, f32[16,232,128]{2,1,0:T(8,128)}, u32[]{:S(2)}) copy-start(f32[16,232,128]{2,1,0:T(8,128)} %copy-done.1) | copy-start | bytes 5701636
  125.7 2.3 %slice-start = ((f32[16,232,128]{2,1,0:T(8,128)}), f32[15,232,128]{2,1,0:T(8,128)S(1)}, s32[]{:S(2)}) async-start(f32[16,232,128]{2,1,0:T(8,128)} %copy-done.1), calls=%async_computation | async-start | bytes 3563520 | tf_op jit(solution)/shard_map/slice | solution.py:66
  125.7 2.3 %slice-start.1 = ((f32[16,232,128]{2,1,0:T(8,128)}), f32[1,232,128]{2,1,0:T(8,128)S(1)}, s32[]{:S(2)}) async-start(f32[16,232,128]{2,1,0:T(8,128)} %copy-done.1), calls=%async_computation.1 | async-start | bytes 237568 | tf_op jit(solution)/shard_map/slice | solution.py:66
  131.4 1.5 %copy-start.15 = (f32[16,232,127]{2,1,0:T(8,128)S(1)}, f32[16,232,127]{2,1,0:T(8,128)}, u32[]{:S(2)}) copy-start(f32[16,232,127]{2,1,0:T(8,128)} %slice.464) | copy-start | bytes 5657092
  136.0 1.2 copy-start.16
  136.0 2.2 %copy-start.8 = (f32[16,232,127]{2,1,0:T(8,128)S(1)}, f32[16,232,127]{2,1,0:T(8,128)}, u32[]{:S(2)}) copy-start(f32[16,232,127]{2,1,0:T(8,128)} %copy-done.7) | copy-start | bytes 5657092
  136.0 2.7 %copy-start.10 = (f32[15,232,128]{2,1,0:T(8,128)S(1)}, f32[15,232,128]{2,1,0:T(8,128)}, u32[]{:S(2)}) copy-start(f32[15,232,128]{2,1,0:T(8,128)} %copy-done.9) | copy-start | bytes 5345284
  136.0 3.3 %copy-start.12 = (f32[15,232,128]{2,1,0:T(8,128)S(1)}, f32[15,232,128]{2,1,0:T(8,128)}, u32[]{:S(2)}) copy-start(f32[15,232,128]{2,1,0:T(8,128)} %copy-done.11) | copy-start | bytes 5345284
  136.0 3.2 %copy-start.24 = (f32[1,232,128]{2,1,0:T(8,128)S(1)}, f32[1,232,128]{2,1,0:T(8,128)}, u32[]{:S(2)}) copy-start(f32[1,232,128]{2,1,0:T(8,128)} %copy-done.23) | copy-start | bytes 356356
  136.1 3.2 %copy-start.26 = (f32[1,232,128]{2,1,0:T(8,128)S(1)}, f32[1,232,128]{2,1,0:T(8,128)}, u32[]{:S(2)}) copy-start(f32[1,232,128]{2,1,0:T(8,128)} %copy-done.25) | copy-start | bytes 356356
  136.1 3.2 %copy-start.30 = (f32[224]{0:T(256)S(1)}, f32[224]{0:T(256)}, u32[]{:S(2)}) copy-start(f32[224]{0:T(256)} %slice.491) | copy-start | bytes 2692

commit v2 on v1

v2 whole, which is shorter than its diff:
```python
import jax
import jax.numpy as jnp
from jax import lax
from jax.experimental import pallas as pl
from jax.experimental.pallas import tpu as pltpu
from jax.sharding import PartitionSpec as P

HALO = 4
PAD = 8


def passed_along(value, axis, steps, periodic):
    count = lax.axis_size(axis)
    if periodic:
        pairs = [(source, (source + steps) % count) for source in range(count)]
    else:
        pairs = [(source, source + steps) for source in range(count) if 0 <= source + steps < count]
    return lax.ppermute(value, axis, pairs)


def pad_rows(part, axis, before, after):
    widths = [(0, 0)] * part.ndim
    widths[axis] = (before, after)
    return jnp.pad(part, widths)


def lon_halo(fields, west_rows, east_rows):
    size = fields[0].shape[0]
    parts = {}
    for key, rows, start in (("east", east_rows, lambda e: 0), ("west", west_rows, lambda w: size - w)):
        pieces = [lax.slice_in_dim(f, start(r), start(r) + r, axis=0) for f, r in zip(fields, rows)]
        wide = pieces[0]
        narrow = jnp.concatenate(pieces[1:], 0)
        parts[key] = passed_along((wide, narrow), "lon", -1 if key == "east" else 1, True)
    out = []
    for key in ("east", "west"):
        wide, narrow = parts[key]
        rows = east_rows if key == "east" else west_rows
        got = [wide]
        at = 0
        for r in rows[1:]:
            got.append(narrow[at:at + r])
            at += r
        parts[key] = got
    for f, w, e, west, east in zip(fields, west_rows, east_rows, parts["west"], parts["east"]):
        west = pad_rows(west, 0, HALO - w, 0)
        east = pad_rows(east, 0, 0, HALO - e)
        out.append(jnp.concatenate([west, f, east], 0))
    return out


def lat_halo(fields):
    size = fields[0].shape[1]
    lows = jnp.stack([f[:, :HALO].astype(jnp.float32) for f in fields])
    highs = jnp.stack([f[:, size - HALO:].astype(jnp.float32) for f in fields])
    from_north = passed_along(lows, "lat", -1, False)
    from_south = passed_along(highs, "lat", 1, False)
    out = []
    for n, f in enumerate(fields):
        gap = jnp.zeros(f.shape[:1] + (PAD - HALO,) + f.shape[2:], f.dtype)
        out.append(jnp.concatenate([gap, from_south[n].astype(f.dtype), f, from_north[n].astype(f.dtype), gap], 1))
    return out


def stencil_kernel(conc_ref, wind_ref, kappa_ref, obs_ref, north_ref, gc_ref, gk_ref,
                   own_ref, oth_ref, mid_ref, lam2_ref, lam1_ref):
    rows, lats, levels = conc_ref.shape
    f32 = jnp.float32
    north_open = north_ref[...]
    upper_open = (lax.broadcasted_iota(jnp.int32, (lats, levels), 1) < levels - 1).astype(f32)

    def next_lat(f):
        return pltpu.roll(f, lats - 1, 0)

    def back_lat(f):
        return pltpu.roll(f, 1, 0)

    def next_lev(f):
        return pltpu.roll(f, levels - 1, 1)

    def back_lev(f):
        return pltpu.roll(f, 1, 1)

    def coef_row(i, carry):
        diffuse = kappa_ref[i].astype(f32)
        for d, opened in ((0, None), (1, north_open), (2, upper_open)):
            speed = wind_ref[d, i].astype(f32)
            own = jnp.maximum(speed, 0.0) + diffuse
            oth = jnp.minimum(speed, 0.0) - diffuse
            if opened is not None:
                own = own * opened
                oth = oth * opened
            own_ref[d, i] = own
            oth_ref[d, i] = oth
        return carry

    lax.fori_loop(0, rows, coef_row, 0)

    def flux0(src, i):
        return own_ref[0, i] * src[i] + oth_ref[0, i] * src[i + 1]

    def advance(src, dst, lo, hi, minus=None):
        def row(i, west0):
            c = src[i]
            f0 = own_ref[0, i] * c + oth_ref[0, i] * src[i + 1]
            f1 = own_ref[1, i] * c + oth_ref[1, i] * next_lat(c)
            f2 = own_ref[2, i] * c + oth_ref[2, i] * next_lev(c)
            out = c - (f0 + f1 + f2) + (west0 + back_lat(f1) + back_lev(f2))
            if minus is not None:
                out = out - minus[i].astype(f32)
            dst[i] = out
            return f0

        lax.fori_loop(lo, hi, row, flux0(src, lo - 1))

    def part0(src, i):
        return oth_ref[0, i] * (src[i + 1] - src[i])

    def retreat_row(src, i, west0):
        lam = src[i]
        g0 = src[i + 1] - lam
        g1 = next_lat(lam) - lam
        g2 = next_lev(lam) - lam
        p0 = oth_ref[0, i] * g0
        p1 = oth_ref[1, i] * g1
        p2 = oth_ref[2, i] * g2
        gained = own_ref[0, i] * g0 + own_ref[1, i] * g1 + own_ref[2, i] * g2
        return lam + gained + (west0 + back_lat(p1) + back_lev(p2)), p0, (g0, g1, g2)

    def kappa_term(gaps, state, i):
        c = state[i]
        return (
            gaps[0] * (c - state[i + 1])
            + gaps[1] * (c - next_lat(c)) * north_open
            + gaps[2] * (c - next_lev(c)) * upper_open
        )

    h = (rows - gc_ref.shape[0]) // 2
    advance(conc_ref, mid_ref, 1, rows - 1)
    advance(mid_ref, lam2_ref, 2, rows - 2, minus=obs_ref)

    def lam1_row(i, west0):
        out, p0, _ = retreat_row(lam2_ref, i, west0)
        lam1_ref[i] = out
        return p0

    lax.fori_loop(3, rows - 3, lam1_row, part0(lam2_ref, 2))

    def last_row(i, west0):
        out, p0, gaps1 = retreat_row(lam1_ref, i, west0)
        lam = lam2_ref[i]
        gaps2 = (lam2_ref[i + 1] - lam, next_lat(lam) - lam, next_lev(lam) - lam)
        kappa = kappa_term(gaps2, mid_ref, i) + kappa_term(gaps1, conc_ref, i)
        gc_ref[i - h] = out[PAD:lats - PAD]
        gk_ref[i - h] = kappa[PAD:lats - PAD]
        return p0

    lax.fori_loop(h, rows - h, last_row, part0(lam1_ref, h - 1))


def body(concentration, wind, kappa, observed):
    lon_rows, lat_rows, levels = concentration.shape
    lat_total = lat_rows * lax.axis_size("lat")
    fields = [concentration, wind[0], wind[1], wind[2], kappa, observed]
    west_rows = [4, 4, 4, 4, 4, 2]
    east_rows = [4, 3, 3, 3, 3, 2]
    fields = lon_halo(fields, west_rows, east_rows)
    fields = lat_halo(fields)
    conc, a0, a1, a2, kap, obs = fields
    ext_rows, ext_lats = conc.shape[0], conc.shape[1]
    lat_place = lax.axis_index("lat") * lat_rows - PAD + lax.broadcasted_iota(jnp.int32, (ext_lats, levels), 0)
    north_open = ((lat_place >= 0) & (lat_place < lat_total - 1)).astype(jnp.float32)
    winds = jnp.stack([a0, a1, a2])
    whole = [conc, winds, kap, obs, north_open]
    vmem = pltpu.MemorySpace.VMEM
    state = pltpu.VMEM((ext_rows, ext_lats, levels), jnp.float32)
    return pl.pallas_call(
        stencil_kernel,
        out_shape=(
            jax.ShapeDtypeStruct((lon_rows, lat_rows, levels), jnp.float32),
            jax.ShapeDtypeStruct((lon_rows, lat_rows, levels), jnp.float32),
        ),
        in_specs=[pl.BlockSpec(memory_space=vmem) for _ in whole],
        out_specs=(pl.BlockSpec(memory_space=vmem), pl.BlockSpec(memory_space=vmem)),
        scratch_shapes=[
            pltpu.VMEM((3, ext_rows, ext_lats, levels), jnp.float32),
            pltpu.VMEM((3, ext_rows, ext_lats, levels), jnp.float32),
            state,
            state,
            state,
        ],
        compiler_params=pltpu.CompilerParams(vmem_limit_bytes=56 * 1024 * 1024),
    )(*whole)


def solution(mesh):
    return jax.shard_map(
        body,
        mesh=mesh,
        in_specs=(
            P("lon", "lat", None),
            P(None, "lon", "lat", None),
            P("lon", "lat", None),
            P("lon", "lat", None),
        ),
        out_specs=(P("lon", "lat", None), P("lon", "lat", None)),
        check_vma=False,
    )
```

time: 149 us -> 108 us (0.72)
  the two profiles are of different devices: /device:TPU:249 before, /device:TPU:6 now
where the time goes in v2:
time: 108 us
  waiting for transfers between devices  35.2 us (33%)
  local copies, waits for them, and re-layouts  28.3 us (26%)
  starting transfers between devices  25.8 us (24%)
  Pallas kernels  14.6 us (14%)
  other arithmetic  2.59 us (2%)
    ppermute x6, waiting for transfers between devices, passed_along(): return lax.ppermute(value, axis, pairs)  35.2 us
    ppermute x6, starting transfers between devices, passed_along(): return lax.ppermute(value, axis, pairs)  25.8 us
    concatenate x6, local copies, waits for them, and re-layouts, lat_halo(): jnp.concatenate([gap, from_south[n].astype(f.dtype), f, from_north[n].ast...  24.4 us
    pallas_call x1, Pallas kernels, body(): pl.pallas_call(stencil_kernel, out_shape=(jax.ShapeDtypeStruct((lon_rows,...  14.6 us
  transfers between devices with their start and end apart: 6, of which 5 were waited for; matrix products, arithmetic and copies ran while one was open for 1% of the time, Pallas kernels for 0%

profile of v2, /device:TPU:6, one launch (start us, length us, event | category | flops | bytes accessed | tf_op | source)
XLA Modules:
  0.0 107.6 jit_solution(1898973837154296126)
XLA Ops:
  0.6 0.0 copy-start
  0.6 0.0 copy-start.6
  0.6 1.4 %fusion.11 = (f32[4,224,128]{2,1,0:T(8,128)S(1)}, f32[4,224,128]{2,1,0:T(8,128)S(1)}) fusion(f32[8,224,128]{2,1,0:T(8,128)} %param.4), kind=kLoop, calls=%fused_computation.69 | loop fusion | bytes 1835008 | tf_op jit(solution)/shard_map/slice | solution.py:31
  2.0 0.0 copy-start.7
  2.0 2.1 %collective-permute-start = (f32[4,224,128]{2,1,0:T(8,128)S(1)}, f32[4,224,128]{2,1,0:T(8,128)S(1)}, u32[]{:S(2)}, u32[]{:S(2)}) collective-permute-start(f32[4,224,128]{2,1,0:T(8,128)S(1)} %get-tuple-element.22), channel_id=1, source_target_pairs={{0,8},{8,16},{16,24},{24,32},{32,40},{40,48},{48,56},{56,64},{64,7... | collective-permute-start | bytes 1376264 | tf_op jit(solution)/shard_map/ppermute | solution.py:18
  4.1 13.3 %collective-permute-start.1 = (f32[4,224,128]{2,1,0:T(8,128)S(1)}, f32[4,224,128]{2,1,0:T(8,128)S(1)}, u32[]{:S(2)}, u32[]{:S(2)}) collective-permute-start(f32[4,224,128]{2,1,0:T(8,128)S(1)} %get-tuple-element.21), channel_id=1, source_target_pairs={{0,504},{8,0},{16,8},{24,16},{32,24},{40,32},{48,40},{56,48},{64,5... | collective-permute-start | bytes 1376264 | tf_op jit(solution)/shard_map/ppermute | solution.py:18
  17.4 0.0 copy-done
  17.6 0.0 copy-done.6
  17.7 0.0 copy-done.7
  17.7 2.6 %collective-permute-start.3 = (bf16[14,224,128]{2,1,0:T(8,128)(2,1)S(1)}, bf16[14,224,128]{2,1,0:T(8,128)(2,1)S(1)}, u32[]{:S(2)}, u32[]{:S(2)}) collective-permute-start(bf16[14,224,128]{2,1,0:T(8,128)(2,1)S(1)} %get-tuple-element.27), channel_id=1, source_target_pairs={{0,504},{8,0},{16,8},{24,16},{32,24},{40,32},{48,40},{56,48},{64,5... | collective-permute-start | bytes 2408456 | tf_op jit(solution)/shard_map/ppermute | solution.py:18
  20.3 0.0 copy-start.4
  20.3 2.1 %collective-permute-start.2 = (bf16[18,224,128]{2,1,0:T(8,128)(2,1)S(1)}, bf16[18,224,128]{2,1,0:T(8,128)(2,1)S(1)}, u32[]{:S(2)}, u32[]{:S(2)}) collective-permute-start(bf16[18,224,128]{2,1,0:T(8,128)(2,1)S(1)} %get-tuple-element.26), channel_id=1, source_target_pairs={{0,8},{8,16},{16,24},{24,32},{32,40},{40,48},{48,56},{56,64},{64,7... | collective-permute-start | bytes 3096584 | tf_op jit(solution)/shard_map/ppermute | solution.py:18
  22.4 0.1 slice_bitcast_fusion
  22.5 0.0 copy-start.8
  22.5 4.0 %collective-permute-done = f32[4,224,128]{2,1,0:T(8,128)S(1)} collective-permute-done((f32[4,224,128]{2,1,0:T(8,128)S(1)}, f32[4,224,128]{2,1,0:T(8,128)S(1)}, u32[]{:S(2)}, u32[]{:S(2)}) %collective-permute-start) | collective-permute-done | bytes 458784 | tf_op jit(solution)/shard_map/ppermute | solution.py:18
  26.5 0.0 copy-done.4
  26.6 0.1 constant_dynamic-update-slice_fusion.1
  26.6 0.0 collective-permute-done.1
  26.7 0.0 copy-start.5
  26.7 14.7 %collective-permute-done.3 = bf16[14,224,128]{2,1,0:T(8,128)(2,1)S(1)} collective-permute-done((bf16[14,224,128]{2,1,0:T(8,128)(2,1)S(1)}, bf16[14,224,128]{2,1,0:T(8,128)(2,1)S(1)}, u32[]{:S(2)}, u32[]{:S(2)}) %collective-permute-start.3) | collective-permute-done | bytes 802848 | tf_op jit(solution)/shard_map/ppermute | solution.py:18
  41.4 0.0 copy-done.8
  41.4 0.1 slice_select_fusion
  41.6 10.1 %collective-permute-done.2 = bf16[18,224,128]{2,1,0:T(8,128)(2,1)S(1)} collective-permute-done((bf16[18,224,128]{2,1,0:T(8,128)(2,1)S(1)}, bf16[18,224,128]{2,1,0:T(8,128)(2,1)S(1)}, u32[]{:S(2)}, u32[]{:S(2)}) %collective-permute-start.2) | collective-permute-done | bytes 1032224 | tf_op jit(solution)/shard_map/ppermute | solution.py:18
  51.7 0.1 fusion.10
  51.7 0.0 copy-done.5
  51.7 0.1 fusion.9
  51.8 0.0 copy-start.2
  51.8 0.1 fusion.6
  51.9 0.0 copy-start.1
  51.9 0.1 pad_maximum_fusion.1
  52.1 0.0 copy-start.3
  52.1 1.1 %copy-done.3 = bf16[16,224,128]{2,1,0:T(8,128)(2,1)} copy-done((bf16[16,224,128]{2,1,0:T(8,128)(2,1)}, bf16[16,224,128]{2,1,0:T(8,128)(2,1)S(1)}, u32[]{:S(2)}) %copy-start.3) | copy-done | bytes 917528
  53.2 0.1 fusion.7
  53.4 0.0 copy-done.2
  53.4 0.0 copy-done.1
  53.4 2.6 %collective-permute-start.4 = (f32[6,16,4,128]{3,2,1,0:T(4,128)S(1)}, f32[6,16,4,128]{3,2,1,0:T(4,128)S(1)}, u32[]{:S(2)}, u32[]{:S(2)}) collective-permute-start(f32[6,16,4,128]{3,2,1,0:T(4,128)S(1)} %get-tuple-element.12), channel_id=1, source_target_pairs={{0,1},{1,2},{2,3},{3,4},{4,5},{5,6},{6,7},{8,9},{9,10},{10,11},{11... | collective-permute-start | bytes 589832 | tf_op jit(solution)/shard_map/ppermute | solution.py:18
  56.1 3.2 %collective-permute-start.5 = (f32[6,16,4,128]{3,2,1,0:T(4,128)S(1)}, f32[6,16,4,128]{3,2,1,0:T(4,128)S(1)}, u32[]{:S(2)}, u32[]{:S(2)}) collective-permute-start(f32[6,16,4,128]{3,2,1,0:T(4,128)S(1)} %get-tuple-element.11), channel_id=1, source_target_pairs={{1,0},{2,1},{3,2},{4,3},{5,4},{6,5},{7,6},{9,8},{10,9},{11,10},{12... | collective-permute-start | bytes 589832 | tf_op jit(solution)/shard_map/ppermute | solution.py:18
  59.3 1.7 %collective-permute-done.4 = f32[6,16,4,128]{3,2,1,0:T(4,128)S(1)} collective-permute-done((f32[6,16,4,128]{3,2,1,0:T(4,128)S(1)}, f32[6,16,4,128]{3,2,1,0:T(4,128)S(1)}, u32[]{:S(2)}, u32[]{:S(2)}) %collective-permute-start.4) | collective-permute-done | bytes 196640 | tf_op jit(solution)/shard_map/ppermute | solution.py:18
  61.1 4.7 %collective-permute-done.5 = f32[6,16,4,128]{3,2,1,0:T(4,128)S(1)} collective-permute-done((f32[6,16,4,128]{3,2,1,0:T(4,128)S(1)}, f32[6,16,4,128]{3,2,1,0:T(4,128)S(1)}, u32[]{:S(2)}, u32[]{:S(2)}) %collective-permute-start.5) | collective-permute-done | bytes 196640 | tf_op jit(solution)/shard_map/ppermute | solution.py:18
  65.8 0.4 concatenate.53
  66.2 0.4 concatenate.52
  66.6 3.9 %concatenate.51 = bf16[16,240,128]{2,1,0:T(8,128)(2,1)S(1)} concatenate(bf16[16,4,128]{2,1,0:T(4,128)(2,1)S(1)} %broadcast.29, bf16[16,4,128]{2,1,0:T(4,128)(2,1)S(1)} %get-tuple-element.37, bf16[16,224,128]{2,1,0:T(8,128)(2,1)} %copy-done.3, bf16[16,4,128]{2,1,0:T(4,128)(2,1)S(1)} %get-tuple-element.32, bf16[16,4,128]{2,1,0:T(4,128)(2,1)S(1)} %broadcast.29), dimensions={1} | concatenate | bytes 1966080 | tf_op jit(solution)/shard_map/concatenate | solution.py:61
  70.5 6.4 %concatenate.54.kappa_ref = bf16[16,240,128]{2,1,0:T(8,128)(2,1)} concatenate(bf16[16,4,128]{2,1,0:T(4,128)(2,1)S(1)} %broadcast.29, bf16[16,4,128]{2,1,0:T(4,128)(2,1)S(1)} %get-tuple-element.34, bf16[16,224,128]{2,1,0:T(8,128)(2,1)} %copy-done.2, bf16[16,4,128]{2,1,0:T(4,128)(2,1)S(1)} %get-tuple-element.29, bf16[16,4,128]{2,1,0:T(4,128)(2,1)S(1)} %broadcast.29), dimensions={1} | concatenate | bytes 1966080 | tf_op jit(solution)/shard_map/concatenate | solution.py:61
  76.9 6.4 %concatenate.55.obs_ref = bf16[16,240,128]{2,1,0:T(8,128)(2,1)} concatenate(bf16[16,4,128]{2,1,0:T(4,128)(2,1)S(1)} %broadcast.29, bf16[16,4,128]{2,1,0:T(4,128)(2,1)S(1)} %get-tuple-element.33, bf16[16,224,128]{2,1,0:T(8,128)(2,1)} %copy-done.1, bf16[16,4,128]{2,1,0:T(4,128)(2,1)S(1)} %get-tuple-element.28, bf16[16,4,128]{2,1,0:T(4,128)(2,1)S(1)} %broadcast.29), dimensions={1} | concatenate | bytes 1966080 | tf_op jit(solution)/shard_map/concatenate | solution.py:61
  83.3 6.9 %concatenate.50.conc_ref = f32[16,240,128]{2,1,0:T(8,128)} concatenate(f32[16,4,128]{2,1,0:T(4,128)S(1)} %broadcast_in_dim.3, f32[16,4,128]{2,1,0:T(4,128)S(1)} %slice_bitcast_fusion.5, f32[16,224,128]{2,1,0:T(8,128)} %copy-done.5, f32[16,4,128]{2,1,0:T(4,128)S(1)} %slice_bitcast_fusion.3, f32[16,4,128]{2,1,0:T(4,128)S(1)} %broadcast_in_dim.3), dimensions={1} | concatenate | bytes 3932160 | tf_op jit(solution)/shard_map/concatenate | solution.py:61
  90.2 1.9 %pad_maximum_fusion.wind_ref = bf16[3,16,240,128]{3,2,1,0:T(8,128)(2,1)} fusion(bf16[1,16,240,128]{3,2,1,0:T(8,128)(2,1)S(1)} %bitcast.103, bf16[1,16,240,128]{3,2,1,0:T(8,128)(2,1)S(1)} %bitcast.104, bf16[1,16,240,128]{3,2,1,0:T(8,128)(2,1)S(1)} %bitcast.105), kind=kLoop, calls=%fused_computation | loop fusion | flops 2949120 | bytes 5898240 | tf_op jit(solution)/shard_map/stack | solution.py:173
  92.2 0.7 iota.7.north_ref
  92.9 14.6 %shard_map.59 = (f32[8,224,128]{2,1,0:T(8,128)}, f32[8,224,128]{2,1,0:T(8,128)}) custom-call(f32[16,240,128]{2,1,0:T(8,128)} %concatenate.50.conc_ref, bf16[3,16,240,128]{3,2,1,0:T(8,128)(2,1)} %pad_maximum_fusion.wind_ref, bf16[16,240,128]{2,1,0:T(8,128)(2,1)} %concatenate.54.kappa_ref, bf16[16,240,128]{2,1,0:T(8,128)(2,1)} %concatenate.55.obs_ref, ...), custom_call_target="tpu_custom_call" | custom-call | tf_op jit(solution)/shard_map/pallas_call | solution.py:177
  (29 shorter events, 0.6 us)
Async XLA Ops:
  0.6 16.7 %copy-start = (bf16[3,8,224,128]{3,2,1,0:T(8,128)(2,1)S(1)}, bf16[3,8,224,128]{3,2,1,0:T(8,128)(2,1)}, u32[]{:S(2)}) copy-start(bf16[3,8,224,128]{3,2,1,0:T(8,128)(2,1)} %param.5) | copy-start | bytes 4128772
  0.6 16.9 %copy-start.6 = (bf16[8,224,128]{2,1,0:T(8,128)(2,1)S(1)}, bf16[8,224,128]{2,1,0:T(8,128)(2,1)}, u32[]{:S(2)}) copy-start(bf16[8,224,128]{2,1,0:T(8,128)(2,1)} %param.6) | copy-start | bytes 1376260
  2.0 15.6 %copy-start.7 = (bf16[8,224,128]{2,1,0:T(8,128)(2,1)S(1)}, bf16[8,224,128]{2,1,0:T(8,128)(2,1)}, u32[]{:S(2)}) copy-start(bf16[8,224,128]{2,1,0:T(8,128)(2,1)} %param.7) | copy-start | bytes 1376260
  2.0 24.5 %collective-permute-start = (f32[4,224,128]{2,1,0:T(8,128)S(1)}, f32[4,224,128]{2,1,0:T(8,128)S(1)}, u32[]{:S(2)}, u32[]{:S(2)}) collective-permute-start(f32[4,224,128]{2,1,0:T(8,128)S(1)} %get-tuple-element.22), channel_id=1, source_target_pairs={{0,8},{8,16},{16,24},{24,32},{32,40},{40,48},{48,56},{56,64},{64,7... | collective-permute-start | bytes 1376264 | tf_op jit(solution)/shard_map/ppermute | solution.py:18
  4.1 22.5 %collective-permute-start.1 = (f32[4,224,128]{2,1,0:T(8,128)S(1)}, f32[4,224,128]{2,1,0:T(8,128)S(1)}, u32[]{:S(2)}, u32[]{:S(2)}) collective-permute-start(f32[4,224,128]{2,1,0:T(8,128)S(1)} %get-tuple-element.21), channel_id=1, source_target_pairs={{0,504},{8,0},{16,8},{24,16},{32,24},{40,32},{48,40},{56,48},{64,5... | collective-permute-start | bytes 1376264 | tf_op jit(solution)/shard_map/ppermute | solution.py:18
  17.7 23.7 %collective-permute-start.3 = (bf16[14,224,128]{2,1,0:T(8,128)(2,1)S(1)}, bf16[14,224,128]{2,1,0:T(8,128)(2,1)S(1)}, u32[]{:S(2)}, u32[]{:S(2)}) collective-permute-start(bf16[14,224,128]{2,1,0:T(8,128)(2,1)S(1)} %get-tuple-element.27), channel_id=1, source_target_pairs={{0,504},{8,0},{16,8},{24,16},{32,24},{40,32},{48,40},{56,48},{64,5... | collective-permute-start | bytes 2408456 | tf_op jit(solution)/shard_map/ppermute | solution.py:18
  20.3 6.2 %copy-start.4 = (f32[8,224,128]{2,1,0:T(8,128)S(1)}, f32[8,224,128]{2,1,0:T(8,128)}, u32[]{:S(2)}) copy-start(f32[8,224,128]{2,1,0:T(8,128)} %param.4) | copy-start | bytes 2752516
  20.3 31.4 %collective-permute-start.2 = (bf16[18,224,128]{2,1,0:T(8,128)(2,1)S(1)}, bf16[18,224,128]{2,1,0:T(8,128)(2,1)S(1)}, u32[]{:S(2)}, u32[]{:S(2)}) collective-permute-start(bf16[18,224,128]{2,1,0:T(8,128)(2,1)S(1)} %get-tuple-element.26), channel_id=1, source_target_pairs={{0,8},{8,16},{16,24},{24,32},{32,40},{40,48},{48,56},{56,64},{64,7... | collective-permute-start | bytes 3096584 | tf_op jit(solution)/shard_map/ppermute | solution.py:18
  22.5 19.0 %copy-start.8 = (pred[4]{0:T(512)(128)(4,1)S(1)}, pred[4]{0:T(512)(128)(4,1)}, u32[]{:S(2)}) copy-start(pred[4]{0:T(512)(128)(4,1)} %constant.4.clone.1) | copy-start | bytes 16
  26.7 25.1 %copy-start.5 = (f32[16,224,128]{2,1,0:T(8,128)}, f32[16,224,128]{2,1,0:T(8,128)S(1)}, u32[]{:S(2)}) copy-start(f32[16,224,128]{2,1,0:T(8,128)S(1)} %constant_dynamic-update-slice_fusion) | copy-start | bytes 5505028
  51.8 1.5 %copy-start.2 = (bf16[16,224,128]{2,1,0:T(8,128)(2,1)}, bf16[16,224,128]{2,1,0:T(8,128)(2,1)S(1)}, u32[]{:S(2)}) copy-start(bf16[16,224,128]{2,1,0:T(8,128)(2,1)S(1)} %fusion.9) | copy-start | bytes 2752516
  51.9 1.5 %copy-start.1 = (bf16[16,224,128]{2,1,0:T(8,128)(2,1)}, bf16[16,224,128]{2,1,0:T(8,128)(2,1)S(1)}, u32[]{:S(2)}) copy-start(bf16[16,224,128]{2,1,0:T(8,128)(2,1)S(1)} %fusion.6) | copy-start | bytes 2752516
  52.1 1.1 %copy-start.3 = (bf16[16,224,128]{2,1,0:T(8,128)(2,1)}, bf16[16,224,128]{2,1,0:T(8,128)(2,1)S(1)}, u32[]{:S(2)}) copy-start(bf16[16,224,128]{2,1,0:T(8,128)(2,1)S(1)} %pad_maximum_fusion.1) | copy-start | bytes 2752516
  53.4 7.6 %collective-permute-start.4 = (f32[6,16,4,128]{3,2,1,0:T(4,128)S(1)}, f32[6,16,4,128]{3,2,1,0:T(4,128)S(1)}, u32[]{:S(2)}, u32[]{:S(2)}) collective-permute-start(f32[6,16,4,128]{3,2,1,0:T(4,128)S(1)} %get-tuple-element.12), channel_id=1, source_target_pairs={{0,1},{1,2},{2,3},{3,4},{4,5},{5,6},{6,7},{8,9},{9,10},{10,11},{11... | collective-permute-start | bytes 589832 | tf_op jit(solution)/shard_map/ppermute | solution.py:18
  56.1 9.7 %collective-permute-start.5 = (f32[6,16,4,128]{3,2,1,0:T(4,128)S(1)}, f32[6,16,4,128]{3,2,1,0:T(4,128)S(1)}, u32[]{:S(2)}, u32[]{:S(2)}) collective-permute-start(f32[6,16,4,128]{3,2,1,0:T(4,128)S(1)} %get-tuple-element.11), channel_id=1, source_target_pairs={{1,0},{2,1},{3,2},{4,3},{5,4},{6,5},{7,6},{9,8},{10,9},{11,10},{12... | collective-permute-start | bytes 589832 | tf_op jit(solution)/shard_map/ppermute | solution.py:18

commit v3 on v2

--- a/solution.py
+++ b/solution.py
@@ -1,3 +1,5 @@
+import functools
+
 import jax
 import jax.numpy as jnp
 from jax import lax
@@ -26,47 +28,80 @@
 
 def lon_halo(fields, west_rows, east_rows):
     size = fields[0].shape[0]
-    parts = {}
-    for key, rows, start in (("east", east_rows, lambda e: 0), ("west", west_rows, lambda w: size - w)):
+    got = {}
+    for key, rows, steps in (("east", east_rows, -1), ("west", west_rows, 1)):
+        start = (lambda r: 0) if key == "east" else (lambda r: size - r)
         pieces = [lax.slice_in_dim(f, start(r), start(r) + r, axis=0) for f, r in zip(fields, rows)]
-        wide = pieces[0]
-        narrow = jnp.concatenate(pieces[1:], 0)
-        parts[key] = passed_along((wide, narrow), "lon", -1 if key == "east" else 1, True)
-    out = []
-    for key in ("east", "west"):
-        wide, narrow = parts[key]
-        rows = east_rows if key == "east" else west_rows
-        got = [wide]
-        at = 0
-        for r in rows[1:]:
-            got.append(narrow[at:at + r])
-            at += r
-        parts[key] = got
-    for f, w, e, west, east in zip(fields, west_rows, east_rows, parts["west"], parts["east"]):
-        west = pad_rows(west, 0, HALO - w, 0)
-        east = pad_rows(east, 0, 0, HALO - e)
-        out.append(jnp.concatenate([west, f, east], 0))
+        got[key] = passed_along((pieces[0], jnp.concatenate(pieces[1:], 0)), "lon", steps, True)
+    return got
+
+
+def unpack(wide, narrow, rows):
+    out = [wide]
+    at = 0
+    for r in rows[1:]:
+        out.append(narrow[at:at + r])
+        at += r
     return out
 
 
-def lat_halo(fields):
+def lat_halo(fields, west, east, west_rows, east_rows):
+    def edge(part):
+        rows = []
+        for f, w, e, pw, pe in zip(fields, west_rows, east_rows, west, east):
+            piece = jnp.concatenate([pad_rows(part(pw), 0, HALO - w, 0), part(f), pad_rows(part(pe), 0, 0, HALO - e)], 0)
+            rows.append(piece.astype(jnp.float32))
+        return jnp.stack(rows)
+
     size = fields[0].shape[1]
-    lows = jnp.stack([f[:, :HALO].astype(jnp.float32) for f in fields])
-    highs = jnp.stack([f[:, size - HALO:].astype(jnp.float32) for f in fields])
-    from_north = passed_along(lows, "lat", -1, False)
-    from_south = passed_along(highs, "lat", 1, False)
-    out = []
-    for n, f in enumerate(fields):
-        gap = jnp.zeros(f.shape[:1] + (PAD - HALO,) + f.shape[2:], f.dtype)
-        out.append(jnp.concatenate([gap, from_south[n].astype(f.dtype), f, from_north[n].astype(f.dtype), gap], 1))
-    return out
-
-
-def stencil_kernel(conc_ref, wind_ref, kappa_ref, obs_ref, north_ref, gc_ref, gk_ref,
-                   own_ref, oth_ref, mid_ref, lam2_ref, lam1_ref):
-    rows, lats, levels = conc_ref.shape
+    lows = edge(lambda x: x[:, :HALO])
+    highs = edge(lambda x: x[:, size - HALO:])
+    return passed_along(highs, "lat", 1, False), passed_along(lows, "lat", -1, False)
+
+
+def stencil_kernel(west_rows, east_rows, conc_in, wind_in, kappa_in, obs_in, west_c, west_p, east_c, east_p,
+                   south_ref, north_halo, north_ref, gc_ref, gk_ref, raw_ref, own_ref, oth_ref, mid_ref, lam2_ref,
+                   lam1_ref):
+    fields, rows, lats, levels = raw_ref.shape
+    block = conc_in.shape[0]
     f32 = jnp.float32
     north_open = north_ref[...]
+    lo = PAD
+    hi = lats - PAD
+    gap = jnp.zeros((PAD - HALO, levels), f32)
+
+    def put(f, r, core):
+        raw_ref[f, r, lo:hi] = core
+        raw_ref[f, r, lo - HALO:lo] = south_ref[f, r]
+        raw_ref[f, r, hi:hi + HALO] = north_halo[f, r]
+        raw_ref[f, r, :lo - HALO] = gap
+        raw_ref[f, r, hi + HALO:] = gap
+
+    def own_row(i, carry):
+        put(0, i + HALO, conc_in[i])
+        for d in range(3):
+            put(1 + d, i + HALO, wind_in[d, i].astype(f32))
+        put(4, i + HALO, kappa_in[i].astype(f32))
+        put(5, i + HALO, obs_in[i].astype(f32))
+        return carry
+
+    lax.fori_loop(0, block, own_row, 0)
+    empty = jnp.zeros((hi - lo, levels), f32)
+    for r in range(HALO):
+        put(0, r, west_c[r])
+        put(0, HALO + block + r, east_c[r])
+    at_w = 0
+    at_e = 0
+    for f in range(1, fields):
+        w = west_rows[f]
+        e = east_rows[f]
+        for r in range(HALO):
+            put(f, r, west_p[at_w + r - (HALO - w)].astype(f32) if r >= HALO - w else empty)
+            put(f, HALO + block + r, east_p[at_e + r].astype(f32) if r < e else empty)
+        at_w += w
+        at_e += e
+    conc_ref = raw_ref.at[0]
+    obs_ref = raw_ref.at[5]
     upper_open = (lax.broadcasted_iota(jnp.int32, (lats, levels), 1) < levels - 1).astype(f32)
 
     def next_lat(f):
@@ -82,9 +117,9 @@
         return pltpu.roll(f, 1, 1)
 
     def coef_row(i, carry):
-        diffuse = kappa_ref[i].astype(f32)
+        diffuse = raw_ref[4, i]
         for d, opened in ((0, None), (1, north_open), (2, upper_open)):
-            speed = wind_ref[d, i].astype(f32)
+            speed = raw_ref[1 + d, i]
             own = jnp.maximum(speed, 0.0) + diffuse
             oth = jnp.minimum(speed, 0.0) - diffuse
             if opened is not None:
@@ -107,7 +142,7 @@
             f2 = own_ref[2, i] * c + oth_ref[2, i] * next_lev(c)
             out = c - (f0 + f1 + f2) + (west0 + back_lat(f1) + back_lev(f2))
             if minus is not None:
-                out = out - minus[i].astype(f32)
+                out = out - minus[i]
             dst[i] = out
             return f0
 
@@ -162,20 +197,21 @@
     lon_rows, lat_rows, levels = concentration.shape
     lat_total = lat_rows * lax.axis_size("lat")
     fields = [concentration, wind[0], wind[1], wind[2], kappa, observed]
-    west_rows = [4, 4, 4, 4, 4, 2]
-    east_rows = [4, 3, 3, 3, 3, 2]
-    fields = lon_halo(fields, west_rows, east_rows)
-    fields = lat_halo(fields)
-    conc, a0, a1, a2, kap, obs = fields
-    ext_rows, ext_lats = conc.shape[0], conc.shape[1]
+    west_rows = (4, 4, 3, 3, 4, 2)
+    east_rows = (4, 3, 3, 3, 3, 2)
+    got = lon_halo(fields, west_rows, east_rows)
+    west = unpack(*got["west"], west_rows)
+    east = unpack(*got["east"], east_rows)
+    south, north = lat_halo(fields, west, east, west_rows, east_rows)
+    ext_rows = lon_rows + 2 * HALO
+    ext_lats = lat_rows + 2 * PAD
     lat_place = lax.axis_index("lat") * lat_rows - PAD + lax.broadcasted_iota(jnp.int32, (ext_lats, levels), 0)
     north_open = ((lat_place >= 0) & (lat_place < lat_total - 1)).astype(jnp.float32)
-    winds = jnp.stack([a0, a1, a2])
-    whole = [conc, winds, kap, obs, north_open]
+    whole = [concentration, wind, kappa, observed, *got["west"], *got["east"], south, north, north_open]
     vmem = pltpu.MemorySpace.VMEM
     state = pltpu.VMEM((ext_rows, ext_lats, levels), jnp.float32)
     return pl.pallas_call(
-        stencil_kernel,
+        functools.partial(stencil_kernel, west_rows, east_rows),
         out_shape=(
             jax.ShapeDtypeStruct((lon_rows, lat_rows, levels), jnp.float32),
             jax.ShapeDtypeStruct((lon_rows, lat_rows, levels), jnp.float32),
@@ -183,13 +219,14 @@
         in_specs=[pl.BlockSpec(memory_space=vmem) for _ in whole],
         out_specs=(pl.BlockSpec(memory_space=vmem), pl.BlockSpec(memory_space=vmem)),
         scratch_shapes=[
+            pltpu.VMEM((len(fields), ext_rows, ext_lats, levels), jnp.float32),
             pltpu.VMEM((3, ext_rows, ext_lats, levels), jnp.float32),
             pltpu.VMEM((3, ext_rows, ext_lats, levels), jnp.float32),
             state,
             state,
             state,
         ],
-        compiler_params=pltpu.CompilerParams(vmem_limit_bytes=56 * 1024 * 1024),
+        compiler_params=pltpu.CompilerParams(vmem_limit_bytes=60 * 1024 * 1024),
     )(*whole)
 
 

time: 108 us -> 89.2 us (0.83)
  the two profiles are of different devices: /device:TPU:6 before, /device:TPU:64 now
where the time goes in v3:
time: 89.2 us; the launch traced here: 88.9 us
  waiting for transfers between devices  41.1 us (46%)
  starting transfers between devices  26.3 us (29%)
  Pallas kernels  14.9 us (17%)
  local copies, waits for them, and re-layouts  5.35 us (6%)
  between operations  1.05 us (1%)
    ppermute x6, waiting for transfers between devices, passed_along(): return lax.ppermute(value, axis, pairs)  41.1 us
    ppermute x6, starting transfers between devices, passed_along(): return lax.ppermute(value, axis, pairs)  26.3 us
    pallas_call x1, Pallas kernels, body(): pl.pallas_call(functools.partial(stencil_kernel, west_rows, east_rows), o...  14.9 us
    unnamed x26, local copies, waits for them, and re-layouts  4.24 us
  transfers between devices with their start and end apart: 6, of which 4 were waited for; matrix products, arithmetic and copies ran while one was open for 0% of the time, Pallas kernels for 0%

profile of v3, /device:TPU:64, one launch (start us, length us, event | category | flops | bytes accessed | tf_op | source)
XLA Modules:
  0.0 88.9 jit_solution(7941322006075297282)
XLA Ops:
  0.6 0.0 copy-start
  0.6 0.0 copy-start.2
  0.7 1.1 %bitcast_dynamic-update-slice_fusion.3 = bf16[14,224,128]{2,1,0:T(8,128)(2,1)S(1)} fusion(bf16[3,8,224,128]{3,2,1,0:T(8,128)(2,1)} %wind_in.1), kind=kLoop, calls=%fused_computation.7 | loop fusion | bytes 344064
  1.7 0.0 copy-start.3
  1.7 1.0 %bitcast_dynamic-update-slice_fusion = bf16[16,224,128]{2,1,0:T(8,128)(2,1)S(1)} fusion(bf16[3,8,224,128]{3,2,1,0:T(8,128)(2,1)} %wind_in.1), kind=kLoop, calls=%fused_computation.3 | loop fusion | bytes 458752
  2.7 0.0 copy-start.1
  2.8 1.1 %bitcast_dynamic-update-slice_fusion.2 = (bf16[14,224,128]{2,1,0:T(8,128)(2,1)S(1)}, bf16[16,224,128]{2,1,0:T(8,128)(2,1)S(1)}) fusion(bf16[14,224,128]{2,1,0:T(8,128)(2,1)S(1)} %bitcast_dynamic-update-slice_fusion.3, bf16[3,8,224,128]{3,2,1,0:T(8,128)(2,1)} %wind_in.1, bf16[16,224,128]{2,1,0:T(8,128)(2,1)S(1)} %bitcast_dynamic-update-slice_fusion), kind=kLoop, calls=%fused_computation.6 | loop fusion | bytes 688128
  3.9 0.0 copy-done
  4.0 0.0 copy-done.2
  4.0 0.0 copy-done.3
  4.1 12.4 %collective-permute-start.3 = (bf16[14,224,128]{2,1,0:T(8,128)(2,1)S(1)}, bf16[14,224,128]{2,1,0:T(8,128)(2,1)S(1)}, u32[]{:S(2)}, u32[]{:S(2)}) collective-permute-start(bf16[14,224,128]{2,1,0:T(8,128)(2,1)S(1)} %get-tuple-element.47), channel_id=1, source_target_pairs={{0,504},{8,0},{16,8},{24,16},{32,24},{40,32},{48,40},{56,48},{64,5... | collective-permute-start | bytes 2408456 | tf_op jit(solution)/shard_map/ppermute | solution.py:20
  16.5 0.0 copy-done.1
  16.5 0.1 fusion.3
  16.6 2.6 %collective-permute-start.2 = (f32[4,224,128]{2,1,0:T(8,128)S(1)}, f32[4,224,128]{2,1,0:T(8,128)S(1)}, u32[]{:S(2)}, u32[]{:S(2)}) collective-permute-start(f32[4,224,128]{2,1,0:T(8,128)S(1)} %get-tuple-element.21), channel_id=1, source_target_pairs={{0,504},{8,0},{16,8},{24,16},{32,24},{40,32},{48,40},{56,48},{64,5... | collective-permute-start | bytes 1376264 | tf_op jit(solution)/shard_map/ppermute | solution.py:20
  19.1 1.9 %collective-permute-start = (f32[4,224,128]{2,1,0:T(8,128)S(1)}, f32[4,224,128]{2,1,0:T(8,128)S(1)}, u32[]{:S(2)}, u32[]{:S(2)}) collective-permute-start(f32[4,224,128]{2,1,0:T(8,128)S(1)} %get-tuple-element.22), channel_id=1, source_target_pairs={{0,8},{8,16},{16,24},{24,32},{32,40},{40,48},{48,56},{56,64},{64,7... | collective-permute-start | bytes 1376264 | tf_op jit(solution)/shard_map/ppermute | solution.py:20
  21.1 1.9 %collective-permute-start.1 = (bf16[16,224,128]{2,1,0:T(8,128)(2,1)S(1)}, bf16[16,224,128]{2,1,0:T(8,128)(2,1)S(1)}, u32[]{:S(2)}, u32[]{:S(2)}) collective-permute-start(bf16[16,224,128]{2,1,0:T(8,128)(2,1)S(1)} %get-tuple-element.48), channel_id=1, source_target_pairs={{0,8},{8,16},{16,24},{24,32},{32,40},{40,48},{48,56},{56,64},{64,7... | collective-permute-start | bytes 2752520 | tf_op jit(solution)/shard_map/ppermute | solution.py:20
  23.0 0.1 slice_bitcast_fusion
  23.2 19.0 %collective-permute-done.2.east_c = f32[4,224,128]{2,1,0:T(8,128)S(1)} collective-permute-done((f32[4,224,128]{2,1,0:T(8,128)S(1)}, f32[4,224,128]{2,1,0:T(8,128)S(1)}, u32[]{:S(2)}, u32[]{:S(2)}) %collective-permute-start.2) | collective-permute-done | bytes 458784 | tf_op jit(solution)/shard_map/ppermute | solution.py:20
  42.2 0.0 copy-start.6
  42.2 0.0 collective-permute-done.west_c
  42.2 0.0 copy-start.7
  42.2 0.0 collective-permute-done.3.east_p
  42.2 0.0 copy-start.5
  42.4 14.4 %collective-permute-done.1.west_p = bf16[16,224,128]{2,1,0:T(8,128)(2,1)S(1)} collective-permute-done((bf16[16,224,128]{2,1,0:T(8,128)(2,1)S(1)}, bf16[16,224,128]{2,1,0:T(8,128)(2,1)S(1)}, u32[]{:S(2)}, u32[]{:S(2)}) %collective-permute-start.1) | collective-permute-done | bytes 917536 | tf_op jit(solution)/shard_map/ppermute | solution.py:20
  56.8 0.0 copy-start.4
  56.8 0.9 copy-done.4
  57.7 0.0 copy-done.5
  57.7 0.0 copy-done.6
  57.8 0.0 copy-done.7
  57.9 5.6 %collective-permute-start.5 = (f32[6,16,4,128]{3,2,1,0:T(4,128)S(1)}, f32[6,16,4,128]{3,2,1,0:T(4,128)S(1)}, u32[]{:S(2)}, u32[]{:S(2)}) collective-permute-start(f32[6,16,4,128]{3,2,1,0:T(4,128)S(1)} %constant_dynamic-update-slice_fusion.6), channel_id=1, source_target_pairs={{1,0},{2,1},{3,2},{4,3},{5,4},{6,5},{7,6},{9,8},{10,9},{11,10},{12... | collective-permute-start | bytes 589832 | tf_op jit(solution)/shard_map/ppermute | solution.py:20
  63.6 1.9 %collective-permute-start.4 = (f32[6,16,4,128]{3,2,1,0:T(4,128)S(1)}, f32[6,16,4,128]{3,2,1,0:T(4,128)S(1)}, u32[]{:S(2)}, u32[]{:S(2)}) collective-permute-start(f32[6,16,4,128]{3,2,1,0:T(4,128)S(1)} %constant_dynamic-update-slice_fusion), channel_id=1, source_target_pairs={{0,1},{1,2},{2,3},{3,4},{4,5},{5,6},{6,7},{8,9},{9,10},{10,11},{11... | collective-permute-start | bytes 589832 | tf_op jit(solution)/shard_map/ppermute | solution.py:20
  65.6 1.1 %collective-permute-done.5.north_halo = f32[6,16,4,128]{3,2,1,0:T(4,128)S(1)} collective-permute-done((f32[6,16,4,128]{3,2,1,0:T(4,128)S(1)}, f32[6,16,4,128]{3,2,1,0:T(4,128)S(1)}, u32[]{:S(2)}, u32[]{:S(2)}) %collective-permute-start.5) | collective-permute-done | bytes 196640 | tf_op jit(solution)/shard_map/ppermute | solution.py:20
  66.7 0.0 copy-start.8
  66.7 6.6 %collective-permute-done.4.south_ref = f32[6,16,4,128]{3,2,1,0:T(4,128)S(1)} collective-permute-done((f32[6,16,4,128]{3,2,1,0:T(4,128)S(1)}, f32[6,16,4,128]{3,2,1,0:T(4,128)S(1)}, u32[]{:S(2)}, u32[]{:S(2)}) %collective-permute-start.4) | collective-permute-done | bytes 196640 | tf_op jit(solution)/shard_map/ppermute | solution.py:20
  73.3 0.0 copy-start.9
  73.3 0.8 iota.7.north_ref
  74.1 0.0 copy-done.8
  74.1 0.0 copy-done.9
  74.1 14.9 %shard_map.59 = (f32[8,224,128]{2,1,0:T(8,128)}, f32[8,224,128]{2,1,0:T(8,128)}) custom-call(f32[8,224,128]{2,1,0:T(8,128)} %conc_in.1, bf16[3,8,224,128]{3,2,1,0:T(8,128)(2,1)} %wind_in.1, bf16[8,224,128]{2,1,0:T(8,128)(2,1)} %kappa_in.1, bf16[8,224,128]{2,1,0:T(8,128)(2,1)} %obs_in.1, f32[4,224,128]{2,1,0:T(8,128)} %copy-done.7, ...), custom_call_target="tpu_custom_call" | custom-call | tf_op jit(solution)/shard_map/pallas_call | solution.py:213
  (36 shorter events, 0.5 us)
Async XLA Ops:
  0.6 3.3 %copy-start = (bf16[3,8,224,128]{3,2,1,0:T(8,128)(2,1)S(1)}, bf16[3,8,224,128]{3,2,1,0:T(8,128)(2,1)}, u32[]{:S(2)}) copy-start(bf16[3,8,224,128]{3,2,1,0:T(8,128)(2,1)} %wind_in.1) | copy-start | bytes 4128772
  0.6 3.3 %copy-start.2 = (bf16[8,224,128]{2,1,0:T(8,128)(2,1)S(1)}, bf16[8,224,128]{2,1,0:T(8,128)(2,1)}, u32[]{:S(2)}) copy-start(bf16[8,224,128]{2,1,0:T(8,128)(2,1)} %kappa_in.1) | copy-start | bytes 1376260
  1.7 2.3 %copy-start.3 = (bf16[8,224,128]{2,1,0:T(8,128)(2,1)S(1)}, bf16[8,224,128]{2,1,0:T(8,128)(2,1)}, u32[]{:S(2)}) copy-start(bf16[8,224,128]{2,1,0:T(8,128)(2,1)} %obs_in.1) | copy-start | bytes 1376260
  2.7 13.7 %copy-start.1 = (f32[8,224,128]{2,1,0:T(8,128)S(1)}, f32[8,224,128]{2,1,0:T(8,128)}, u32[]{:S(2)}) copy-start(f32[8,224,128]{2,1,0:T(8,128)} %conc_in.1) | copy-start | bytes 2752516
  4.1 38.2 %collective-permute-start.3 = (bf16[14,224,128]{2,1,0:T(8,128)(2,1)S(1)}, bf16[14,224,128]{2,1,0:T(8,128)(2,1)S(1)}, u32[]{:S(2)}, u32[]{:S(2)}) collective-permute-start(bf16[14,224,128]{2,1,0:T(8,128)(2,1)S(1)} %get-tuple-element.47), channel_id=1, source_target_pairs={{0,504},{8,0},{16,8},{24,16},{32,24},{40,32},{48,40},{56,48},{64,5... | collective-permute-start | bytes 2408456 | tf_op jit(solution)/shard_map/ppermute | solution.py:20
  16.6 25.6 %collective-permute-start.2 = (f32[4,224,128]{2,1,0:T(8,128)S(1)}, f32[4,224,128]{2,1,0:T(8,128)S(1)}, u32[]{:S(2)}, u32[]{:S(2)}) collective-permute-start(f32[4,224,128]{2,1,0:T(8,128)S(1)} %get-tuple-element.21), channel_id=1, source_target_pairs={{0,504},{8,0},{16,8},{24,16},{32,24},{40,32},{48,40},{56,48},{64,5... | collective-permute-start | bytes 1376264 | tf_op jit(solution)/shard_map/ppermute | solution.py:20
  19.1 23.0 %collective-permute-start = (f32[4,224,128]{2,1,0:T(8,128)S(1)}, f32[4,224,128]{2,1,0:T(8,128)S(1)}, u32[]{:S(2)}, u32[]{:S(2)}) collective-permute-start(f32[4,224,128]{2,1,0:T(8,128)S(1)} %get-tuple-element.22), channel_id=1, source_target_pairs={{0,8},{8,16},{16,24},{24,32},{32,40},{40,48},{48,56},{56,64},{64,7... | collective-permute-start | bytes 1376264 | tf_op jit(solution)/shard_map/ppermute | solution.py:20
  21.1 35.7 %collective-permute-start.1 = (bf16[16,224,128]{2,1,0:T(8,128)(2,1)S(1)}, bf16[16,224,128]{2,1,0:T(8,128)(2,1)S(1)}, u32[]{:S(2)}, u32[]{:S(2)}) collective-permute-start(bf16[16,224,128]{2,1,0:T(8,128)(2,1)S(1)} %get-tuple-element.48), channel_id=1, source_target_pairs={{0,8},{8,16},{16,24},{24,32},{32,40},{40,48},{48,56},{56,64},{64,7... | collective-permute-start | bytes 2752520 | tf_op jit(solution)/shard_map/ppermute | solution.py:20
  42.2 15.6 %copy-start.6 = (f32[4,224,128]{2,1,0:T(8,128)}, f32[4,224,128]{2,1,0:T(8,128)S(1)}, u32[]{:S(2)}) copy-start(f32[4,224,128]{2,1,0:T(8,128)S(1)} %collective-permute-done.2.east_c) | copy-start | bytes 1376260
  42.2 15.6 %copy-start.7 = (f32[4,224,128]{2,1,0:T(8,128)}, f32[4,224,128]{2,1,0:T(8,128)S(1)}, u32[]{:S(2)}) copy-start(f32[4,224,128]{2,1,0:T(8,128)S(1)} %collective-permute-done.west_c) | copy-start | bytes 1376260
  42.2 15.5 %copy-start.5 = (bf16[14,224,128]{2,1,0:T(8,128)(2,1)}, bf16[14,224,128]{2,1,0:T(8,128)(2,1)S(1)}, u32[]{:S(2)}) copy-start(bf16[14,224,128]{2,1,0:T(8,128)(2,1)S(1)} %collective-permute-done.3.east_p) | copy-start | bytes 2408452
  56.8 0.9 %copy-start.4 = (bf16[16,224,128]{2,1,0:T(8,128)(2,1)}, bf16[16,224,128]{2,1,0:T(8,128)(2,1)S(1)}, u32[]{:S(2)}) copy-start(bf16[16,224,128]{2,1,0:T(8,128)(2,1)S(1)} %collective-permute-done.1.west_p) | copy-start | bytes 2752516
  57.9 8.8 %collective-permute-start.5 = (f32[6,16,4,128]{3,2,1,0:T(4,128)S(1)}, f32[6,16,4,128]{3,2,1,0:T(4,128)S(1)}, u32[]{:S(2)}, u32[]{:S(2)}) collective-permute-start(f32[6,16,4,128]{3,2,1,0:T(4,128)S(1)} %constant_dynamic-update-slice_fusion.6), channel_id=1, source_target_pairs={{1,0},{2,1},{3,2},{4,3},{5,4},{6,5},{7,6},{9,8},{10,9},{11,10},{12... | collective-permute-start | bytes 589832 | tf_op jit(solution)/shard_map/ppermute | solution.py:20
  63.6 9.7 %collective-permute-start.4 = (f32[6,16,4,128]{3,2,1,0:T(4,128)S(1)}, f32[6,16,4,128]{3,2,1,0:T(4,128)S(1)}, u32[]{:S(2)}, u32[]{:S(2)}) collective-permute-start(f32[6,16,4,128]{3,2,1,0:T(4,128)S(1)} %constant_dynamic-update-slice_fusion), channel_id=1, source_target_pairs={{0,1},{1,2},{2,3},{3,4},{4,5},{5,6},{6,7},{8,9},{9,10},{10,11},{11... | collective-permute-start | bytes 589832 | tf_op jit(solution)/shard_map/ppermute | solution.py:20
  66.7 7.4 %copy-start.8 = (f32[6,16,4,128]{3,2,1,0:T(4,128)}, f32[6,16,4,128]{3,2,1,0:T(4,128)S(1)}, u32[]{:S(2)}) copy-start(f32[6,16,4,128]{3,2,1,0:T(4,128)S(1)} %collective-permute-done.5.north_halo) | copy-start | bytes 589828
  73.3 0.8 copy-start.9

commit v4 on v3

--- a/solution.py
+++ b/solution.py
@@ -32,15 +32,17 @@
     for key, rows, steps in (("east", east_rows, -1), ("west", west_rows, 1)):
         start = (lambda r: 0) if key == "east" else (lambda r: size - r)
         pieces = [lax.slice_in_dim(f, start(r), start(r) + r, axis=0) for f, r in zip(fields, rows)]
-        got[key] = passed_along((pieces[0], jnp.concatenate(pieces[1:], 0)), "lon", steps, True)
+        high = pieces[0].astype(jnp.bfloat16)
+        low = (pieces[0] - high.astype(jnp.float32)).astype(jnp.bfloat16)
+        got[key] = passed_along(jnp.concatenate([high, low] + pieces[1:], 0), "lon", steps, True)
     return got
 
 
-def unpack(wide, narrow, rows):
-    out = [wide]
-    at = 0
+def unpack(pack, rows):
+    out = [pack[:rows[0]].astype(jnp.float32) + pack[rows[0]:2 * rows[0]].astype(jnp.float32)]
+    at = 2 * rows[0]
     for r in rows[1:]:
-        out.append(narrow[at:at + r])
+        out.append(pack[at:at + r])
         at += r
     return out
 
@@ -59,7 +61,7 @@
     return passed_along(highs, "lat", 1, False), passed_along(lows, "lat", -1, False)
 
 
-def stencil_kernel(west_rows, east_rows, conc_in, wind_in, kappa_in, obs_in, west_c, west_p, east_c, east_p,
+def stencil_kernel(west_rows, east_rows, conc_in, wind_in, kappa_in, obs_in, west_p, east_p,
                    south_ref, north_halo, north_ref, gc_ref, gk_ref, raw_ref, own_ref, oth_ref, mid_ref, lam2_ref,
                    lam1_ref):
     fields, rows, lats, levels = raw_ref.shape
@@ -88,10 +90,10 @@
     lax.fori_loop(0, block, own_row, 0)
     empty = jnp.zeros((hi - lo, levels), f32)
     for r in range(HALO):
-        put(0, r, west_c[r])
-        put(0, HALO + block + r, east_c[r])
-    at_w = 0
-    at_e = 0
+        put(0, r, west_p[r].astype(f32) + west_p[HALO + r].astype(f32))
+        put(0, HALO + block + r, east_p[r].astype(f32) + east_p[HALO + r].astype(f32))
+    at_w = 2 * HALO
+    at_e = 2 * HALO
     for f in range(1, fields):
         w = west_rows[f]
         e = east_rows[f]
@@ -200,14 +202,14 @@
     west_rows = (4, 4, 3, 3, 4, 2)
     east_rows = (4, 3, 3, 3, 3, 2)
     got = lon_halo(fields, west_rows, east_rows)
-    west = unpack(*got["west"], west_rows)
-    east = unpack(*got["east"], east_rows)
+    west = unpack(got["west"], west_rows)
+    east = unpack(got["east"], east_rows)
     south, north = lat_halo(fields, west, east, west_rows, east_rows)
     ext_rows = lon_rows + 2 * HALO
     ext_lats = lat_rows + 2 * PAD
     lat_place = lax.axis_index("lat") * lat_rows - PAD + lax.broadcasted_iota(jnp.int32, (ext_lats, levels), 0)
     north_open = ((lat_place >= 0) & (lat_place < lat_total - 1)).astype(jnp.float32)
-    whole = [concentration, wind, kappa, observed, *got["west"], *got["east"], south, north, north_open]
+    whole = [concentration, wind, kappa, observed, got["west"], got["east"], south, north, north_open]
     vmem = pltpu.MemorySpace.VMEM
     state = pltpu.VMEM((ext_rows, ext_lats, levels), jnp.float32)
     return pl.pallas_call(

time: 89.2 us -> 78.3 us (0.88)
  waiting for transfers between devices: 41.1 us -> 35.6 us
  starting transfers between devices: 26.3 us -> 21.4 us
    ppermute x6 -> x4, waiting for transfers between devices: 41.1 us -> 35.6 us  [passed_along(): return lax.ppermute(value, axis, pairs)]
    ppermute x6 -> x4, starting transfers between devices: 26.3 us -> 21.4 us  [passed_along(): return lax.ppermute(value, axis, pairs)]
    unnamed x26 -> x23, local copies, waits for them, and re-layouts: 4.24 us -> 3.79 us
  transfers between devices with their start and end apart: 6 -> 4, of which waited for: 4 -> 4; matrix products, arithmetic and copies ran while one was open for 0% -> 0% of each run, Pallas kernels for 0% -> 0%
where the time goes in v4:
time: 78.3 us; the launch traced here: 78.1 us
  waiting for transfers between devices  35.6 us (45%)
  starting transfers between devices  21.4 us (27%)
  Pallas kernels  14.9 us (19%)
  local copies, waits for them, and re-layouts  4.82 us (6%)
  between operations  0.99 us (1%)
    ppermute x4, waiting for transfers between devices, passed_along(): return lax.ppermute(value, axis, pairs)  35.6 us
    ppermute x4, starting transfers between devices, passed_along(): return lax.ppermute(value, axis, pairs)  21.4 us
    pallas_call x1, Pallas kernels, body(): pl.pallas_call(functools.partial(stencil_kernel, west_rows, east_rows), o...  14.9 us
    unnamed x23, local copies, waits for them, and re-layouts  3.79 us
  transfers between devices with their start and end apart: 4, of which 4 were waited for; matrix products, arithmetic and copies ran while one was open for 0% of the time, Pallas kernels for 0%

profile of v4, /device:TPU:64, one launch (start us, length us, event | category | flops | bytes accessed | tf_op | source)
XLA Modules:
  0.0 78.1 jit_solution(7860872407452768960)
XLA Ops:
  0.6 0.0 copy-start.1
  0.6 0.0 copy-start
  0.7 1.4 %fusion.3 = (bf16[22,224,128]{2,1,0:T(8,128)(2,1)S(1)}, bf16[24,224,128]{2,1,0:T(8,128)(2,1)S(1)}) fusion(f32[8,224,128]{2,1,0:T(8,128)} %conc_in.1), kind=kLoop, calls=%fused_computation.22 | loop fusion | bytes 917504
  2.0 0.1 copy-done.1
  2.1 0.1 fusion.1
  2.2 0.0 copy-start.4
  2.2 0.3 copy-done
  2.6 0.0 copy-start.5
  2.7 0.6 copy-done.4
  3.4 0.3 copy-done.5
  3.7 1.9 %collective-permute-start = (bf16[24,224,128]{2,1,0:T(8,128)(2,1)S(1)}, bf16[24,224,128]{2,1,0:T(8,128)(2,1)S(1)}, u32[]{:S(2)}, u32[]{:S(2)}) collective-permute-start(bf16[24,224,128]{2,1,0:T(8,128)(2,1)S(1)} %get-tuple-element.50), channel_id=1, source_target_pairs={{0,8},{8,16},{16,24},{24,32},{32,40},{40,48},{48,56},{56,64},{64,7... | collective-permute-start | bytes 4128776 | tf_op jit(solution)/shard_map/ppermute | solution.py:20
  5.6 12.4 %collective-permute-start.1 = (bf16[22,224,128]{2,1,0:T(8,128)(2,1)S(1)}, bf16[22,224,128]{2,1,0:T(8,128)(2,1)S(1)}, u32[]{:S(2)}, u32[]{:S(2)}) collective-permute-start(bf16[22,224,128]{2,1,0:T(8,128)(2,1)S(1)} %get-tuple-element.49), channel_id=1, source_target_pairs={{0,504},{8,0},{16,8},{24,16},{32,24},{40,32},{48,40},{56,48},{64,5... | collective-permute-start | bytes 3784712 | tf_op jit(solution)/shard_map/ppermute | solution.py:20
  18.0 0.1 slice_bitcast_fusion
  18.2 25.6 %collective-permute-done.1.east_p = bf16[22,224,128]{2,1,0:T(8,128)(2,1)S(1)} collective-permute-done((bf16[22,224,128]{2,1,0:T(8,128)(2,1)S(1)}, bf16[22,224,128]{2,1,0:T(8,128)(2,1)S(1)}, u32[]{:S(2)}, u32[]{:S(2)}) %collective-permute-start.1) | collective-permute-done | bytes 1261600 | tf_op jit(solution)/shard_map/ppermute | solution.py:20
  43.8 0.0 copy-start.3
  43.9 2.3 %collective-permute-done.west_p = bf16[24,224,128]{2,1,0:T(8,128)(2,1)S(1)} collective-permute-done((bf16[24,224,128]{2,1,0:T(8,128)(2,1)S(1)}, bf16[24,224,128]{2,1,0:T(8,128)(2,1)S(1)}, u32[]{:S(2)}, u32[]{:S(2)}) %collective-permute-start) | collective-permute-done | bytes 1376288 | tf_op jit(solution)/shard_map/ppermute | solution.py:20
  46.2 0.0 copy-start.2
  46.4 1.0 %copy-done.2 = bf16[24,224,128]{2,1,0:T(8,128)(2,1)} copy-done((bf16[24,224,128]{2,1,0:T(8,128)(2,1)}, bf16[24,224,128]{2,1,0:T(8,128)(2,1)S(1)}, u32[]{:S(2)}) %copy-start.2) | copy-done | bytes 1376280
  47.5 5.2 %collective-permute-start.3 = (f32[6,16,4,128]{3,2,1,0:T(4,128)S(1)}, f32[6,16,4,128]{3,2,1,0:T(4,128)S(1)}, u32[]{:S(2)}, u32[]{:S(2)}) collective-permute-start(f32[6,16,4,128]{3,2,1,0:T(4,128)S(1)} %constant_dynamic-update-slice_fusion.6), channel_id=1, source_target_pairs={{1,0},{2,1},{3,2},{4,3},{5,4},{6,5},{7,6},{9,8},{10,9},{11,10},{12... | collective-permute-start | bytes 589832 | tf_op jit(solution)/shard_map/ppermute | solution.py:20
  52.8 0.0 copy-done.3
  52.8 1.9 %collective-permute-start.2 = (f32[6,16,4,128]{3,2,1,0:T(4,128)S(1)}, f32[6,16,4,128]{3,2,1,0:T(4,128)S(1)}, u32[]{:S(2)}, u32[]{:S(2)}) collective-permute-start(f32[6,16,4,128]{3,2,1,0:T(4,128)S(1)} %constant_dynamic-update-slice_fusion), channel_id=1, source_target_pairs={{0,1},{1,2},{2,3},{3,4},{4,5},{5,6},{6,7},{8,9},{9,10},{10,11},{11... | collective-permute-start | bytes 589832 | tf_op jit(solution)/shard_map/ppermute | solution.py:20
  54.8 1.1 %collective-permute-done.3.north_halo = f32[6,16,4,128]{3,2,1,0:T(4,128)S(1)} collective-permute-done((f32[6,16,4,128]{3,2,1,0:T(4,128)S(1)}, f32[6,16,4,128]{3,2,1,0:T(4,128)S(1)}, u32[]{:S(2)}, u32[]{:S(2)}) %collective-permute-start.3) | collective-permute-done | bytes 196640 | tf_op jit(solution)/shard_map/ppermute | solution.py:20
  55.9 0.0 copy-start.6
  55.9 6.7 %collective-permute-done.2.south_ref = f32[6,16,4,128]{3,2,1,0:T(4,128)S(1)} collective-permute-done((f32[6,16,4,128]{3,2,1,0:T(4,128)S(1)}, f32[6,16,4,128]{3,2,1,0:T(4,128)S(1)}, u32[]{:S(2)}, u32[]{:S(2)}) %collective-permute-start.2) | collective-permute-done | bytes 196640 | tf_op jit(solution)/shard_map/ppermute | solution.py:20
  62.5 0.0 copy-start.7
  62.5 0.7 iota.7.north_ref
  63.2 0.0 copy-done.6
  63.2 0.0 copy-done.7
  63.3 14.9 %shard_map.59 = (f32[8,224,128]{2,1,0:T(8,128)}, f32[8,224,128]{2,1,0:T(8,128)}) custom-call(f32[8,224,128]{2,1,0:T(8,128)} %conc_in.1, bf16[3,8,224,128]{3,2,1,0:T(8,128)(2,1)} %wind_in.1, bf16[8,224,128]{2,1,0:T(8,128)(2,1)} %kappa_in.1, bf16[8,224,128]{2,1,0:T(8,128)(2,1)} %obs_in.1, bf16[24,224,128]{2,1,0:T(8,128)(2,1)} %copy-done.2, ...), custom_call_target="tpu_custom_call" | custom-call | tf_op jit(solution)/shard_map/pallas_call | solution.py:215
  (41 shorter events, 0.7 us)
Async XLA Ops:
  0.6 1.5 %copy-start.1 = (f32[8,224,128]{2,1,0:T(8,128)S(1)}, f32[8,224,128]{2,1,0:T(8,128)}, u32[]{:S(2)}) copy-start(f32[8,224,128]{2,1,0:T(8,128)} %conc_in.1) | copy-start | bytes 2752516
  0.6 1.9 %copy-start = (bf16[3,8,224,128]{3,2,1,0:T(8,128)(2,1)S(1)}, bf16[3,8,224,128]{3,2,1,0:T(8,128)(2,1)}, u32[]{:S(2)}) copy-start(bf16[3,8,224,128]{3,2,1,0:T(8,128)(2,1)} %wind_in.1) | copy-start | bytes 4128772
  2.2 1.1 %copy-start.4 = (bf16[8,224,128]{2,1,0:T(8,128)(2,1)S(1)}, bf16[8,224,128]{2,1,0:T(8,128)(2,1)}, u32[]{:S(2)}) copy-start(bf16[8,224,128]{2,1,0:T(8,128)(2,1)} %kappa_in.1) | copy-start | bytes 1376260
  2.6 1.1 %copy-start.5 = (bf16[8,224,128]{2,1,0:T(8,128)(2,1)S(1)}, bf16[8,224,128]{2,1,0:T(8,128)(2,1)}, u32[]{:S(2)}) copy-start(bf16[8,224,128]{2,1,0:T(8,128)(2,1)} %obs_in.1) | copy-start | bytes 1376260
  3.7 42.6 %collective-permute-start = (bf16[24,224,128]{2,1,0:T(8,128)(2,1)S(1)}, bf16[24,224,128]{2,1,0:T(8,128)(2,1)S(1)}, u32[]{:S(2)}, u32[]{:S(2)}) collective-permute-start(bf16[24,224,128]{2,1,0:T(8,128)(2,1)S(1)} %get-tuple-element.50), channel_id=1, source_target_pairs={{0,8},{8,16},{16,24},{24,32},{32,40},{40,48},{48,56},{56,64},{64,7... | collective-permute-start | bytes 4128776 | tf_op jit(solution)/shard_map/ppermute | solution.py:20
  5.6 38.2 %collective-permute-start.1 = (bf16[22,224,128]{2,1,0:T(8,128)(2,1)S(1)}, bf16[22,224,128]{2,1,0:T(8,128)(2,1)S(1)}, u32[]{:S(2)}, u32[]{:S(2)}) collective-permute-start(bf16[22,224,128]{2,1,0:T(8,128)(2,1)S(1)} %get-tuple-element.49), channel_id=1, source_target_pairs={{0,504},{8,0},{16,8},{24,16},{32,24},{40,32},{48,40},{56,48},{64,5... | collective-permute-start | bytes 3784712 | tf_op jit(solution)/shard_map/ppermute | solution.py:20
  43.8 9.0 %copy-start.3 = (bf16[22,224,128]{2,1,0:T(8,128)(2,1)}, bf16[22,224,128]{2,1,0:T(8,128)(2,1)S(1)}, u32[]{:S(2)}) copy-start(bf16[22,224,128]{2,1,0:T(8,128)(2,1)S(1)} %collective-permute-done.1.east_p) | copy-start | bytes 3784708
  46.2 1.1 %copy-start.2 = (bf16[24,224,128]{2,1,0:T(8,128)(2,1)}, bf16[24,224,128]{2,1,0:T(8,128)(2,1)S(1)}, u32[]{:S(2)}) copy-start(bf16[24,224,128]{2,1,0:T(8,128)(2,1)S(1)} %collective-permute-done.west_p) | copy-start | bytes 4128772
  47.5 8.4 %collective-permute-start.3 = (f32[6,16,4,128]{3,2,1,0:T(4,128)S(1)}, f32[6,16,4,128]{3,2,1,0:T(4,128)S(1)}, u32[]{:S(2)}, u32[]{:S(2)}) collective-permute-start(f32[6,16,4,128]{3,2,1,0:T(4,128)S(1)} %constant_dynamic-update-slice_fusion.6), channel_id=1, source_target_pairs={{1,0},{2,1},{3,2},{4,3},{5,4},{6,5},{7,6},{9,8},{10,9},{11,10},{12... | collective-permute-start | bytes 589832 | tf_op jit(solution)/shard_map/ppermute | solution.py:20
  52.8 9.7 %collective-permute-start.2 = (f32[6,16,4,128]{3,2,1,0:T(4,128)S(1)}, f32[6,16,4,128]{3,2,1,0:T(4,128)S(1)}, u32[]{:S(2)}, u32[]{:S(2)}) collective-permute-start(f32[6,16,4,128]{3,2,1,0:T(4,128)S(1)} %constant_dynamic-update-slice_fusion), channel_id=1, source_target_pairs={{0,1},{1,2},{2,3},{3,4},{4,5},{5,6},{6,7},{8,9},{9,10},{10,11},{11... | collective-permute-start | bytes 589832 | tf_op jit(solution)/shard_map/ppermute | solution.py:20
  55.9 7.4 %copy-start.6 = (f32[6,16,4,128]{3,2,1,0:T(4,128)}, f32[6,16,4,128]{3,2,1,0:T(4,128)S(1)}, u32[]{:S(2)}) copy-start(f32[6,16,4,128]{3,2,1,0:T(4,128)S(1)} %collective-permute-done.3.north_halo) | copy-start | bytes 589828
  62.5 0.7 copy-start.7

commit v5 on v4

--- a/solution.py
+++ b/solution.py
@@ -32,9 +32,10 @@
     for key, rows, steps in (("east", east_rows, -1), ("west", west_rows, 1)):
         start = (lambda r: 0) if key == "east" else (lambda r: size - r)
         pieces = [lax.slice_in_dim(f, start(r), start(r) + r, axis=0) for f, r in zip(fields, rows)]
-        high = pieces[0].astype(jnp.bfloat16)
-        low = (pieces[0] - high.astype(jnp.float32)).astype(jnp.bfloat16)
-        got[key] = passed_along(jnp.concatenate([high, low] + pieces[1:], 0), "lon", steps, True)
+        high = lax.reduce_precision(pieces[0], exponent_bits=8, mantissa_bits=7)
+        low = pieces[0] - high
+        parts = [high.astype(jnp.bfloat16), low.astype(jnp.bfloat16)] + pieces[1:]
+        got[key] = passed_along(jnp.concatenate(parts, 0), "lon", steps, True)
     return got
 
 

time: 78.3 us -> 78.3 us (level)
  local copies, waits for them, and re-layouts: 4.82 us -> 3.42 us
  other arithmetic: 0.41 us -> 1.8 us
    unnamed x23 -> x22, local copies, waits for them, and re-layouts: 3.79 us -> 2.39 us
    unnamed x10 -> x11, other arithmetic: 0.27 us -> 1.66 us
where the time goes in v5:
time: 78.3 us; the launch traced here: 78.1 us
  waiting for transfers between devices  35.6 us (45%)
  starting transfers between devices  21.4 us (27%)
  Pallas kernels  14.9 us (19%)
  local copies, waits for them, and re-layouts  3.42 us (4%)
  other arithmetic  1.8 us (2%)
  between operations  0.99 us (1%)
    ppermute x4, waiting for transfers between devices, passed_along(): return lax.ppermute(value, axis, pairs)  35.6 us
    ppermute x4, starting transfers between devices, passed_along(): return lax.ppermute(value, axis, pairs)  21.4 us
    pallas_call x1, Pallas kernels, body(): pl.pallas_call(functools.partial(stencil_kernel, west_rows, east_rows), o...  14.9 us
    unnamed x22, local copies, waits for them, and re-layouts  2.39 us
    unnamed x11, other arithmetic  1.66 us
  transfers between devices with their start and end apart: 4, of which 4 were waited for; matrix products, arithmetic and copies ran while one was open for 0% of the time, Pallas kernels for 0%

profile of v5, /device:TPU:64, one launch (start us, length us, event | category | flops | bytes accessed | tf_op | source)
XLA Modules:
  0.0 78.1 jit_solution(4925529358950879992)
XLA Ops:
  0.6 0.0 copy-start.1
  0.6 0.0 copy-start
  0.7 1.4 %fusion.5 = (bf16[22,224,128]{2,1,0:T(8,128)(2,1)S(1)}, bf16[24,224,128]{2,1,0:T(8,128)(2,1)S(1)}) fusion(f32[8,224,128]{2,1,0:T(8,128)} %conc_in.1), kind=kLoop, calls=%fused_computation.14 | loop fusion | flops 458750 | bytes 1376256
  2.0 0.1 copy-done.1
  2.1 0.1 fusion.2
  2.2 0.0 copy-start.4
  2.2 0.3 copy-done
  2.6 0.0 copy-start.5
  2.7 0.6 copy-done.4
  3.4 0.2 copy-done.5
  3.7 1.9 %collective-permute-start = (bf16[24,224,128]{2,1,0:T(8,128)(2,1)S(1)}, bf16[24,224,128]{2,1,0:T(8,128)(2,1)S(1)}, u32[]{:S(2)}, u32[]{:S(2)}) collective-permute-start(bf16[24,224,128]{2,1,0:T(8,128)(2,1)S(1)} %get-tuple-element.50), channel_id=1, source_target_pairs={{0,8},{8,16},{16,24},{24,32},{32,40},{40,48},{48,56},{56,64},{64,7... | collective-permute-start | bytes 4128776 | tf_op jit(solution)/shard_map/ppermute | solution.py:20
  5.6 12.4 %collective-permute-start.1 = (bf16[22,224,128]{2,1,0:T(8,128)(2,1)S(1)}, bf16[22,224,128]{2,1,0:T(8,128)(2,1)S(1)}, u32[]{:S(2)}, u32[]{:S(2)}) collective-permute-start(bf16[22,224,128]{2,1,0:T(8,128)(2,1)S(1)} %get-tuple-element.49), channel_id=1, source_target_pairs={{0,504},{8,0},{16,8},{24,16},{32,24},{40,32},{48,40},{56,48},{64,5... | collective-permute-start | bytes 3784712 | tf_op jit(solution)/shard_map/ppermute | solution.py:20
  18.0 0.1 slice_bitcast_fusion
  18.2 25.6 %collective-permute-done.1.east_p = bf16[22,224,128]{2,1,0:T(8,128)(2,1)S(1)} collective-permute-done((bf16[22,224,128]{2,1,0:T(8,128)(2,1)S(1)}, bf16[22,224,128]{2,1,0:T(8,128)(2,1)S(1)}, u32[]{:S(2)}, u32[]{:S(2)}) %collective-permute-start.1) | collective-permute-done | bytes 1261600 | tf_op jit(solution)/shard_map/ppermute | solution.py:20
  43.8 0.0 copy-start.3
  43.9 2.3 %collective-permute-done.west_p = bf16[24,224,128]{2,1,0:T(8,128)(2,1)S(1)} collective-permute-done((bf16[24,224,128]{2,1,0:T(8,128)(2,1)S(1)}, bf16[24,224,128]{2,1,0:T(8,128)(2,1)S(1)}, u32[]{:S(2)}, u32[]{:S(2)}) %collective-permute-start) | collective-permute-done | bytes 1376288 | tf_op jit(solution)/shard_map/ppermute | solution.py:20
  46.2 0.0 copy-start.2
  46.4 1.0 %copy-done.2 = bf16[24,224,128]{2,1,0:T(8,128)(2,1)} copy-done((bf16[24,224,128]{2,1,0:T(8,128)(2,1)}, bf16[24,224,128]{2,1,0:T(8,128)(2,1)S(1)}, u32[]{:S(2)}) %copy-start.2) | copy-done | bytes 1376280
  47.5 5.2 %collective-permute-start.3 = (f32[6,16,4,128]{3,2,1,0:T(4,128)S(1)}, f32[6,16,4,128]{3,2,1,0:T(4,128)S(1)}, u32[]{:S(2)}, u32[]{:S(2)}) collective-permute-start(f32[6,16,4,128]{3,2,1,0:T(4,128)S(1)} %constant_dynamic-update-slice_fusion.6), channel_id=1, source_target_pairs={{1,0},{2,1},{3,2},{4,3},{5,4},{6,5},{7,6},{9,8},{10,9},{11,10},{12... | collective-permute-start | bytes 589832 | tf_op jit(solution)/shard_map/ppermute | solution.py:20
  52.8 0.0 copy-done.3
  52.8 1.9 %collective-permute-start.2 = (f32[6,16,4,128]{3,2,1,0:T(4,128)S(1)}, f32[6,16,4,128]{3,2,1,0:T(4,128)S(1)}, u32[]{:S(2)}, u32[]{:S(2)}) collective-permute-start(f32[6,16,4,128]{3,2,1,0:T(4,128)S(1)} %constant_dynamic-update-slice_fusion), channel_id=1, source_target_pairs={{0,1},{1,2},{2,3},{3,4},{4,5},{5,6},{6,7},{8,9},{9,10},{10,11},{11... | collective-permute-start | bytes 589832 | tf_op jit(solution)/shard_map/ppermute | solution.py:20
  54.8 1.1 %collective-permute-done.3.north_halo = f32[6,16,4,128]{3,2,1,0:T(4,128)S(1)} collective-permute-done((f32[6,16,4,128]{3,2,1,0:T(4,128)S(1)}, f32[6,16,4,128]{3,2,1,0:T(4,128)S(1)}, u32[]{:S(2)}, u32[]{:S(2)}) %collective-permute-start.3) | collective-permute-done | bytes 196640 | tf_op jit(solution)/shard_map/ppermute | solution.py:20
  55.9 0.0 copy-start.6
  55.9 6.7 %collective-permute-done.2.south_ref = f32[6,16,4,128]{3,2,1,0:T(4,128)S(1)} collective-permute-done((f32[6,16,4,128]{3,2,1,0:T(4,128)S(1)}, f32[6,16,4,128]{3,2,1,0:T(4,128)S(1)}, u32[]{:S(2)}, u32[]{:S(2)}) %collective-permute-start.2) | collective-permute-done | bytes 196640 | tf_op jit(solution)/shard_map/ppermute | solution.py:20
  62.5 0.0 copy-start.7
  62.5 0.7 iota.7.north_ref
  63.2 0.0 copy-done.6
  63.2 0.0 copy-done.7
  63.3 14.9 %shard_map.59 = (f32[8,224,128]{2,1,0:T(8,128)}, f32[8,224,128]{2,1,0:T(8,128)}) custom-call(f32[8,224,128]{2,1,0:T(8,128)} %conc_in.1, bf16[3,8,224,128]{3,2,1,0:T(8,128)(2,1)} %wind_in.1, bf16[8,224,128]{2,1,0:T(8,128)(2,1)} %kappa_in.1, bf16[8,224,128]{2,1,0:T(8,128)(2,1)} %obs_in.1, bf16[24,224,128]{2,1,0:T(8,128)(2,1)} %copy-done.2, ...), custom_call_target="tpu_custom_call" | custom-call | tf_op jit(solution)/shard_map/pallas_call | solution.py:216
  (41 shorter events, 0.7 us)
Async XLA Ops:
  0.6 1.5 %copy-start.1 = (f32[8,224,128]{2,1,0:T(8,128)S(1)}, f32[8,224,128]{2,1,0:T(8,128)}, u32[]{:S(2)}) copy-start(f32[8,224,128]{2,1,0:T(8,128)} %conc_in.1) | copy-start | bytes 2752516
  0.6 1.9 %copy-start = (bf16[3,8,224,128]{3,2,1,0:T(8,128)(2,1)S(1)}, bf16[3,8,224,128]{3,2,1,0:T(8,128)(2,1)}, u32[]{:S(2)}) copy-start(bf16[3,8,224,128]{3,2,1,0:T(8,128)(2,1)} %wind_in.1) | copy-start | bytes 4128772
  2.2 1.1 %copy-start.4 = (bf16[8,224,128]{2,1,0:T(8,128)(2,1)S(1)}, bf16[8,224,128]{2,1,0:T(8,128)(2,1)}, u32[]{:S(2)}) copy-start(bf16[8,224,128]{2,1,0:T(8,128)(2,1)} %kappa_in.1) | copy-start | bytes 1376260
  2.6 1.1 %copy-start.5 = (bf16[8,224,128]{2,1,0:T(8,128)(2,1)S(1)}, bf16[8,224,128]{2,1,0:T(8,128)(2,1)}, u32[]{:S(2)}) copy-start(bf16[8,224,128]{2,1,0:T(8,128)(2,1)} %obs_in.1) | copy-start | bytes 1376260
  3.7 42.6 %collective-permute-start = (bf16[24,224,128]{2,1,0:T(8,128)(2,1)S(1)}, bf16[24,224,128]{2,1,0:T(8,128)(2,1)S(1)}, u32[]{:S(2)}, u32[]{:S(2)}) collective-permute-start(bf16[24,224,128]{2,1,0:T(8,128)(2,1)S(1)} %get-tuple-element.50), channel_id=1, source_target_pairs={{0,8},{8,16},{16,24},{24,32},{32,40},{40,48},{48,56},{56,64},{64,7... | collective-permute-start | bytes 4128776 | tf_op jit(solution)/shard_map/ppermute | solution.py:20
  5.6 38.2 %collective-permute-start.1 = (bf16[22,224,128]{2,1,0:T(8,128)(2,1)S(1)}, bf16[22,224,128]{2,1,0:T(8,128)(2,1)S(1)}, u32[]{:S(2)}, u32[]{:S(2)}) collective-permute-start(bf16[22,224,128]{2,1,0:T(8,128)(2,1)S(1)} %get-tuple-element.49), channel_id=1, source_target_pairs={{0,504},{8,0},{16,8},{24,16},{32,24},{40,32},{48,40},{56,48},{64,5... | collective-permute-start | bytes 3784712 | tf_op jit(solution)/shard_map/ppermute | solution.py:20
  43.8 9.0 %copy-start.3 = (bf16[22,224,128]{2,1,0:T(8,128)(2,1)}, bf16[22,224,128]{2,1,0:T(8,128)(2,1)S(1)}, u32[]{:S(2)}) copy-start(bf16[22,224,128]{2,1,0:T(8,128)(2,1)S(1)} %collective-permute-done.1.east_p) | copy-start | bytes 3784708
  46.2 1.1 %copy-start.2 = (bf16[24,224,128]{2,1,0:T(8,128)(2,1)}, bf16[24,224,128]{2,1,0:T(8,128)(2,1)S(1)}, u32[]{:S(2)}) copy-start(bf16[24,224,128]{2,1,0:T(8,128)(2,1)S(1)} %collective-permute-done.west_p) | copy-start | bytes 4128772
  47.5 8.4 %collective-permute-start.3 = (f32[6,16,4,128]{3,2,1,0:T(4,128)S(1)}, f32[6,16,4,128]{3,2,1,0:T(4,128)S(1)}, u32[]{:S(2)}, u32[]{:S(2)}) collective-permute-start(f32[6,16,4,128]{3,2,1,0:T(4,128)S(1)} %constant_dynamic-update-slice_fusion.6), channel_id=1, source_target_pairs={{1,0},{2,1},{3,2},{4,3},{5,4},{6,5},{7,6},{9,8},{10,9},{11,10},{12... | collective-permute-start | bytes 589832 | tf_op jit(solution)/shard_map/ppermute | solution.py:20
  52.8 9.7 %collective-permute-start.2 = (f32[6,16,4,128]{3,2,1,0:T(4,128)S(1)}, f32[6,16,4,128]{3,2,1,0:T(4,128)S(1)}, u32[]{:S(2)}, u32[]{:S(2)}) collective-permute-start(f32[6,16,4,128]{3,2,1,0:T(4,128)S(1)} %constant_dynamic-update-slice_fusion), channel_id=1, source_target_pairs={{0,1},{1,2},{2,3},{3,4},{4,5},{5,6},{6,7},{8,9},{9,10},{10,11},{11... | collective-permute-start | bytes 589832 | tf_op jit(solution)/shard_map/ppermute | solution.py:20
  55.9 7.4 %copy-start.6 = (f32[6,16,4,128]{3,2,1,0:T(4,128)}, f32[6,16,4,128]{3,2,1,0:T(4,128)S(1)}, u32[]{:S(2)}) copy-start(f32[6,16,4,128]{3,2,1,0:T(4,128)S(1)} %collective-permute-done.3.north_halo) | copy-start | bytes 589828
  62.5 0.7 copy-start.7

commit v6 on v5

--- a/solution.py
+++ b/solution.py
@@ -62,23 +62,39 @@
     return passed_along(highs, "lat", 1, False), passed_along(lows, "lat", -1, False)
 
 
-def stencil_kernel(west_rows, east_rows, conc_in, wind_in, kappa_in, obs_in, west_p, east_p,
-                   south_ref, north_halo, north_ref, gc_ref, gk_ref, raw_ref, own_ref, oth_ref, mid_ref, lam2_ref,
-                   lam1_ref):
+def stencil_kernel(west_rows, east_rows, layout, conc_in, wind_in, kappa_in, obs_in, west_p, east_p, south_ref,
+                   north_halo, north_ref, *rest):
+    own_at, south_at, north_at, out_at = layout
+    gc_ref, gk_ref, raw_ref, own_ref, oth_ref, mid_ref, lam2_ref, lam1_ref = rest[-8:]
     fields, rows, lats, levels = raw_ref.shape
     block = conc_in.shape[0]
+    own_n = conc_in.shape[1]
+    out_n = gc_ref.shape[1]
     f32 = jnp.float32
     north_open = north_ref[...]
-    lo = PAD
-    hi = lats - PAD
-    gap = jnp.zeros((PAD - HALO, levels), f32)
+    covered = [(own_at, own_at + own_n)]
+    if south_at is not None:
+        covered.append((south_at, south_at + HALO))
+    if north_at is not None:
+        covered.append((north_at, north_at + HALO))
+    covered.sort()
+    gaps = []
+    at = 0
+    for lo, hi in covered:
+        if lo > at:
+            gaps.append((at, lo))
+        at = hi
+    if at < lats:
+        gaps.append((at, lats))
 
     def put(f, r, core):
-        raw_ref[f, r, lo:hi] = core
-        raw_ref[f, r, lo - HALO:lo] = south_ref[f, r]
-        raw_ref[f, r, hi:hi + HALO] = north_halo[f, r]
-        raw_ref[f, r, :lo - HALO] = gap
-        raw_ref[f, r, hi + HALO:] = gap
+        raw_ref[f, r, own_at:own_at + own_n] = core
+        if south_at is not None:
+            raw_ref[f, r, south_at:south_at + HALO] = south_ref[f, r]
+        if north_at is not None:
+            raw_ref[f, r, north_at:north_at + HALO] = north_halo[f, r]
+        for lo, hi in gaps:
+            raw_ref[f, r, lo:hi] = jnp.zeros((hi - lo, levels), f32)
 
     def own_row(i, carry):
         put(0, i + HALO, conc_in[i])
@@ -89,7 +105,7 @@
         return carry
 
     lax.fori_loop(0, block, own_row, 0)
-    empty = jnp.zeros((hi - lo, levels), f32)
+    empty = jnp.zeros((own_n, levels), f32)
     for r in range(HALO):
         put(0, r, west_p[r].astype(f32) + west_p[HALO + r].astype(f32))
         put(0, HALO + block + r, east_p[r].astype(f32) + east_p[HALO + r].astype(f32))
@@ -189,8 +205,8 @@
         lam = lam2_ref[i]
         gaps2 = (lam2_ref[i + 1] - lam, next_lat(lam) - lam, next_lev(lam) - lam)
         kappa = kappa_term(gaps2, mid_ref, i) + kappa_term(gaps1, conc_ref, i)
-        gc_ref[i - h] = out[PAD:lats - PAD]
-        gk_ref[i - h] = kappa[PAD:lats - PAD]
+        gc_ref[i - h] = out[out_at:out_at + out_n]
+        gk_ref[i - h] = kappa[out_at:out_at + out_n]
         return p0
 
     lax.fori_loop(h, rows - h, last_row, part0(lam1_ref, h - 1))
@@ -210,27 +226,65 @@
     ext_lats = lat_rows + 2 * PAD
     lat_place = lax.axis_index("lat") * lat_rows - PAD + lax.broadcasted_iota(jnp.int32, (ext_lats, levels), 0)
     north_open = ((lat_place >= 0) & (lat_place < lat_total - 1)).astype(jnp.float32)
-    whole = [concentration, wind, kappa, observed, got["west"], got["east"], south, north, north_open]
+    packs = [got["west"], got["east"]]
+    own = [concentration, wind, kappa, observed]
     vmem = pltpu.MemorySpace.VMEM
-    state = pltpu.VMEM((ext_rows, ext_lats, levels), jnp.float32)
-    return pl.pallas_call(
-        functools.partial(stencil_kernel, west_rows, east_rows),
-        out_shape=(
-            jax.ShapeDtypeStruct((lon_rows, lat_rows, levels), jnp.float32),
-            jax.ShapeDtypeStruct((lon_rows, lat_rows, levels), jnp.float32),
-        ),
-        in_specs=[pl.BlockSpec(memory_space=vmem) for _ in whole],
-        out_specs=(pl.BlockSpec(memory_space=vmem), pl.BlockSpec(memory_space=vmem)),
-        scratch_shapes=[
-            pltpu.VMEM((len(fields), ext_rows, ext_lats, levels), jnp.float32),
-            pltpu.VMEM((3, ext_rows, ext_lats, levels), jnp.float32),
-            pltpu.VMEM((3, ext_rows, ext_lats, levels), jnp.float32),
+    out_type = jax.ShapeDtypeStruct((lon_rows, lat_rows, levels), jnp.float32)
+
+    def scratch(window):
+        state = pltpu.VMEM((ext_rows, window, levels), jnp.float32)
+        return [
+            pltpu.VMEM((len(fields), ext_rows, window, levels), jnp.float32),
+            pltpu.VMEM((3, ext_rows, window, levels), jnp.float32),
+            pltpu.VMEM((3, ext_rows, window, levels), jnp.float32),
             state,
             state,
             state,
-        ],
+        ]
+
+    empty_halo = jnp.zeros_like(north)
+    whole = own + packs + [empty_halo, empty_halo, north_open]
+    grad_conc, grad_kappa = pl.pallas_call(
+        functools.partial(stencil_kernel, west_rows, east_rows, (PAD, None, None, PAD)),
+        out_shape=(out_type, out_type),
+        in_specs=[pl.BlockSpec(memory_space=vmem) for _ in whole],
+        out_specs=(pl.BlockSpec(memory_space=vmem), pl.BlockSpec(memory_space=vmem)),
+        scratch_shapes=scratch(ext_lats),
         compiler_params=pltpu.CompilerParams(vmem_limit_bytes=60 * 1024 * 1024),
     )(*whole)
+
+    strip = 2 * PAD
+    window = 3 * PAD
+    for side in ("south", "north"):
+        if side == "south":
+            layout = (PAD, PAD - HALO, None, PAD)
+            first = 0
+            mask = north_open[:window]
+        else:
+            layout = (0, None, strip, PAD)
+            first = lat_rows - strip
+            mask = north_open[ext_lats - window:]
+        out_block = first // PAD + (0 if side == "south" else 1)
+        in_block = first // strip
+
+        def rows_of(array, lead):
+            shape = array.shape[:lead] + (strip, levels)
+            return pl.BlockSpec(shape, lambda i, lead=lead: (0,) * lead + (in_block, 0))
+
+        args = own + packs + [south, north, mask, grad_conc, grad_kappa]
+        specs = [rows_of(a, a.ndim - 2) for a in own + packs]
+        specs += [pl.BlockSpec(memory_space=vmem)] * 3 + [pl.BlockSpec(memory_space=pl.ANY)] * 2
+        out_spec = pl.BlockSpec((lon_rows, PAD, levels), lambda i: (0, out_block, 0))
+        grad_conc, grad_kappa = pl.pallas_call(
+            functools.partial(stencil_kernel, west_rows, east_rows, layout),
+            out_shape=(out_type, out_type),
+            grid=(1,),
+            in_specs=specs,
+            out_specs=(out_spec, out_spec),
+            scratch_shapes=scratch(window),
+            input_output_aliases={len(args) - 2: 0, len(args) - 1: 1},
+        )(*args)
+    return grad_conc, grad_kappa
 
 
 def solution(mesh):

time: 78.3 us -> 99.8 us (1.27)
  the two profiles are of different devices: /device:TPU:64 before, /device:TPU:6 now
where the time goes in v6:
time: 99.8 us; the launch traced here: 99.4 us
  Pallas kernels  31.7 us (32%)
  waiting for transfers between devices  27.4 us (27%)
  starting transfers between devices  23.1 us (23%)
  local copies, waits for them, and re-layouts  11.8 us (12%)
  other arithmetic  4.38 us (4%)
    ppermute x4, waiting for transfers between devices, passed_along(): return lax.ppermute(value, axis, pairs)  27.4 us
    ppermute x4, starting transfers between devices, passed_along(): return lax.ppermute(value, axis, pairs)  23.1 us
    pallas_call x2, Pallas kernels, body(): pl.pallas_call(functools.partial(stencil_kernel, west_rows, east_rows, la...  16.9 us
    pallas_call x1, Pallas kernels, body(): pl.pallas_call(functools.partial(stencil_kernel, west_rows, east_rows, (P...  14.8 us
    unnamed x24, local copies, waits for them, and re-layouts  4.39 us
    unnamed x11, other arithmetic  3.2 us
    concatenate x13, local copies, waits for them, and re-layouts, edge(): jnp.concatenate([pad_rows(part(pw), 0, HALO - w, 0), part(f), pad_rows(pa...  2.2 us
    iota x3, local copies, waits for them, and re-layouts, body(): lax.broadcasted_iota(jnp.int32, (ext_lats, levels), 0)  2.12 us
  transfers between devices with their start and end apart: 4, of which 2 were waited for; matrix products, arithmetic and copies ran while one was open for 3% of the time, Pallas kernels for 15%

profile of v6, /device:TPU:6, one launch (start us, length us, event | category | flops | bytes accessed | tf_op | source)
XLA Modules:
  0.0 99.4 jit_solution(8235766433925814479)
XLA Ops:
  0.6 0.0 copy-start.1
  0.6 0.0 copy-start
  0.7 2.2 %fusion.5 = (bf16[22,224,128]{2,1,0:T(8,128)(2,1)}, bf16[24,224,128]{2,1,0:T(8,128)(2,1)}) fusion(f32[8,224,128]{2,1,0:T(8,128)} %conc_in.5), kind=kLoop, calls=%fused_computation.14 | loop fusion | flops 458750 | bytes 1376256
  2.8 0.0 copy-done.1
  2.8 0.9 fusion.2
  3.7 0.0 copy-start.3
  3.7 0.0 copy-done
  3.7 0.7 bitcast_dynamic-update-slice_fusion
  4.4 0.0 copy-start.4
  4.4 0.7 bitcast_dynamic-update-slice_fusion.3
  5.1 0.8 bitcast_dynamic-update-slice_fusion.2
  5.9 0.8 bitcast_dynamic-update-slice_fusion.1
  6.6 0.0 copy-done.3
  6.6 0.7 slice_dynamic-update-slice_fusion
  7.3 0.7 slice_dynamic-update-slice_fusion.1
  8.0 0.0 copy-done.4
  8.0 0.7 slice_dynamic-update-slice_fusion.2
  8.7 1.9 %collective-permute-start = (bf16[24,224,128]{2,1,0:T(8,128)(2,1)}, bf16[24,224,128]{2,1,0:T(8,128)(2,1)}, u32[]{:S(2)}, u32[]{:S(2)}) collective-permute-start(bf16[24,224,128]{2,1,0:T(8,128)(2,1)} %get-tuple-element.58), channel_id=1, source_target_pairs={{0,8},{8,16},{16,24},{24,32},{32,40},{40,48},{48,56},{56,64},{64,7... | collective-permute-start | bytes 4128776 | tf_op jit(solution)/shard_map/ppermute | solution.py:20
  10.6 13.3 %collective-permute-start.1 = (bf16[22,224,128]{2,1,0:T(8,128)(2,1)}, bf16[22,224,128]{2,1,0:T(8,128)(2,1)S(1)}, u32[]{:S(2)}, u32[]{:S(2)}) collective-permute-start(bf16[22,224,128]{2,1,0:T(8,128)(2,1)} %get-tuple-element.57), channel_id=1, source_target_pairs={{0,504},{8,0},{16,8},{24,16},{32,24},{40,32},{48,40},{56,48},{64,5... | collective-permute-start | bytes 3784712 | tf_op jit(solution)/shard_map/ppermute | solution.py:20
  23.9 0.6 slice_bitcast_fusion.10
  24.5 0.7 slice_bitcast_fusion.9
  25.3 0.1 slice_bitcast_fusion
  25.4 0.0 copy-start.8
  25.5 0.0 copy-start.7
  25.5 22.8 %collective-permute-done.1.east_p = bf16[22,224,128]{2,1,0:T(8,128)(2,1)S(1)} collective-permute-done((bf16[22,224,128]{2,1,0:T(8,128)(2,1)}, bf16[22,224,128]{2,1,0:T(8,128)(2,1)S(1)}, u32[]{:S(2)}, u32[]{:S(2)}) %collective-permute-start.1) | collective-permute-done | bytes 1261600 | tf_op jit(solution)/shard_map/ppermute | solution.py:20
  48.3 0.0 copy-start.2
  48.5 4.6 %collective-permute-done.west_p = bf16[24,224,128]{2,1,0:T(8,128)(2,1)} collective-permute-done((bf16[24,224,128]{2,1,0:T(8,128)(2,1)}, bf16[24,224,128]{2,1,0:T(8,128)(2,1)}, u32[]{:S(2)}, u32[]{:S(2)}) %collective-permute-start) | collective-permute-done | bytes 1376288 | tf_op jit(solution)/shard_map/ppermute | solution.py:20
  53.0 1.1 %convert_add_fusion.1 = f32[4,224,128]{2,1,0:T(8,128)S(1)} fusion(bf16[24,224,128]{2,1,0:T(8,128)(2,1)} %collective-permute-done.west_p), kind=kLoop, calls=%fused_computation.10 | loop fusion | flops 344064 | bytes 917504 | tf_op jit(solution)/shard_map/add | solution.py:43
  54.2 0.8 fusion.7
  54.9 0.7 fusion.6
  55.6 0.8 slice_bitcast_fusion.13
  56.5 0.0 copy-done.8
  56.5 2.7 %collective-permute-start.3 = (f32[6,16,4,128]{3,2,1,0:T(4,128)S(1)}, f32[6,16,4,128]{3,2,1,0:T(4,128)S(1)}, u32[]{:S(2)}, u32[]{:S(2)}) collective-permute-start(f32[6,16,4,128]{3,2,1,0:T(4,128)S(1)} %constant_dynamic-update-slice_fusion.6), channel_id=1, source_target_pairs={{1,0},{2,1},{3,2},{4,3},{5,4},{6,5},{7,6},{9,8},{10,9},{11,10},{12... | collective-permute-start | bytes 589832 | tf_op jit(solution)/shard_map/ppermute | solution.py:20
  59.4 0.0 copy-done.2
  59.4 0.0 copy-done.7
  59.4 5.2 %collective-permute-start.2 = (f32[6,16,4,128]{3,2,1,0:T(4,128)S(1)}, f32[6,16,4,128]{3,2,1,0:T(4,128)S(1)}, u32[]{:S(2)}, u32[]{:S(2)}) collective-permute-start(f32[6,16,4,128]{3,2,1,0:T(4,128)S(1)} %constant_dynamic-update-slice_fusion), channel_id=1, source_target_pairs={{0,1},{1,2},{2,3},{3,4},{4,5},{5,6},{6,7},{8,9},{9,10},{10,11},{11... | collective-permute-start | bytes 589832 | tf_op jit(solution)/shard_map/ppermute | solution.py:20
  64.7 0.1 fusion.13
  64.7 0.7 iota.13.north_ref
  65.5 0.7 broadcast_in_dim.3.south_ref.north_halo
  66.2 14.8 %shard_map.59 = (f32[8,224,128]{2,1,0:T(8,128)}, f32[8,224,128]{2,1,0:T(8,128)}) custom-call(f32[8,224,128]{2,1,0:T(8,128)} %conc_in.5, bf16[3,8,224,128]{3,2,1,0:T(8,128)(2,1)} %wind_in.5, bf16[8,224,128]{2,1,0:T(8,128)(2,1)} %kappa_in.5, bf16[8,224,128]{2,1,0:T(8,128)(2,1)} %obs_in.5, bf16[24,224,128]{2,1,0:T(8,128)(2,1)} %collective-permute-done.west_p, ...), custom_call_target="tpu_custom_call" | custom-call | tf_op jit(solution)/shard_map/pallas_call | solution.py:247
  81.0 0.0 collective-permute-done.3.north_halo
  81.0 0.0 copy-start.5
  81.0 0.0 collective-permute-done.2.south_ref
  81.1 0.0 copy-start.6
  81.1 0.7 iota.12.north_ref
  81.8 0.0 copy-done.5
  81.8 0.0 copy-done.6
  81.8 8.4 %shard_map.60 = (f32[8,224,128]{2,1,0:T(8,128)}, f32[8,224,128]{2,1,0:T(8,128)}) custom-call(f32[8,224,128]{2,1,0:T(8,128)} %conc_in.5, bf16[3,8,224,128]{3,2,1,0:T(8,128)(2,1)} %wind_in.5, bf16[8,224,128]{2,1,0:T(8,128)(2,1)} %kappa_in.5, bf16[8,224,128]{2,1,0:T(8,128)(2,1)} %obs_in.5, ...), custom_call_target="tpu_custom_call", output_to_operand_aliasing={{0}: (9, {}), {1}: (10, {})} | custom-call | tf_op jit(solution)/shard_map/pallas_call | solution.py:278
  90.3 0.7 iota.11.north_ref
  90.9 8.4 %shard_map.61 = (f32[8,224,128]{2,1,0:T(8,128)}, f32[8,224,128]{2,1,0:T(8,128)}) custom-call(f32[8,224,128]{2,1,0:T(8,128)} %conc_in.5, bf16[3,8,224,128]{3,2,1,0:T(8,128)(2,1)} %wind_in.5, bf16[8,224,128]{2,1,0:T(8,128)(2,1)} %kappa_in.5, bf16[8,224,128]{2,1,0:T(8,128)(2,1)} %obs_in.5, ...), custom_call_target="tpu_custom_call", output_to_operand_aliasing={{0}: (9, {}), {1}: (10, {})} | custom-call | tf_op jit(solution)/shard_map/pallas_call | solution.py:278
  (28 shorter events, 0.4 us)
Async XLA Ops:
  0.6 2.2 %copy-start.1 = (f32[8,224,128]{2,1,0:T(8,128)S(1)}, f32[8,224,128]{2,1,0:T(8,128)}, u32[]{:S(2)}) copy-start(f32[8,224,128]{2,1,0:T(8,128)} %conc_in.5) | copy-start | bytes 2752516
  0.6 3.1 %copy-start = (bf16[3,8,224,128]{3,2,1,0:T(8,128)(2,1)S(1)}, bf16[3,8,224,128]{3,2,1,0:T(8,128)(2,1)}, u32[]{:S(2)}) copy-start(bf16[3,8,224,128]{3,2,1,0:T(8,128)(2,1)} %wind_in.5) | copy-start | bytes 4128772
  3.7 2.9 %copy-start.3 = (bf16[8,224,128]{2,1,0:T(8,128)(2,1)S(1)}, bf16[8,224,128]{2,1,0:T(8,128)(2,1)}, u32[]{:S(2)}) copy-start(bf16[8,224,128]{2,1,0:T(8,128)(2,1)} %kappa_in.5) | copy-start | bytes 1376260
  4.4 3.6 %copy-start.4 = (bf16[8,224,128]{2,1,0:T(8,128)(2,1)S(1)}, bf16[8,224,128]{2,1,0:T(8,128)(2,1)}, u32[]{:S(2)}) copy-start(bf16[8,224,128]{2,1,0:T(8,128)(2,1)} %obs_in.5) | copy-start | bytes 1376260
  8.7 44.3 %collective-permute-start = (bf16[24,224,128]{2,1,0:T(8,128)(2,1)}, bf16[24,224,128]{2,1,0:T(8,128)(2,1)}, u32[]{:S(2)}, u32[]{:S(2)}) collective-permute-start(bf16[24,224,128]{2,1,0:T(8,128)(2,1)} %get-tuple-element.58), channel_id=1, source_target_pairs={{0,8},{8,16},{16,24},{24,32},{32,40},{40,48},{48,56},{56,64},{64,7... | collective-permute-start | bytes 4128776 | tf_op jit(solution)/shard_map/ppermute | solution.py:20
  10.6 37.7 %collective-permute-start.1 = (bf16[22,224,128]{2,1,0:T(8,128)(2,1)}, bf16[22,224,128]{2,1,0:T(8,128)(2,1)S(1)}, u32[]{:S(2)}, u32[]{:S(2)}) collective-permute-start(bf16[22,224,128]{2,1,0:T(8,128)(2,1)} %get-tuple-element.57), channel_id=1, source_target_pairs={{0,504},{8,0},{16,8},{24,16},{32,24},{40,32},{48,40},{56,48},{64,5... | collective-permute-start | bytes 3784712 | tf_op jit(solution)/shard_map/ppermute | solution.py:20
  25.4 31.1 %copy-start.8 = (bf16[1,8,4,128]{3,2,1,0:T(4,128)(2,1)S(1)}, bf16[1,8,4,128]{3,2,1,0:T(4,128)(2,1)}, u32[]{:S(2)}) copy-start(bf16[1,8,4,128]{3,2,1,0:T(4,128)(2,1)} %get-tuple-element.45) | copy-start | bytes 24580
  25.5 33.9 %copy-start.7 = (bf16[1,8,4,128]{3,2,1,0:T(4,128)(2,1)S(1)}, bf16[1,8,4,128]{3,2,1,0:T(4,128)(2,1)}, u32[]{:S(2)}) copy-start(bf16[1,8,4,128]{3,2,1,0:T(4,128)(2,1)} %get-tuple-element.46) | copy-start | bytes 24580
  48.3 11.1 %copy-start.2 = (bf16[22,224,128]{2,1,0:T(8,128)(2,1)}, bf16[22,224,128]{2,1,0:T(8,128)(2,1)S(1)}, u32[]{:S(2)}) copy-start(bf16[22,224,128]{2,1,0:T(8,128)(2,1)S(1)} %collective-permute-done.1.east_p) | copy-start | bytes 3784708
  56.5 24.5 %collective-permute-start.3 = (f32[6,16,4,128]{3,2,1,0:T(4,128)S(1)}, f32[6,16,4,128]{3,2,1,0:T(4,128)S(1)}, u32[]{:S(2)}, u32[]{:S(2)}) collective-permute-start(f32[6,16,4,128]{3,2,1,0:T(4,128)S(1)} %constant_dynamic-update-slice_fusion.6), channel_id=1, source_target_pairs={{1,0},{2,1},{3,2},{4,3},{5,4},{6,5},{7,6},{9,8},{10,9},{11,10},{12... | collective-permute-start | bytes 589832 | tf_op jit(solution)/shard_map/ppermute | solution.py:20
  59.4 21.6 %collective-permute-start.2 = (f32[6,16,4,128]{3,2,1,0:T(4,128)S(1)}, f32[6,16,4,128]{3,2,1,0:T(4,128)S(1)}, u32[]{:S(2)}, u32[]{:S(2)}) collective-permute-start(f32[6,16,4,128]{3,2,1,0:T(4,128)S(1)} %constant_dynamic-update-slice_fusion), channel_id=1, source_target_pairs={{0,1},{1,2},{2,3},{3,4},{4,5},{5,6},{6,7},{8,9},{9,10},{10,11},{11... | collective-permute-start | bytes 589832 | tf_op jit(solution)/shard_map/ppermute | solution.py:20
  81.0 0.7 copy-start.5
  81.1 0.8 copy-start.6

commit v7 on v5

--- a/solution.py
+++ b/solution.py
@@ -48,18 +48,17 @@
     return out
 
 
-def lat_halo(fields, west, east, west_rows, east_rows):
-    def edge(part):
-        rows = []
-        for f, w, e, pw, pe in zip(fields, west_rows, east_rows, west, east):
-            piece = jnp.concatenate([pad_rows(part(pw), 0, HALO - w, 0), part(f), pad_rows(part(pe), 0, 0, HALO - e)], 0)
-            rows.append(piece.astype(jnp.float32))
-        return jnp.stack(rows)
-
+def lat_halo(fields, west_rows, east_rows):
     size = fields[0].shape[1]
-    lows = edge(lambda x: x[:, :HALO])
-    highs = edge(lambda x: x[:, size - HALO:])
-    return passed_along(highs, "lat", 1, False), passed_along(lows, "lat", -1, False)
+    lows = jnp.stack([f[:, :HALO].astype(jnp.float32) for f in fields])
+    highs = jnp.stack([f[:, size - HALO:].astype(jnp.float32) for f in fields])
+    from_south = passed_along(highs, "lat", 1, False)
+    from_north = passed_along(lows, "lat", -1, False)
+    both = jnp.stack([from_south, from_north])
+    block = fields[0].shape[0]
+    west = passed_along(both[:, :, block - HALO:], "lon", 1, True)
+    east = passed_along(both[:, :, :HALO], "lon", -1, True)
+    return [jnp.concatenate([west[n], both[n], east[n]], 1) for n in range(2)]
 
 
 def stencil_kernel(west_rows, east_rows, conc_in, wind_in, kappa_in, obs_in, west_p, east_p,
@@ -203,9 +202,7 @@
     west_rows = (4, 4, 3, 3, 4, 2)
     east_rows = (4, 3, 3, 3, 3, 2)
     got = lon_halo(fields, west_rows, east_rows)
-    west = unpack(got["west"], west_rows)
-    east = unpack(got["east"], east_rows)
-    south, north = lat_halo(fields, west, east, west_rows, east_rows)
+    south, north = lat_halo(fields, west_rows, east_rows)
     ext_rows = lon_rows + 2 * HALO
     ext_lats = lat_rows + 2 * PAD
     lat_place = lax.axis_index("lat") * lat_rows - PAD + lax.broadcasted_iota(jnp.int32, (ext_lats, levels), 0)

time: 78.3 us -> 90.3 us (1.15)
  the two profiles are of different devices: /device:TPU:64 before, /device:TPU:6 now
where the time goes in v7:
time: 90.3 us; the launch traced here: 90 us
  starting transfers between devices  38.2 us (42%)
  waiting for transfers between devices  26.3 us (29%)
  Pallas kernels  14.9 us (17%)
  local copies, waits for them, and re-layouts  5.92 us (7%)
  other arithmetic  4.03 us (4%)
    ppermute x6, starting transfers between devices, passed_along(): return lax.ppermute(value, axis, pairs)  38.2 us
    ppermute x6, waiting for transfers between devices, passed_along(): return lax.ppermute(value, axis, pairs)  26.3 us
    pallas_call x1, Pallas kernels, body(): pl.pallas_call(functools.partial(stencil_kernel, west_rows, east_rows), o...  14.9 us
    unnamed x15, local copies, waits for them, and re-layouts  4.33 us
    unnamed x6, other arithmetic  3.09 us
  transfers between devices with their start and end apart: 6, of which 3 were waited for; matrix products, arithmetic and copies ran while one was open for 1% of the time, Pallas kernels for 0%

profile of v7, /device:TPU:6, one launch (start us, length us, event | category | flops | bytes accessed | tf_op | source)
XLA Modules:
  0.0 90.0 jit_solution(14829705773864359879)
XLA Ops:
  0.6 0.0 copy-start.1
  0.6 0.0 copy-start
  0.7 2.2 %fusion.5 = (bf16[22,224,128]{2,1,0:T(8,128)(2,1)}, bf16[24,224,128]{2,1,0:T(8,128)(2,1)}) fusion(f32[8,224,128]{2,1,0:T(8,128)} %conc_in.1), kind=kLoop, calls=%fused_computation.12 | loop fusion | flops 458750 | bytes 1376256
  2.8 0.0 copy-done.1
  2.8 0.9 fusion.2
  3.7 0.0 copy-start.2
  3.7 0.0 copy-done
  3.7 0.7 bitcast_dynamic-update-slice_fusion.3
  4.4 0.0 copy-start.3
  4.4 0.7 bitcast_dynamic-update-slice_fusion
  5.1 0.8 bitcast_dynamic-update-slice_fusion.2
  5.9 0.8 bitcast_dynamic-update-slice_fusion.1
  6.6 0.0 copy-done.2
  6.6 0.7 slice_dynamic-update-slice_fusion.1
  7.3 0.7 slice_dynamic-update-slice_fusion
  8.0 0.0 copy-done.3
  8.0 0.7 slice_dynamic-update-slice_fusion.2
  8.7 1.9 %collective-permute-start = (bf16[24,224,128]{2,1,0:T(8,128)(2,1)}, bf16[24,224,128]{2,1,0:T(8,128)(2,1)}, u32[]{:S(2)}, u32[]{:S(2)}) collective-permute-start(bf16[24,224,128]{2,1,0:T(8,128)(2,1)} %get-tuple-element.26), channel_id=1, source_target_pairs={{0,8},{8,16},{16,24},{24,32},{32,40},{40,48},{48,56},{56,64},{64,7... | collective-permute-start | bytes 4128776 | tf_op jit(solution)/shard_map/ppermute | solution.py:20
  10.6 13.3 %collective-permute-start.1 = (bf16[22,224,128]{2,1,0:T(8,128)(2,1)}, bf16[22,224,128]{2,1,0:T(8,128)(2,1)}, u32[]{:S(2)}, u32[]{:S(2)}) collective-permute-start(bf16[22,224,128]{2,1,0:T(8,128)(2,1)} %get-tuple-element.25), channel_id=1, source_target_pairs={{0,504},{8,0},{16,8},{24,16},{32,24},{40,32},{48,40},{56,48},{64,5... | collective-permute-start | bytes 3784712 | tf_op jit(solution)/shard_map/ppermute | solution.py:20
  24.0 0.1 slice_bitcast_fusion
  24.2 3.3 %collective-permute-start.2 = (f32[6,8,4,128]{3,2,1,0:T(4,128)S(1)}, f32[6,8,4,128]{3,2,1,0:T(4,128)S(1)}, u32[]{:S(2)}, u32[]{:S(2)}) collective-permute-start(f32[6,8,4,128]{3,2,1,0:T(4,128)S(1)} %get-tuple-element.15), channel_id=1, source_target_pairs={{0,1},{1,2},{2,3},{3,4},{4,5},{5,6},{6,7},{8,9},{9,10},{10,11},{11... | collective-permute-start | bytes 294920 | tf_op jit(solution)/shard_map/ppermute | solution.py:20
  27.5 2.5 %collective-permute-start.3 = (f32[6,8,4,128]{3,2,1,0:T(4,128)S(1)}, f32[6,8,4,128]{3,2,1,0:T(4,128)S(1)}, u32[]{:S(2)}, u32[]{:S(2)}) collective-permute-start(f32[6,8,4,128]{3,2,1,0:T(4,128)S(1)} %get-tuple-element.16), channel_id=1, source_target_pairs={{1,0},{2,1},{3,2},{4,3},{5,4},{6,5},{7,6},{9,8},{10,9},{11,10},{12... | collective-permute-start | bytes 294920 | tf_op jit(solution)/shard_map/ppermute | solution.py:20
  30.0 18.0 %collective-permute-done.2 = f32[6,8,4,128]{3,2,1,0:T(4,128)S(1)} collective-permute-done((f32[6,8,4,128]{3,2,1,0:T(4,128)S(1)}, f32[6,8,4,128]{3,2,1,0:T(4,128)S(1)}, u32[]{:S(2)}, u32[]{:S(2)}) %collective-permute-start.2) | collective-permute-done | bytes 98336 | tf_op jit(solution)/shard_map/ppermute | solution.py:20
  48.1 0.0 collective-permute-done.3
  48.1 15.2 %collective-permute-start.5 = (f32[2,6,4,4,128]{4,3,2,1,0:T(4,128)S(1)}, f32[2,6,4,4,128]{4,3,2,1,0:T(4,128)S(1)}, u32[]{:S(2)}, u32[]{:S(2)}) collective-permute-start(f32[2,6,4,4,128]{4,3,2,1,0:T(4,128)S(1)} %get-tuple-element.28), channel_id=1, source_target_pairs={{0,504},{8,0},{16,8},{24,16},{32,24},{40,32},{48,40},{56,48},{64,5... | collective-permute-start | bytes 294920 | tf_op jit(solution)/shard_map/ppermute | solution.py:20
  63.4 1.9 %collective-permute-start.4 = (f32[2,6,4,4,128]{4,3,2,1,0:T(4,128)S(1)}, f32[2,6,4,4,128]{4,3,2,1,0:T(4,128)S(1)}, u32[]{:S(2)}, u32[]{:S(2)}) collective-permute-start(f32[2,6,4,4,128]{4,3,2,1,0:T(4,128)S(1)} %get-tuple-element.27), channel_id=1, source_target_pairs={{0,8},{8,16},{16,24},{24,32},{32,40},{40,48},{48,56},{56,64},{64,7... | collective-permute-start | bytes 294920 | tf_op jit(solution)/shard_map/ppermute | solution.py:20
  65.3 0.3 collective-permute-done.5
  65.5 8.0 %collective-permute-done.4 = f32[2,6,4,4,128]{4,3,2,1,0:T(4,128)S(1)} collective-permute-done((f32[2,6,4,4,128]{4,3,2,1,0:T(4,128)S(1)}, f32[2,6,4,4,128]{4,3,2,1,0:T(4,128)S(1)}, u32[]{:S(2)}, u32[]{:S(2)}) %collective-permute-start.4) | collective-permute-done | bytes 98336 | tf_op jit(solution)/shard_map/ppermute | solution.py:20
  73.5 0.9 pad_maximum_fusion
  74.4 0.0 collective-permute-done.1.east_p
  74.4 0.0 collective-permute-done.west_p
  74.4 0.8 iota.7.north_ref
  75.1 14.9 %shard_map.59 = (f32[8,224,128]{2,1,0:T(8,128)}, f32[8,224,128]{2,1,0:T(8,128)}) custom-call(f32[8,224,128]{2,1,0:T(8,128)} %conc_in.1, bf16[3,8,224,128]{3,2,1,0:T(8,128)(2,1)} %wind_in.1, bf16[8,224,128]{2,1,0:T(8,128)(2,1)} %kappa_in.1, bf16[8,224,128]{2,1,0:T(8,128)(2,1)} %obs_in.1, bf16[24,224,128]{2,1,0:T(8,128)(2,1)} %collective-permute-done.west_p, ...), custom_call_target="tpu_custom_call" | custom-call | tf_op jit(solution)/shard_map/pallas_call | solution.py:213
  (10 shorter events, 0.2 us)
Async XLA Ops:
  0.6 2.2 %copy-start.1 = (f32[8,224,128]{2,1,0:T(8,128)S(1)}, f32[8,224,128]{2,1,0:T(8,128)}, u32[]{:S(2)}) copy-start(f32[8,224,128]{2,1,0:T(8,128)} %conc_in.1) | copy-start | bytes 2752516
  0.6 3.0 %copy-start = (bf16[3,8,224,128]{3,2,1,0:T(8,128)(2,1)S(1)}, bf16[3,8,224,128]{3,2,1,0:T(8,128)(2,1)}, u32[]{:S(2)}) copy-start(bf16[3,8,224,128]{3,2,1,0:T(8,128)(2,1)} %wind_in.1) | copy-start | bytes 4128772
  3.7 2.9 %copy-start.2 = (bf16[8,224,128]{2,1,0:T(8,128)(2,1)S(1)}, bf16[8,224,128]{2,1,0:T(8,128)(2,1)}, u32[]{:S(2)}) copy-start(bf16[8,224,128]{2,1,0:T(8,128)(2,1)} %kappa_in.1) | copy-start | bytes 1376260
  4.4 3.6 %copy-start.3 = (bf16[8,224,128]{2,1,0:T(8,128)(2,1)S(1)}, bf16[8,224,128]{2,1,0:T(8,128)(2,1)}, u32[]{:S(2)}) copy-start(bf16[8,224,128]{2,1,0:T(8,128)(2,1)} %obs_in.1) | copy-start | bytes 1376260
  8.7 65.7 %collective-permute-start = (bf16[24,224,128]{2,1,0:T(8,128)(2,1)}, bf16[24,224,128]{2,1,0:T(8,128)(2,1)}, u32[]{:S(2)}, u32[]{:S(2)}) collective-permute-start(bf16[24,224,128]{2,1,0:T(8,128)(2,1)} %get-tuple-element.26), channel_id=1, source_target_pairs={{0,8},{8,16},{16,24},{24,32},{32,40},{40,48},{48,56},{56,64},{64,7... | collective-permute-start | bytes 4128776 | tf_op jit(solution)/shard_map/ppermute | solution.py:20
  10.6 63.7 %collective-permute-start.1 = (bf16[22,224,128]{2,1,0:T(8,128)(2,1)}, bf16[22,224,128]{2,1,0:T(8,128)(2,1)}, u32[]{:S(2)}, u32[]{:S(2)}) collective-permute-start(bf16[22,224,128]{2,1,0:T(8,128)(2,1)} %get-tuple-element.25), channel_id=1, source_target_pairs={{0,504},{8,0},{16,8},{24,16},{32,24},{40,32},{48,40},{56,48},{64,5... | collective-permute-start | bytes 3784712 | tf_op jit(solution)/shard_map/ppermute | solution.py:20
  24.2 23.9 %collective-permute-start.2 = (f32[6,8,4,128]{3,2,1,0:T(4,128)S(1)}, f32[6,8,4,128]{3,2,1,0:T(4,128)S(1)}, u32[]{:S(2)}, u32[]{:S(2)}) collective-permute-start(f32[6,8,4,128]{3,2,1,0:T(4,128)S(1)} %get-tuple-element.15), channel_id=1, source_target_pairs={{0,1},{1,2},{2,3},{3,4},{4,5},{5,6},{6,7},{8,9},{9,10},{10,11},{11... | collective-permute-start | bytes 294920 | tf_op jit(solution)/shard_map/ppermute | solution.py:20
  27.5 20.6 %collective-permute-start.3 = (f32[6,8,4,128]{3,2,1,0:T(4,128)S(1)}, f32[6,8,4,128]{3,2,1,0:T(4,128)S(1)}, u32[]{:S(2)}, u32[]{:S(2)}) collective-permute-start(f32[6,8,4,128]{3,2,1,0:T(4,128)S(1)} %get-tuple-element.16), channel_id=1, source_target_pairs={{1,0},{2,1},{3,2},{4,3},{5,4},{6,5},{7,6},{9,8},{10,9},{11,10},{12... | collective-permute-start | bytes 294920 | tf_op jit(solution)/shard_map/ppermute | solution.py:20
  48.1 17.4 %collective-permute-start.5 = (f32[2,6,4,4,128]{4,3,2,1,0:T(4,128)S(1)}, f32[2,6,4,4,128]{4,3,2,1,0:T(4,128)S(1)}, u32[]{:S(2)}, u32[]{:S(2)}) collective-permute-start(f32[2,6,4,4,128]{4,3,2,1,0:T(4,128)S(1)} %get-tuple-element.28), channel_id=1, source_target_pairs={{0,504},{8,0},{16,8},{24,16},{32,24},{40,32},{48,40},{56,48},{64,5... | collective-permute-start | bytes 294920 | tf_op jit(solution)/shard_map/ppermute | solution.py:20
  63.4 10.2 %collective-permute-start.4 = (f32[2,6,4,4,128]{4,3,2,1,0:T(4,128)S(1)}, f32[2,6,4,4,128]{4,3,2,1,0:T(4,128)S(1)}, u32[]{:S(2)}, u32[]{:S(2)}) collective-permute-start(f32[2,6,4,4,128]{4,3,2,1,0:T(4,128)S(1)} %get-tuple-element.27), channel_id=1, source_target_pairs={{0,8},{8,16},{16,24},{24,32},{32,40},{40,48},{48,56},{56,64},{64,7... | collective-permute-start | bytes 294920 | tf_op jit(solution)/shard_map/ppermute | solution.py:20

commit v8 on v7

--- a/solution.py
+++ b/solution.py
@@ -6,6 +6,7 @@
 from jax.experimental import pallas as pl
 from jax.experimental.pallas import tpu as pltpu
 from jax.sharding import PartitionSpec as P
+
 
 HALO = 4
 PAD = 8
@@ -18,12 +19,6 @@
     else:
         pairs = [(source, source + steps) for source in range(count) if 0 <= source + steps < count]
     return lax.ppermute(value, axis, pairs)
-
-
-def pad_rows(part, axis, before, after):
-    widths = [(0, 0)] * part.ndim
-    widths[axis] = (before, after)
-    return jnp.pad(part, widths)
 
 
 def lon_halo(fields, west_rows, east_rows):
@@ -39,16 +34,7 @@
     return got
 
 
-def unpack(pack, rows):
-    out = [pack[:rows[0]].astype(jnp.float32) + pack[rows[0]:2 * rows[0]].astype(jnp.float32)]
-    at = 2 * rows[0]
-    for r in rows[1:]:
-        out.append(pack[at:at + r])
-        at += r
-    return out
-
-
-def lat_halo(fields, west_rows, east_rows):
+def lat_halo(fields):
     size = fields[0].shape[1]
     lows = jnp.stack([f[:, :HALO].astype(jnp.float32) for f in fields])
     highs = jnp.stack([f[:, size - HALO:].astype(jnp.float32) for f in fields])
@@ -195,14 +181,14 @@
     lax.fori_loop(h, rows - h, last_row, part0(lam1_ref, h - 1))
 
 
-def body(concentration, wind, kappa, observed):
+def chain(concentration, wind, kappa, observed):
     lon_rows, lat_rows, levels = concentration.shape
     lat_total = lat_rows * lax.axis_size("lat")
     fields = [concentration, wind[0], wind[1], wind[2], kappa, observed]
     west_rows = (4, 4, 3, 3, 4, 2)
     east_rows = (4, 3, 3, 3, 3, 2)
     got = lon_halo(fields, west_rows, east_rows)
-    south, north = lat_halo(fields, west_rows, east_rows)
+    south, north = lat_halo(fields)
     ext_rows = lon_rows + 2 * HALO
     ext_lats = lat_rows + 2 * PAD
     lat_place = lax.axis_index("lat") * lat_rows - PAD + lax.broadcasted_iota(jnp.int32, (ext_lats, levels), 0)
@@ -231,8 +217,12 @@
 
 
 def solution(mesh):
+    return step(mesh)
+
+
+def step(mesh):
     return jax.shard_map(
-        body,
+        chain,
         mesh=mesh,
         in_specs=(
             P("lon", "lat", None),

time: 90.3 us -> 90.3 us (level)
  no operation moved by 1% of the time
where the time goes in v8:
time: 90.3 us; the launch traced here: 90 us
  starting transfers between devices  38.2 us (42%)
  waiting for transfers between devices  26.3 us (29%)
  Pallas kernels  14.9 us (17%)
  local copies, waits for them, and re-layouts  5.92 us (7%)
  other arithmetic  4.03 us (4%)
    ppermute x6, starting transfers between devices, passed_along(): return lax.ppermute(value, axis, pairs)  38.2 us
    ppermute x6, waiting for transfers between devices, passed_along(): return lax.ppermute(value, axis, pairs)  26.3 us
    pallas_call x1, Pallas kernels, chain(): pl.pallas_call(functools.partial(stencil_kernel, west_rows, east_rows), o...  14.9 us
    unnamed x15, local copies, waits for them, and re-layouts  4.33 us
    unnamed x6, other arithmetic  3.09 us
  transfers between devices with their start and end apart: 6, of which 3 were waited for; matrix products, arithmetic and copies ran while one was open for 1% of the time, Pallas kernels for 0%

profile of v8, /device:TPU:6, one launch (start us, length us, event | category | flops | bytes accessed | tf_op | source)
XLA Modules:
  0.0 90.0 jit_solution(14829705773864359879)
XLA Ops:
  0.6 0.0 copy-start.1
  0.6 0.0 copy-start
  0.7 2.2 %fusion.5 = (bf16[22,224,128]{2,1,0:T(8,128)(2,1)}, bf16[24,224,128]{2,1,0:T(8,128)(2,1)}) fusion(f32[8,224,128]{2,1,0:T(8,128)} %conc_in.1), kind=kLoop, calls=%fused_computation.12 | loop fusion | flops 458750 | bytes 1376256
  2.8 0.0 copy-done.1
  2.8 0.9 fusion.2
  3.7 0.0 copy-start.2
  3.7 0.0 copy-done
  3.7 0.7 bitcast_dynamic-update-slice_fusion.3
  4.4 0.0 copy-start.3
  4.4 0.7 bitcast_dynamic-update-slice_fusion
  5.1 0.8 bitcast_dynamic-update-slice_fusion.2
  5.9 0.8 bitcast_dynamic-update-slice_fusion.1
  6.6 0.0 copy-done.2
  6.6 0.7 slice_dynamic-update-slice_fusion.1
  7.3 0.7 slice_dynamic-update-slice_fusion
  8.0 0.0 copy-done.3
  8.0 0.7 slice_dynamic-update-slice_fusion.2
  8.7 1.9 %collective-permute-start = (bf16[24,224,128]{2,1,0:T(8,128)(2,1)}, bf16[24,224,128]{2,1,0:T(8,128)(2,1)}, u32[]{:S(2)}, u32[]{:S(2)}) collective-permute-start(bf16[24,224,128]{2,1,0:T(8,128)(2,1)} %get-tuple-element.26), channel_id=1, source_target_pairs={{0,8},{8,16},{16,24},{24,32},{32,40},{40,48},{48,56},{56,64},{64,7... | collective-permute-start | bytes 4128776 | tf_op jit(solution)/shard_map/ppermute | solution.py:21
  10.6 13.3 %collective-permute-start.1 = (bf16[22,224,128]{2,1,0:T(8,128)(2,1)}, bf16[22,224,128]{2,1,0:T(8,128)(2,1)}, u32[]{:S(2)}, u32[]{:S(2)}) collective-permute-start(bf16[22,224,128]{2,1,0:T(8,128)(2,1)} %get-tuple-element.25), channel_id=1, source_target_pairs={{0,504},{8,0},{16,8},{24,16},{32,24},{40,32},{48,40},{56,48},{64,5... | collective-permute-start | bytes 3784712 | tf_op jit(solution)/shard_map/ppermute | solution.py:21
  24.0 0.1 slice_bitcast_fusion
  24.2 3.3 %collective-permute-start.2 = (f32[6,8,4,128]{3,2,1,0:T(4,128)S(1)}, f32[6,8,4,128]{3,2,1,0:T(4,128)S(1)}, u32[]{:S(2)}, u32[]{:S(2)}) collective-permute-start(f32[6,8,4,128]{3,2,1,0:T(4,128)S(1)} %get-tuple-element.15), channel_id=1, source_target_pairs={{0,1},{1,2},{2,3},{3,4},{4,5},{5,6},{6,7},{8,9},{9,10},{10,11},{11... | collective-permute-start | bytes 294920 | tf_op jit(solution)/shard_map/ppermute | solution.py:21
  27.5 2.5 %collective-permute-start.3 = (f32[6,8,4,128]{3,2,1,0:T(4,128)S(1)}, f32[6,8,4,128]{3,2,1,0:T(4,128)S(1)}, u32[]{:S(2)}, u32[]{:S(2)}) collective-permute-start(f32[6,8,4,128]{3,2,1,0:T(4,128)S(1)} %get-tuple-element.16), channel_id=1, source_target_pairs={{1,0},{2,1},{3,2},{4,3},{5,4},{6,5},{7,6},{9,8},{10,9},{11,10},{12... | collective-permute-start | bytes 294920 | tf_op jit(solution)/shard_map/ppermute | solution.py:21
  30.0 18.0 %collective-permute-done.2 = f32[6,8,4,128]{3,2,1,0:T(4,128)S(1)} collective-permute-done((f32[6,8,4,128]{3,2,1,0:T(4,128)S(1)}, f32[6,8,4,128]{3,2,1,0:T(4,128)S(1)}, u32[]{:S(2)}, u32[]{:S(2)}) %collective-permute-start.2) | collective-permute-done | bytes 98336 | tf_op jit(solution)/shard_map/ppermute | solution.py:21
  48.1 0.0 collective-permute-done.3
  48.1 15.2 %collective-permute-start.5 = (f32[2,6,4,4,128]{4,3,2,1,0:T(4,128)S(1)}, f32[2,6,4,4,128]{4,3,2,1,0:T(4,128)S(1)}, u32[]{:S(2)}, u32[]{:S(2)}) collective-permute-start(f32[2,6,4,4,128]{4,3,2,1,0:T(4,128)S(1)} %get-tuple-element.28), channel_id=1, source_target_pairs={{0,504},{8,0},{16,8},{24,16},{32,24},{40,32},{48,40},{56,48},{64,5... | collective-permute-start | bytes 294920 | tf_op jit(solution)/shard_map/ppermute | solution.py:21
  63.4 1.9 %collective-permute-start.4 = (f32[2,6,4,4,128]{4,3,2,1,0:T(4,128)S(1)}, f32[2,6,4,4,128]{4,3,2,1,0:T(4,128)S(1)}, u32[]{:S(2)}, u32[]{:S(2)}) collective-permute-start(f32[2,6,4,4,128]{4,3,2,1,0:T(4,128)S(1)} %get-tuple-element.27), channel_id=1, source_target_pairs={{0,8},{8,16},{16,24},{24,32},{32,40},{40,48},{48,56},{56,64},{64,7... | collective-permute-start | bytes 294920 | tf_op jit(solution)/shard_map/ppermute | solution.py:21
  65.3 0.3 collective-permute-done.5
  65.5 8.0 %collective-permute-done.4 = f32[2,6,4,4,128]{4,3,2,1,0:T(4,128)S(1)} collective-permute-done((f32[2,6,4,4,128]{4,3,2,1,0:T(4,128)S(1)}, f32[2,6,4,4,128]{4,3,2,1,0:T(4,128)S(1)}, u32[]{:S(2)}, u32[]{:S(2)}) %collective-permute-start.4) | collective-permute-done | bytes 98336 | tf_op jit(solution)/shard_map/ppermute | solution.py:21
  73.5 0.9 pad_maximum_fusion
  74.4 0.0 collective-permute-done.1.east_p
  74.4 0.0 collective-permute-done.west_p
  74.4 0.8 iota.7.north_ref
  75.1 14.9 %shard_map.59 = (f32[8,224,128]{2,1,0:T(8,128)}, f32[8,224,128]{2,1,0:T(8,128)}) custom-call(f32[8,224,128]{2,1,0:T(8,128)} %conc_in.1, bf16[3,8,224,128]{3,2,1,0:T(8,128)(2,1)} %wind_in.1, bf16[8,224,128]{2,1,0:T(8,128)(2,1)} %kappa_in.1, bf16[8,224,128]{2,1,0:T(8,128)(2,1)} %obs_in.1, bf16[24,224,128]{2,1,0:T(8,128)(2,1)} %collective-permute-done.west_p, ...), custom_call_target="tpu_custom_call" | custom-call | tf_op jit(solution)/shard_map/pallas_call | solution.py:199
  (10 shorter events, 0.2 us)
Async XLA Ops:
  0.6 2.2 %copy-start.1 = (f32[8,224,128]{2,1,0:T(8,128)S(1)}, f32[8,224,128]{2,1,0:T(8,128)}, u32[]{:S(2)}) copy-start(f32[8,224,128]{2,1,0:T(8,128)} %conc_in.1) | copy-start | bytes 2752516
  0.6 3.0 %copy-start = (bf16[3,8,224,128]{3,2,1,0:T(8,128)(2,1)S(1)}, bf16[3,8,224,128]{3,2,1,0:T(8,128)(2,1)}, u32[]{:S(2)}) copy-start(bf16[3,8,224,128]{3,2,1,0:T(8,128)(2,1)} %wind_in.1) | copy-start | bytes 4128772
  3.7 2.9 %copy-start.2 = (bf16[8,224,128]{2,1,0:T(8,128)(2,1)S(1)}, bf16[8,224,128]{2,1,0:T(8,128)(2,1)}, u32[]{:S(2)}) copy-start(bf16[8,224,128]{2,1,0:T(8,128)(2,1)} %kappa_in.1) | copy-start | bytes 1376260
  4.4 3.6 %copy-start.3 = (bf16[8,224,128]{2,1,0:T(8,128)(2,1)S(1)}, bf16[8,224,128]{2,1,0:T(8,128)(2,1)}, u32[]{:S(2)}) copy-start(bf16[8,224,128]{2,1,0:T(8,128)(2,1)} %obs_in.1) | copy-start | bytes 1376260
  8.7 65.7 %collective-permute-start = (bf16[24,224,128]{2,1,0:T(8,128)(2,1)}, bf16[24,224,128]{2,1,0:T(8,128)(2,1)}, u32[]{:S(2)}, u32[]{:S(2)}) collective-permute-start(bf16[24,224,128]{2,1,0:T(8,128)(2,1)} %get-tuple-element.26), channel_id=1, source_target_pairs={{0,8},{8,16},{16,24},{24,32},{32,40},{40,48},{48,56},{56,64},{64,7... | collective-permute-start | bytes 4128776 | tf_op jit(solution)/shard_map/ppermute | solution.py:21
  10.6 63.7 %collective-permute-start.1 = (bf16[22,224,128]{2,1,0:T(8,128)(2,1)}, bf16[22,224,128]{2,1,0:T(8,128)(2,1)}, u32[]{:S(2)}, u32[]{:S(2)}) collective-permute-start(bf16[22,224,128]{2,1,0:T(8,128)(2,1)} %get-tuple-element.25), channel_id=1, source_target_pairs={{0,504},{8,0},{16,8},{24,16},{32,24},{40,32},{48,40},{56,48},{64,5... | collective-permute-start | bytes 3784712 | tf_op jit(solution)/shard_map/ppermute | solution.py:21
  24.2 23.9 %collective-permute-start.2 = (f32[6,8,4,128]{3,2,1,0:T(4,128)S(1)}, f32[6,8,4,128]{3,2,1,0:T(4,128)S(1)}, u32[]{:S(2)}, u32[]{:S(2)}) collective-permute-start(f32[6,8,4,128]{3,2,1,0:T(4,128)S(1)} %get-tuple-element.15), channel_id=1, source_target_pairs={{0,1},{1,2},{2,3},{3,4},{4,5},{5,6},{6,7},{8,9},{9,10},{10,11},{11... | collective-permute-start | bytes 294920 | tf_op jit(solution)/shard_map/ppermute | solution.py:21
  27.5 20.6 %collective-permute-start.3 = (f32[6,8,4,128]{3,2,1,0:T(4,128)S(1)}, f32[6,8,4,128]{3,2,1,0:T(4,128)S(1)}, u32[]{:S(2)}, u32[]{:S(2)}) collective-permute-start(f32[6,8,4,128]{3,2,1,0:T(4,128)S(1)} %get-tuple-element.16), channel_id=1, source_target_pairs={{1,0},{2,1},{3,2},{4,3},{5,4},{6,5},{7,6},{9,8},{10,9},{11,10},{12... | collective-permute-start | bytes 294920 | tf_op jit(solution)/shard_map/ppermute | solution.py:21
  48.1 17.4 %collective-permute-start.5 = (f32[2,6,4,4,128]{4,3,2,1,0:T(4,128)S(1)}, f32[2,6,4,4,128]{4,3,2,1,0:T(4,128)S(1)}, u32[]{:S(2)}, u32[]{:S(2)}) collective-permute-start(f32[2,6,4,4,128]{4,3,2,1,0:T(4,128)S(1)} %get-tuple-element.28), channel_id=1, source_target_pairs={{0,504},{8,0},{16,8},{24,16},{32,24},{40,32},{48,40},{56,48},{64,5... | collective-permute-start | bytes 294920 | tf_op jit(solution)/shard_map/ppermute | solution.py:21
  63.4 10.2 %collective-permute-start.4 = (f32[2,6,4,4,128]{4,3,2,1,0:T(4,128)S(1)}, f32[2,6,4,4,128]{4,3,2,1,0:T(4,128)S(1)}, u32[]{:S(2)}, u32[]{:S(2)}) collective-permute-start(f32[2,6,4,4,128]{4,3,2,1,0:T(4,128)S(1)} %get-tuple-element.27), channel_id=1, source_target_pairs={{0,8},{8,16},{16,24},{24,32},{32,40},{40,48},{48,56},{56,64},{64,7... | collective-permute-start | bytes 294920 | tf_op jit(solution)/shard_map/ppermute | solution.py:21
